TPU v7x, 32 devices: a whole 2x2x4 slice. The times are simulated.
32 devices in a mesh: dp: 2 (over y), seq: 16 (over z, x, core).
Axes of the slice: x: 2, y: 2, z: 4, core: 2. Of those that a mesh axis runs over, the one named last changes fastest.
Arguments:
- inputs: bfloat16 [2, 256, 512, 512], P('dp', 'seq'), may hold values from -6 to 6
- gate_logits: bfloat16 [2, 256, 512, 512], P('dp', 'seq'), may hold values from -8 to 8
- kernel: bfloat16 [256, 512, 512], P(None, 'seq'), may hold values from -1.5 to 1.5
- cotangent: bfloat16 [2, 256, 512, 512], P('dp', 'seq'), may hold values from -6 to 6
- block_one: bfloat16 [256, 512, 512], P('seq'), may hold values from -0.25 to 0.25
- block_two: bfloat16 [512, 256, 256], P('seq'), may hold values from -0.375 to 0.375
Outputs:
- output: bfloat16 [2, 256, 512, 512], P('dp', 'seq')
- grad_inputs: bfloat16 [2, 256, 512, 512], P('dp', 'seq')
- grad_gate: bfloat16 [2, 256, 512, 512], P('dp', 'seq')
- grad_kernel: bfloat16 [256, 512, 512], P(None, 'seq', 'dp')
- grad_block_one: bfloat16 [256, 512, 512], P('seq', None, 'dp')
- grad_block_two: bfloat16 [512, 256, 256], P('seq', None, 'dp')
All inputs are finite; a program needn't handle non-finite values.
Results may differ from a plain program's by a relative error of at most 0.009.
Values may be sent and summed in bfloat16 or wider, within the bound.
No kernel may reach another device: no remote copies, remote signals or barrier semaphores. Data moves between devices by JAX's collectives and lax.ppermute only.
A program may use at most 320 MiB of HBM per device.

v0:
```python
import jax
import jax.numpy as jnp
from jax import lax
from jax.sharding import PartitionSpec as P


def body(inputs, gate_logits, kernel, cotangent, block_one, block_two):
    tokens = inputs[0]
    kernel_wide = kernel.astype(jnp.float32)
    grad_scale = (lax.axis_size("dp") * tokens.shape[2]) ** (-0.5)
    first = jnp.einsum(
        "acb,abd->acd", block_one, tokens, preferred_element_type=jnp.float32
    ).astype(jnp.bfloat16)
    arrived = lax.all_to_all(first, "seq", split_axis=1, concat_axis=0, tiled=True)
    first_cols = arrived
    second = jnp.einsum("cea,acd->ecd", block_two, arrived, preferred_element_type=jnp.float32)
    filtered = (kernel_wide * second).astype(jnp.bfloat16)
    third = jnp.einsum(
        "cef,ecd->fcd", block_two, filtered, preferred_element_type=jnp.float32
    ).astype(jnp.bfloat16)
    arrived = lax.all_to_all(third, "seq", split_axis=0, concat_axis=1, tiled=True)
    third_rows = arrived
    fourth = jnp.einsum(
        "fch,fcd->fhd", block_one, arrived, preferred_element_type=jnp.float32
    ).astype(jnp.bfloat16)
    opened = jax.nn.sigmoid(gate_logits[0].astype(jnp.float32))
    incoming = cotangent[0].astype(jnp.float32)
    fourth_wide = fourth.astype(jnp.float32)
    output = (opened * fourth_wide).astype(jnp.bfloat16)
    grad_gate = (incoming * fourth_wide * opened * (1.0 - opened)).astype(jnp.bfloat16)
    grad_fourth = (incoming * opened).astype(jnp.bfloat16)
    outer_one = jnp.einsum(
        "fhd,fcd->fch", grad_fourth, third_rows, preferred_element_type=jnp.float32
    )
    grad_third = jnp.einsum(
        "fch,fhd->fcd", block_one, grad_fourth, preferred_element_type=jnp.float32
    ).astype(jnp.bfloat16)
    arrived = lax.all_to_all(grad_third, "seq", split_axis=1, concat_axis=0, tiled=True)
    grad_third_cols = arrived
    grad_filtered = jnp.einsum(
        "cef,fcd->ecd", block_two, arrived, preferred_element_type=jnp.float32
    )
    outer_two = jnp.einsum(
        "fcd,ecd->cef", grad_third_cols, filtered, preferred_element_type=jnp.float32
    )
    grad_kernel = grad_filtered * second
    grad_second = (kernel_wide * grad_filtered).astype(jnp.bfloat16)
    grad_block_two = (
        outer_two
        + jnp.einsum("ecd,acd->cea", grad_second, first_cols, preferred_element_type=jnp.float32)
    ) * grad_scale
    grad_first = jnp.einsum(
        "cea,ecd->acd", block_two, grad_second, preferred_element_type=jnp.float32
    ).astype(jnp.bfloat16)
    arrived = lax.all_to_all(grad_first, "seq", split_axis=0, concat_axis=1, tiled=True)
    grad_tokens = jnp.einsum(
        "acb,acd->abd", block_one, arrived, preferred_element_type=jnp.float32
    ).astype(jnp.bfloat16)
    grad_block_one = (
        outer_one + jnp.einsum("acd,abd->acb", arrived, tokens, preferred_element_type=jnp.float32)
    ) * grad_scale
    grad_block_one, grad_block_two, grad_kernel = (
        lax.psum_scatter(grad_block_one, "dp", scatter_dimension=2, tiled=True),
        lax.psum_scatter(grad_block_two, "dp", scatter_dimension=2, tiled=True),
        lax.psum_scatter(grad_kernel, "dp", scatter_dimension=2, tiled=True),
    )
    return (
        output[None],
        grad_tokens[None],
        grad_gate[None],
        grad_kernel.astype(jnp.bfloat16),
        grad_block_one.astype(jnp.bfloat16),
        grad_block_two.astype(jnp.bfloat16),
    )


def solution(mesh):
    return jax.shard_map(
        body,
        mesh=mesh,
        in_specs=(
            P("dp", "seq", None, None),
            P("dp", "seq", None, None),
            P(None, "seq", None),
            P("dp", "seq", None, None),
            P("seq", None, None),
            P("seq", None, None),
        ),
        out_specs=(
            P("dp", "seq", None, None),
            P("dp", "seq", None, None),
            P("dp", "seq", None, None),
            P(None, "seq", "dp"),
            P("seq", None, "dp"),
            P("seq", None, "dp"),
        ),
        check_vma=False,
    )
```

profile of v0, /device:TPU:10, one launch (start us, length us, event | category | flops | bytes accessed | tf_op | source)
XLA Modules:
  0.0 1186.8 jit_solution(1900922170163310603)
XLA Ops:
  7.2 12.3 %copy.77 = bf16[1,16,512,512]{2,3,1,0:T(8,128)(2,1)} copy(bf16[1,16,512,512]{3,2,1,0:T(8,128)(2,1)} %param.7) | data formatting | bytes 16777216 | tf_op args[1]
  19.4 12.3 %copy.86 = bf16[1,16,512,512]{2,3,1,0:T(8,128)(2,1)} copy(bf16[1,16,512,512]{3,2,1,0:T(8,128)(2,1)} %param.9) | data formatting | bytes 16777216 | tf_op args[3]
  31.7 12.7 %convert_bitcast_fusion.2 = bf16[16,512,512]{1,2,0:T(8,128)(2,1)} fusion(bf16[16,512,512]{2,1,0:T(8,128)(2,1)} %param.10, bf16[1,16,512,512]{2,3,1,0:T(8,128)(2,1)} %copy.86, bf16[1,16,512,512]{2,3,1,0:T(8,128)(2,1)} %copy.77), kind=kOutput, calls=%fused_computation.25 | convolution fusion | flops 4328521728 | bytes 33554432 | tf_op jit(solution)/shard_map/fch,fhd->fcd/dot_general | solution.py:35
  44.4 14.9 %copy.87 = bf16[16,512,512]{2,0,1:T(8,128)(2,1)} copy(bf16[16,512,512]{1,2,0:T(8,128)(2,1)} %convert_bitcast_fusion.2) | data formatting | bytes 16777216 | tf_op jit(solution)/shard_map/convert_element_type | solution.py:37
  65.8 13.7 %fusion.21 = bf16[16,512,512]{2,1,0:T(8,128)(2,1)} fusion(bf16[16,512,512]{2,1,0:T(8,128)(2,1)} %param.10, bf16[1,16,512,512]{3,2,1,0:T(8,128)(2,1)} %param.6), kind=kOutput, calls=%fused_computation.35 | convolution fusion | flops 4299161600 | bytes 25165824 | tf_op jit(solution)/shard_map/acb,abd->acd/dot_general | solution.py:11
  79.5 11.3 copy.79
  90.9 156.9 %all-to-all-done.2 = bf16[16,512,512]{2,0,1:T(8,128)(2,1)} async-done(((bf16[16,512,512]{2,0,1:T(8,128)(2,1)}), bf16[16,512,512]{2,0,1:T(8,128)(2,1)}, u32[]{:S(2)}, u32[]{:S(2)}) %all-to-all-start.2) | async-done | bytes 8388640 | tf_op jit(solution)/shard_map/all_to_all | solution.py:38
  252.8 13.9 %copy.78 = bf16[256,32,512]{0,2,1:T(8,128)(2,1)} copy(bf16[256,32,512]{2,1,0:T(8,128)(2,1)} %param.8) | data formatting | bytes 16777216 | tf_op args[2]
  266.7 12.3 %copy.89 = bf16[16,16,32,512]{3,2,1,0:T(8,128)(2,1)} copy(bf16[16,16,32,512]{3,1,2,0:T(8,128)(2,1)} %bitcast.17) | data formatting | bytes 16777216 | tf_op jit(solution)/shard_map/all_to_all | solution.py:38
  279.0 155.8 %all-to-all-done = bf16[16,512,512]{2,0,1:T(8,128)(2,1)} async-done(((bf16[16,512,512]{2,0,1:T(8,128)(2,1)}), bf16[16,512,512]{2,0,1:T(8,128)(2,1)}, u32[]{:S(2)}, u32[]{:S(2)}) %all-to-all-start) | async-done | bytes 8388640 | tf_op jit(solution)/shard_map/all_to_all | solution.py:14
  434.9 12.7 %copy.81 = bf16[16,16,32,512]{3,2,1,0:T(8,128)(2,1)} copy(bf16[16,16,32,512]{3,1,2,0:T(8,128)(2,1)} %bitcast.4) | data formatting | bytes 16777216 | tf_op jit(solution)/shard_map/all_to_all | solution.py:14
  447.6 20.4 %fusion.13 = f32[32,512,256]{2,1,0:T(8,128)} fusion(bf16[32,256,256]{2,1,0:T(8,128)(2,1)} %param.11, bf16[256,32,512]{2,1,0:T(8,128)(2,1)} %bitcast.89), kind=kOutput, calls=%fused_computation.27 | convolution fusion | flops 2147483648 | bytes 29360128 | tf_op jit(solution)/shard_map/cea,acd->ecd/dot_general | solution.py:16
  467.9 22.1 %bitcast_multiply_fusion = (f32[256,32,512]{0,2,1:T(8,128)}, f32[32,512,256]{2,1,0:T(8,128)}) fusion(f32[32,512,256]{2,1,0:T(8,128)} %fusion.13, bf16[32,256,256]{2,1,0:T(8,128)(2,1)} %param.11, bf16[256,32,512]{2,1,0:T(8,128)(2,1)} %bitcast.87), kind=kOutput, calls=%fused_computation.10 | convolution fusion | flops 2151677952 | bytes 62914560 | tf_op jit(solution)/shard_map/cef,fcd->ecd/dot_general | solution.py:40
  490.0 21.2 %fusion.15 = f32[32,256,256]{2,1,0:T(8,128)} fusion(bf16[256,32,512]{2,1,0:T(8,128)(2,1)} %bitcast.90, bf16[256,32,512]{0,2,1:T(8,128)(2,1)} %copy.78, f32[32,512,256]{2,1,0:T(8,128)} %get-tuple-element.33), kind=kOutput, calls=%fused_computation.29 | convolution fusion | flops 2160066560 | bytes 41943040 | tf_op jit(solution)/shard_map/ecd,acd->cea/dot_general | solution.py:50
  511.3 23.3 %add_multiply_fusion.1 = f32[32,256,256]{2,1,0:T(8,128)} fusion(f32[32,256,256]{2,1,0:T(8,128)} %fusion.15, bf16[256,32,512]{2,1,0:T(8,128)(2,1)} %bitcast.88, bf16[256,32,512]{0,2,1:T(8,128)(2,1)} %copy.78, f32[32,512,256]{2,1,0:T(8,128)} %fusion.13), kind=kOutput, calls=%fused_computation.22 | convolution fusion | flops 2164260864 | bytes 50331648 | tf_op jit(solution)/shard_map/fcd,ecd->cef/dot_general | solution.py:43
  534.6 14.9 %convert_bitcast_fusion.3 = bf16[256,32,512]{0,2,1:T(8,128)(2,1)} fusion(bf16[32,256,256]{2,1,0:T(8,128)(2,1)} %param.11, bf16[256,32,512]{0,2,1:T(8,128)(2,1)} %copy.78, f32[32,512,256]{2,1,0:T(8,128)} %fusion.13), kind=kOutput, calls=%fused_computation.26 | convolution fusion | flops 2164260864 | bytes 37748736 | tf_op jit(solution)/shard_map/cef,ecd->fcd/dot_general | solution.py:18
  549.5 14.9 %copy.83 = bf16[256,32,512]{2,1,0:T(8,128)(2,1)} copy(bf16[256,32,512]{0,2,1:T(8,128)(2,1)} %convert_bitcast_fusion.3) | data formatting | bytes 16777216 | tf_op jit(solution)/shard_map/convert_element_type | solution.py:20
  569.9 14.6 %convert_bitcast_fusion.1 = bf16[256,32,512]{0,2,1:T(8,128)(2,1)} fusion(bf16[32,256,256]{2,1,0:T(8,128)(2,1)} %param.11, bf16[256,32,512]{0,2,1:T(8,128)(2,1)} %copy.78, f32[32,512,256]{2,1,0:T(8,128)} %get-tuple-element.33), kind=kOutput, calls=%fused_computation.24 | convolution fusion | flops 2164260864 | bytes 37748736 | tf_op jit(solution)/shard_map/cea,ecd->acd/dot_general | solution.py:52
  584.5 14.7 %copy.91 = bf16[256,32,512]{2,1,0:T(8,128)(2,1)} copy(bf16[256,32,512]{0,2,1:T(8,128)(2,1)} %convert_bitcast_fusion.1) | data formatting | bytes 16777216 | tf_op jit(solution)/shard_map/convert_element_type | solution.py:54
  599.3 152.0 %all-to-all-done.1 = bf16[256,32,512]{2,1,0:T(8,128)(2,1)} async-done(((bf16[256,32,512]{2,1,0:T(8,128)(2,1)}), bf16[256,32,512]{2,1,0:T(8,128)(2,1)}, u32[]{:S(2)}, u32[]{:S(2)}) %all-to-all-start.1) | async-done | bytes 8388640 | tf_op jit(solution)/shard_map/all_to_all | solution.py:21
  756.4 8.7 copy.84
  765.1 173.3 %all-to-all-done.3 = bf16[256,32,512]{2,1,0:T(8,128)(2,1)} async-done(((bf16[256,32,512]{2,1,0:T(8,128)(2,1)}), bf16[256,32,512]{2,1,0:T(8,128)(2,1)}, u32[]{:S(2)}, u32[]{:S(2)}) %all-to-all-start.3) | async-done | bytes 8388640 | tf_op jit(solution)/shard_map/all_to_all | solution.py:55
  938.4 8.2 copy.92
  946.6 16.1 %fusion.9 = f32[16,512,512]{2,1,0:T(8,128)} fusion(bf16[16,512,512]{2,1,0:T(8,128)(2,1)} %bitcast.91, bf16[1,16,512,512]{3,2,1,0:T(8,128)(2,1)} %param.6), kind=kOutput, calls=%fused_computation.18 | convolution fusion | flops 4294967296 | bytes 33554432 | tf_op jit(solution)/shard_map/acd,abd->acb/dot_general | solution.py:60
  962.7 22.1 %add_multiply_fusion = f32[16,512,512]{2,1,0:T(8,128)} fusion(f32[16,512,512]{2,1,0:T(8,128)} %fusion.9, bf16[16,512,512]{2,1,0:T(8,128)(2,1)} %bitcast.93, bf16[1,16,512,512]{2,3,1,0:T(8,128)(2,1)} %copy.86, bf16[1,16,512,512]{2,3,1,0:T(8,128)(2,1)} %copy.77), kind=kOutput, calls=%fused_computation.14 | convolution fusion | flops 4332716032 | bytes 58720256 | tf_op jit(solution)/shard_map/fhd,fcd->fch/dot_general | solution.py:32
  984.8 20.4 %fusion.8 = (bf16[1,16,512,512]{2,3,1,0:T(8,128)(2,1)}, bf16[1,16,512,512]{2,3,1,0:T(8,128)(2,1)}) fusion(bf16[1,16,512,512]{2,3,1,0:T(8,128)(2,1)} %copy.86, bf16[1,16,512,512]{2,3,1,0:T(8,128)(2,1)} %copy.77, bf16[16,512,512]{2,1,0:T(8,128)(2,1)} %bitcast.94, bf16[16,512,512]{2,1,0:T(8,128)(2,1)} %param.10), kind=kOutput, calls=%fused_computation.17 | convolution fusion | flops 4353687552 | bytes 50331648 | tf_op jit(solution)/shard_map/fch,fcd->fhd/dot_general | solution.py:23
  1005.2 12.4 %copy.101 = bf16[1,16,512,512]{3,2,1,0:T(8,128)(2,1)} copy(bf16[1,16,512,512]{2,3,1,0:T(8,128)(2,1)} %get-tuple-element.30) | data formatting | bytes 16777216
  1017.6 12.3 %copy.99 = bf16[1,16,512,512]{3,2,1,0:T(8,128)(2,1)} copy(bf16[1,16,512,512]{2,3,1,0:T(8,128)(2,1)} %get-tuple-element.31) | data formatting | bytes 16777216
  1029.9 11.6 convert_bitcast_fusion
  1041.5 12.3 %copy.100 = bf16[1,16,512,512]{3,2,1,0:T(8,128)(2,1)} copy(bf16[1,16,512,512]{2,3,1,0:T(8,128)(2,1)} %convert_bitcast_fusion) | data formatting | bytes 16777216
  1063.6 7.9 copy.102
  1071.5 102.6 %reduce-scatter.6.cloned.1.call-done = f32[16,512,256]{2,1,0:T(8,128)} async-done(((f32[16,512,512]{2,1,0:T(8,128)}), f32[16,512,256]{2,1,0:T(8,128)}) %reduce-scatter.6.cloned.1.call-update) | async-done | bytes 8388624 | tf_op jit(solution)/shard_map/reduce_scatter | solution.py:63
  (15 shorter events, 38.0 us)
Async XLA Ops:
  59.3 188.5 %all-to-all-start.2 = ((bf16[16,512,512]{2,0,1:T(8,128)(2,1)}), bf16[16,512,512]{2,0,1:T(8,128)(2,1)}, u32[]{:S(2)}, u32[]{:S(2)}) async-start(bf16[16,512,512]{2,0,1:T(8,128)(2,1)} %copy.87), calls=%async_computation.2 | async-start | bytes 16777216 | tf_op jit(solution)/shard_map/all_to_all | solution.py:38
  247.8 187.1 %all-to-all-start = ((bf16[16,512,512]{2,0,1:T(8,128)(2,1)}), bf16[16,512,512]{2,0,1:T(8,128)(2,1)}, u32[]{:S(2)}, u32[]{:S(2)}) async-start(bf16[16,512,512]{2,0,1:T(8,128)(2,1)} %copy.79), calls=%async_computation | async-start | bytes 16777216 | tf_op jit(solution)/shard_map/all_to_all | solution.py:14
  252.8 801.0 %reduce-scatter.8.cloned.1.call-start = ((), (), s32[]{:S(2)}) async-start(), calls=%async_computation.9 | async-start | bytes 12582912 | tf_op jit(solution)/shard_map/reduce_scatter | solution.py:64
  564.4 186.9 %all-to-all-start.1 = ((bf16[256,32,512]{2,1,0:T(8,128)(2,1)}), bf16[256,32,512]{2,1,0:T(8,128)(2,1)}, u32[]{:S(2)}, u32[]{:S(2)}) async-start(bf16[256,32,512]{2,1,0:T(8,128)(2,1)} %copy.83), calls=%async_computation.1 | async-start | bytes 16777216 | tf_op jit(solution)/shard_map/all_to_all | solution.py:21
  569.2 488.4 %reduce-scatter.4.cloned.1.call-start = ((), (), s32[]{:S(2)}) async-start(), calls=%async_computation.7 | async-start | bytes 25165824 | tf_op jit(solution)/shard_map/reduce_scatter | solution.py:65
  751.3 187.1 %all-to-all-start.3 = ((bf16[256,32,512]{2,1,0:T(8,128)(2,1)}), bf16[256,32,512]{2,1,0:T(8,128)(2,1)}, u32[]{:S(2)}, u32[]{:S(2)}) async-start(bf16[256,32,512]{2,1,0:T(8,128)(2,1)} %copy.91), calls=%async_computation.3 | async-start | bytes 16777216 | tf_op jit(solution)/shard_map/all_to_all | solution.py:55
  756.3 417.8 %reduce-scatter.6.cloned.1.call-start = ((), (), s32[]{:S(2)}) async-start(), calls=%async_computation.8 | async-start | bytes 25165824 | tf_op jit(solution)/shard_map/reduce_scatter | solution.py:63
Sparse Core Ops, SparseCore 0:
  534.7 99.2 reduce-scatter.7
  636.3 189.1 reduce-scatter.3
  984.9 189.1 reduce-scatter.5
where the time goes:
time: 1200 us; the launch traced here: 1190 us
  waiting for transfers between devices  741 us (62%)
  matrix products  213 us (18%)
  local copies, waits for them, and re-layouts  181 us (15%)
  starting transfers between devices  21.6 us (2%)
  other arithmetic  15.7 us (1%)
  between operations  14 us (1%)
    all_to_all x1, waiting for transfers between devices, body(): lax.all_to_all(grad_first, 'seq', split_axis=0, concat_axis=1, tiled=True)  173 us
    all_to_all x1, waiting for transfers between devices, body(): lax.all_to_all(grad_third, 'seq', split_axis=1, concat_axis=0, tiled=True)  157 us
    all_to_all x1, waiting for transfers between devices, body(): lax.all_to_all(first, 'seq', split_axis=1, concat_axis=0, tiled=True)  156 us
    all_to_all x1, waiting for transfers between devices, body(): lax.all_to_all(third, 'seq', split_axis=0, concat_axis=1, tiled=True)  152 us
    reduce_scatter x1, waiting for transfers between devices, body(): lax.psum_scatter(grad_block_one, 'dp', scatter_dimension=2, tiled=True)  103 us
    unnamed x7, local copies, waits for them, and re-layouts  83.3 us
  transfers between devices with their start and end apart: 7, of which 5 were waited for; matrix products, arithmetic and copies ran while one was open for 21% of the time, Pallas kernels for 0%

commit v1 on v0

v1 whole, which is shorter than its diff:
```python
import jax
import jax.numpy as jnp
from jax import lax
from jax.sharding import PartitionSpec as P


def to_cols(x):
    return lax.all_to_all(x, "seq", split_axis=1, concat_axis=0, tiled=True)


def to_rows(x):
    return lax.all_to_all(x, "seq", split_axis=0, concat_axis=1, tiled=True)


def held(x):
    return lax.optimization_barrier(x)


def body(inputs, gate_logits, kernel, cotangent, block_one, block_two):
    tokens = inputs[0]
    kernel_wide = kernel.astype(jnp.float32)
    grad_scale = (lax.axis_size("dp") * tokens.shape[2]) ** (-0.5)
    f32 = jnp.float32

    opened = jax.nn.sigmoid(gate_logits[0].astype(f32))
    incoming = cotangent[0].astype(f32)
    grad_fourth = held((incoming * opened).astype(jnp.bfloat16))
    grad_third = jnp.einsum(
        "fch,fhd->fcd", block_one, grad_fourth, preferred_element_type=f32
    ).astype(jnp.bfloat16)
    grad_third_cols = to_cols(held(grad_third))

    first = jnp.einsum(
        "acb,abd->acd", block_one, tokens, preferred_element_type=f32
    ).astype(jnp.bfloat16)
    first, grad_third_cols = held((first, grad_third_cols))
    first_cols = to_cols(first)

    grad_filtered = held(
        jnp.einsum("cef,fcd->ecd", block_two, grad_third_cols, preferred_element_type=f32)
    )
    grad_second = (kernel_wide * grad_filtered).astype(jnp.bfloat16)
    grad_first = jnp.einsum(
        "cea,ecd->acd", block_two, grad_second, preferred_element_type=f32
    ).astype(jnp.bfloat16)
    grad_first, first_cols = held((grad_first, first_cols))
    grad_first_rows = to_rows(grad_first)

    second = held(
        jnp.einsum("cea,acd->ecd", block_two, first_cols, preferred_element_type=f32)
    )
    filtered = (kernel_wide * second).astype(jnp.bfloat16)
    third = jnp.einsum(
        "cef,ecd->fcd", block_two, filtered, preferred_element_type=f32
    ).astype(jnp.bfloat16)
    third, grad_first_rows = held((third, grad_first_rows))
    third_rows = to_rows(third)

    grad_kernel = (grad_filtered * second).astype(jnp.bfloat16)
    grad_block_two = (
        (
            jnp.einsum("fcd,ecd->cef", grad_third_cols, filtered, preferred_element_type=f32)
            + jnp.einsum("ecd,acd->cea", grad_second, first_cols, preferred_element_type=f32)
        )
        * grad_scale
    ).astype(jnp.bfloat16)
    grad_kernel = lax.psum_scatter(grad_kernel, "dp", scatter_dimension=2, tiled=True)
    grad_block_two = lax.psum_scatter(grad_block_two, "dp", scatter_dimension=2, tiled=True)

    grad_tokens = jnp.einsum(
        "acb,acd->abd", block_one, grad_first_rows, preferred_element_type=f32
    ).astype(jnp.bfloat16)
    outer_inputs = jnp.einsum(
        "acd,abd->acb", grad_first_rows, tokens, preferred_element_type=f32
    )

    fourth = jnp.einsum(
        "fch,fcd->fhd", block_one, third_rows, preferred_element_type=f32
    ).astype(jnp.bfloat16)
    fourth_wide = fourth.astype(f32)
    output = (opened * fourth_wide).astype(jnp.bfloat16)
    grad_gate = (incoming * fourth_wide * opened * (1.0 - opened)).astype(jnp.bfloat16)
    outer_one = jnp.einsum(
        "fhd,fcd->fch", grad_fourth, third_rows, preferred_element_type=f32
    )
    grad_block_one = ((outer_one + outer_inputs) * grad_scale).astype(jnp.bfloat16)
    grad_block_one = lax.psum_scatter(grad_block_one, "dp", scatter_dimension=2, tiled=True)
    return (
        output[None],
        grad_tokens[None],
        grad_gate[None],
        grad_kernel,
        grad_block_one,
        grad_block_two,
    )


def solution(mesh):
    return jax.shard_map(
        body,
        mesh=mesh,
        in_specs=(
            P("dp", "seq", None, None),
            P("dp", "seq", None, None),
            P(None, "seq", None),
            P("dp", "seq", None, None),
            P("seq", None, None),
            P("seq", None, None),
        ),
        out_specs=(
            P("dp", "seq", None, None),
            P("dp", "seq", None, None),
            P("dp", "seq", None, None),
            P(None, "seq", "dp"),
            P("seq", None, "dp"),
            P("seq", None, "dp"),
        ),
        check_vma=False,
    )
```

time: 1200 us -> 1030 us (0.86)
  waiting for transfers between devices: 741 us -> 570 us
  matrix products: 213 us -> 189 us
  local copies, waits for them, and re-layouts: 181 us -> 198 us
    reduce_scatter x1, waiting for transfers between devices: 103 us -> 16.7 us  [body(): lax.psum_scatter(grad_block_one, 'dp', scatter_dimension=2, tiled=True)]
    all_to_all x4, waiting for transfers between devices: 638 us -> 553 us  [the longest x2 302 us: to_cols(): return lax.all_to_all(x, 'seq', split_axis=1, concat_axis=0, tiled=True)]
    optimization_barrier x0 -> x4, local copies, waits for them, and re-layouts: none -> 56 us  [held(): return lax.optimization_barrier(x)]
    convert_element_type x4 -> x0, local copies, waits for them, and re-layouts: 55.8 us -> none  [the longest x1 14.9 us: body(): grad_third = jnp.einsum('fch,fhd->fcd', block_one, grad_fourth, preferred...]
    unnamed x7 -> x11, local copies, waits for them, and re-layouts: 83.3 us -> 105 us
    convert_element_type x3 -> x2, other arithmetic: 15.7 us -> 26.3 us  [the longest x1 14.9 us: body(): grad_kernel = (grad_filtered * second).astype(jnp.bfloat16)]
  transfers between devices with their start and end apart: 7 -> 7, of which waited for: 5 -> 5; matrix products, arithmetic and copies ran while one was open for 21% -> 30% of each run, Pallas kernels for 0% -> 0%
where the time goes in v1:
time: 1030 us; the launch traced here: 1020 us
  waiting for transfers between devices  570 us (55%)
  local copies, waits for them, and re-layouts  198 us (19%)
  matrix products  189 us (18%)
  other arithmetic  26.3 us (3%)
  starting transfers between devices  21.7 us (2%)
  between operations  14 us (1%)
    all_to_all x2, waiting for transfers between devices, to_cols(): return lax.all_to_all(x, 'seq', split_axis=1, concat_axis=0, tiled=True)  302 us
    all_to_all x2, waiting for transfers between devices, to_rows(): return lax.all_to_all(x, 'seq', split_axis=0, concat_axis=1, tiled=True)  251 us
    unnamed x11, local copies, waits for them, and re-layouts  105 us
    optimization_barrier x4, local copies, waits for them, and re-layouts, held(): return lax.optimization_barrier(x)  56 us
    dot_general x1, matrix products, body(): jnp.einsum('fcd,ecd->cef', grad_third_cols, filtered, preferred_element_t...  21.2 us
  transfers between devices with their start and end apart: 7, of which 5 were waited for; matrix products, arithmetic and copies ran while one was open for 30% of the time, Pallas kernels for 0%

profile of v1, /device:TPU:10, one launch (start us, length us, event | category | flops | bytes accessed | tf_op | source)
XLA Modules:
  0.0 1019.1 jit_solution(17853031852421777675)
XLA Ops:
  7.2 12.3 %copy.71 = bf16[1,16,512,512]{2,3,1,0:T(8,128)(2,1)} copy(bf16[1,16,512,512]{3,2,1,0:T(8,128)(2,1)} %param.7) | data formatting | bytes 16777216 | tf_op args[1]
  19.4 12.3 %copy.73 = bf16[1,16,512,512]{2,3,1,0:T(8,128)(2,1)} copy(bf16[1,16,512,512]{3,2,1,0:T(8,128)(2,1)} %param.9) | data formatting | bytes 16777216 | tf_op args[3]
  31.7 11.4 %fusion.2 = bf16[16,512,512]{1,2,0:T(8,128)(2,1)} fusion(bf16[1,16,512,512]{2,3,1,0:T(8,128)(2,1)} %copy.73, bf16[1,16,512,512]{2,3,1,0:T(8,128)(2,1)} %copy.71), kind=kLoop, calls=%fused_computation.6 | loop fusion | flops 29360128 | bytes 25165824 | tf_op jit(solution)/shard_map/convert_element_type | solution.py:27
  43.1 11.5 %convert_bitcast_fusion.3 = bf16[16,512,512]{1,2,0:T(8,128)(2,1)} fusion(bf16[16,512,512]{1,2,0:T(8,128)(2,1)} %fusion.2, bf16[16,512,512]{2,1,0:T(8,128)(2,1)} %param.10), kind=kOutput, calls=%fused_computation.28 | convolution fusion | flops 4299161600 | bytes 25165824 | tf_op jit(solution)/shard_map/fch,fhd->fcd/dot_general | solution.py:28
  54.5 14.9 %copy.74 = bf16[16,512,512]{2,0,1:T(8,128)(2,1)} copy(bf16[16,512,512]{1,2,0:T(8,128)(2,1)} %convert_bitcast_fusion.3) | data formatting | bytes 16777216 | tf_op jit(solution)/shard_map/optimization_barrier | solution.py:16
  75.8 13.7 %fusion.16 = bf16[16,512,512]{2,1,0:T(8,128)(2,1)} fusion(bf16[16,512,512]{2,1,0:T(8,128)(2,1)} %param.10, bf16[1,16,512,512]{3,2,1,0:T(8,128)(2,1)} %param.6), kind=kOutput, calls=%fused_computation.32 | convolution fusion | flops 4299161600 | bytes 25165824 | tf_op jit(solution)/shard_map/acb,abd->acd/dot_general | solution.py:33
  89.5 168.2 %all-to-all-done = bf16[16,512,512]{2,0,1:T(8,128)(2,1)} async-done(((bf16[16,512,512]{2,0,1:T(8,128)(2,1)}), bf16[16,512,512]{2,0,1:T(8,128)(2,1)}, u32[]{:S(2)}, u32[]{:S(2)}) %all-to-all-start) | async-done | bytes 8388640 | tf_op jit(solution)/shard_map/all_to_all | solution.py:8
  257.7 12.3 %copy.76 = bf16[16,16,32,512]{3,2,1,0:T(8,128)(2,1)} copy(bf16[16,16,32,512]{3,1,2,0:T(8,128)(2,1)} %bitcast.6) | data formatting | bytes 16777216 | tf_op jit(solution)/shard_map/all_to_all | solution.py:8
  270.0 11.7 %copy.78 = bf16[16,512,512]{2,0,1:T(8,128)(2,1)} copy(bf16[16,512,512]{2,1,0:T(8,128)(2,1)} %fusion.16) | data formatting | bytes 16777216 | tf_op jit(solution)/shard_map/optimization_barrier | solution.py:16
  286.8 13.7 %copy.72 = bf16[256,32,512]{0,2,1:T(8,128)(2,1)} copy(bf16[256,32,512]{2,1,0:T(8,128)(2,1)} %param.8) | data formatting | bytes 16777216 | tf_op args[2]
  300.6 20.4 %convolution_bitcast_fusion.1 = f32[256,32,512]{0,2,1:T(8,128)} fusion(bf16[32,256,256]{2,1,0:T(8,128)(2,1)} %param.11, bf16[256,32,512]{2,1,0:T(8,128)(2,1)} %bitcast.90), kind=kOutput, calls=%fused_computation.17 | convolution fusion | flops 2147483648 | bytes 29360128 | tf_op jit(solution)/shard_map/cef,fcd->ecd/dot_general | solution.py:40
  320.9 14.2 %convert_bitcast_fusion.2 = bf16[256,32,512]{0,2,1:T(8,128)(2,1)} fusion(bf16[32,256,256]{2,1,0:T(8,128)(2,1)} %param.11, f32[256,32,512]{0,2,1:T(8,128)} %convolution_bitcast_fusion.1, bf16[256,32,512]{0,2,1:T(8,128)(2,1)} %copy.72), kind=kOutput, calls=%fused_computation.27 | convolution fusion | flops 2164260864 | bytes 37748736 | tf_op jit(solution)/shard_map/cea,ecd->acd/dot_general | solution.py:43
  335.2 133.7 %all-to-all-done.1 = bf16[16,512,512]{2,0,1:T(8,128)(2,1)} async-done(((bf16[16,512,512]{2,0,1:T(8,128)(2,1)}), bf16[16,512,512]{2,0,1:T(8,128)(2,1)}, u32[]{:S(2)}, u32[]{:S(2)}) %all-to-all-start.1) | async-done | bytes 8388640 | tf_op jit(solution)/shard_map/all_to_all | solution.py:8
  477.1 14.7 %copy.81 = bf16[256,32,512]{2,1,0:T(8,128)(2,1)} copy(bf16[256,32,512]{0,2,1:T(8,128)(2,1)} %convert_bitcast_fusion.2) | data formatting | bytes 16777216 | tf_op jit(solution)/shard_map/optimization_barrier | solution.py:16
  496.9 12.8 %convolution_bitcast_fusion = f32[256,32,512]{0,2,1:T(8,128)} fusion(bf16[256,32,512]{2,0,1:T(8,128)(2,1)} %bitcast.88, bf16[32,256,256]{2,1,0:T(8,128)(2,1)} %param.11), kind=kOutput, calls=%fused_computation.16 | convolution fusion | flops 2147483648 | bytes 29360128 | tf_op jit(solution)/shard_map/cea,acd->ecd/dot_general | solution.py:50
  509.7 21.2 %fusion.14 = f32[32,256,256]{2,1,0:T(8,128)} fusion(bf16[256,32,512]{2,1,0:T(8,128)(2,1)} %bitcast.91, f32[256,32,512]{0,2,1:T(8,128)} %convolution_bitcast_fusion, bf16[256,32,512]{0,2,1:T(8,128)(2,1)} %copy.72), kind=kOutput, calls=%fused_computation.30 | convolution fusion | flops 2160066560 | bytes 41943040 | tf_op jit(solution)/shard_map/fcd,ecd->cef/dot_general | solution.py:62
  530.8 16.4 %multiply_convert_fusion.2 = bf16[32,256,256]{2,1,0:T(8,128)(2,1)} fusion(f32[32,256,256]{2,1,0:T(8,128)} %fusion.14, bf16[256,32,512]{2,0,1:T(8,128)(2,1)} %bitcast.89, f32[256,32,512]{0,2,1:T(8,128)} %convolution_bitcast_fusion.1, bf16[256,32,512]{0,2,1:T(8,128)(2,1)} %copy.72), kind=kOutput, calls=%fused_computation.24 | convolution fusion | flops 2166358016 | bytes 46137344 | tf_op jit(solution)/shard_map/ecd,acd->cea/dot_general | solution.py:63
  555.5 8.5 copy.104
  564.0 14.6 %convert_bitcast_fusion.1 = bf16[256,32,512]{0,2,1:T(8,128)(2,1)} fusion(bf16[32,256,256]{2,1,0:T(8,128)(2,1)} %param.11, f32[256,32,512]{0,2,1:T(8,128)} %convolution_bitcast_fusion, bf16[256,32,512]{0,2,1:T(8,128)(2,1)} %copy.72), kind=kOutput, calls=%fused_computation.26 | convolution fusion | flops 2164260864 | bytes 37748736 | tf_op jit(solution)/shard_map/cef,ecd->fcd/dot_general | solution.py:53
  578.5 100.4 %all-to-all-done.2 = bf16[256,32,512]{2,1,0:T(8,128)(2,1)} async-done(((bf16[256,32,512]{2,1,0:T(8,128)(2,1)}), bf16[256,32,512]{2,1,0:T(8,128)(2,1)}, u32[]{:S(2)}, u32[]{:S(2)}) %all-to-all-start.2) | async-done | bytes 8388640 | tf_op jit(solution)/shard_map/all_to_all | solution.py:12
  687.2 14.7 %copy.83 = bf16[256,32,512]{2,1,0:T(8,128)(2,1)} copy(bf16[256,32,512]{0,2,1:T(8,128)(2,1)} %convert_bitcast_fusion.1) | data formatting | bytes 16777216 | tf_op jit(solution)/shard_map/optimization_barrier | solution.py:16
  707.0 14.9 %multiply_convert_fusion.1 = bf16[256,32,512]{0,2,1:T(8,128)(2,1)} fusion(f32[256,32,512]{0,2,1:T(8,128)} %convolution_bitcast_fusion.1, f32[256,32,512]{0,2,1:T(8,128)} %convolution_bitcast_fusion), kind=kLoop, calls=%fused_computation.14 | loop fusion | flops 8388608 | bytes 41943040 | tf_op jit(solution)/shard_map/convert_element_type | solution.py:59
  721.9 16.1 %fusion.9 = f32[16,512,512]{2,1,0:T(8,128)} fusion(bf16[16,512,512]{2,1,0:T(8,128)(2,1)} %bitcast.92, bf16[1,16,512,512]{3,2,1,0:T(8,128)(2,1)} %param.6), kind=kOutput, calls=%fused_computation.20 | convolution fusion | flops 4294967296 | bytes 33554432 | tf_op jit(solution)/shard_map/acd,abd->acb/dot_general | solution.py:73
  738.0 151.0 %all-to-all-done.3 = bf16[256,32,512]{2,1,0:T(8,128)(2,1)} async-done(((bf16[256,32,512]{2,1,0:T(8,128)(2,1)}), bf16[256,32,512]{2,1,0:T(8,128)(2,1)}, u32[]{:S(2)}, u32[]{:S(2)}) %all-to-all-start.3) | async-done | bytes 8388640 | tf_op jit(solution)/shard_map/all_to_all | solution.py:12
  889.0 8.3 copy.84
  897.3 15.7 %multiply_convert_fusion = bf16[16,512,512]{2,1,0:T(8,128)(2,1)} fusion(f32[16,512,512]{2,1,0:T(8,128)} %fusion.9, bf16[16,512,512]{2,1,0:T(8,128)(2,1)} %bitcast.94, bf16[16,512,512]{1,2,0:T(8,128)(2,1)} %fusion.2), kind=kOutput, calls=%fused_computation.13 | convolution fusion | flops 4307550208 | bytes 41943040 | tf_op jit(solution)/shard_map/fhd,fcd->fch/dot_general | solution.py:83
  918.2 12.1 %convert_bitcast_fusion = bf16[1,16,512,512]{2,3,1,0:T(8,128)(2,1)} fusion(bf16[16,512,512]{2,1,0:T(8,128)(2,1)} %bitcast.93, bf16[16,512,512]{2,1,0:T(8,128)(2,1)} %param.10), kind=kOutput, calls=%fused_computation.25 | convolution fusion | flops 4299161600 | bytes 25165824 | tf_op jit(solution)/shard_map/acb,acd->abd/dot_general | solution.py:70
  930.3 12.3 %copy.92 = bf16[1,16,512,512]{3,2,1,0:T(8,128)(2,1)} copy(bf16[1,16,512,512]{2,3,1,0:T(8,128)(2,1)} %convert_bitcast_fusion) | data formatting | bytes 16777216
  950.5 20.6 %fusion.8 = (bf16[1,16,512,512]{2,3,1,0:T(8,128)(2,1)}, bf16[1,16,512,512]{2,3,1,0:T(8,128)(2,1)}) fusion(bf16[1,16,512,512]{2,3,1,0:T(8,128)(2,1)} %copy.73, bf16[1,16,512,512]{2,3,1,0:T(8,128)(2,1)} %copy.71, bf16[16,512,512]{2,1,0:T(8,128)(2,1)} %bitcast.95, bf16[16,512,512]{2,1,0:T(8,128)(2,1)} %param.10), kind=kOutput, calls=%fused_computation.19 | convolution fusion | flops 4353687552 | bytes 50331648 | tf_op jit(solution)/shard_map/fch,fcd->fhd/dot_general | solution.py:77
  971.1 12.4 %copy.93 = bf16[1,16,512,512]{3,2,1,0:T(8,128)(2,1)} copy(bf16[1,16,512,512]{2,3,1,0:T(8,128)(2,1)} %get-tuple-element.42) | data formatting | bytes 16777216
  983.5 12.3 %copy.91 = bf16[1,16,512,512]{3,2,1,0:T(8,128)(2,1)} copy(bf16[1,16,512,512]{2,3,1,0:T(8,128)(2,1)} %get-tuple-element.43) | data formatting | bytes 16777216
  995.8 16.7 %reduce-scatter.8.cloned.1.call-done = bf16[16,512,256]{2,1,0:T(8,128)(2,1)} async-done(((bf16[16,512,512]{2,1,0:T(8,128)(2,1)}), bf16[16,512,256]{2,1,0:T(8,128)(2,1)}) %reduce-scatter.8.cloned.1.call-update) | async-done | bytes 4194320 | tf_op jit(solution)/shard_map/reduce_scatter | solution.py:87
  (18 shorter events, 59.6 us)
Async XLA Ops:
  69.4 188.3 %all-to-all-start = ((bf16[16,512,512]{2,0,1:T(8,128)(2,1)}), bf16[16,512,512]{2,0,1:T(8,128)(2,1)}, u32[]{:S(2)}, u32[]{:S(2)}) async-start(bf16[16,512,512]{2,0,1:T(8,128)(2,1)} %copy.74), calls=%async_computation | async-start | bytes 16777216 | tf_op jit(solution)/shard_map/all_to_all | solution.py:8
  281.8 187.1 %all-to-all-start.1 = ((bf16[16,512,512]{2,0,1:T(8,128)(2,1)}), bf16[16,512,512]{2,0,1:T(8,128)(2,1)}, u32[]{:S(2)}, u32[]{:S(2)}) async-start(bf16[16,512,512]{2,0,1:T(8,128)(2,1)} %copy.78), calls=%async_computation.1 | async-start | bytes 16777216 | tf_op jit(solution)/shard_map/all_to_all | solution.py:8
  491.8 187.1 %all-to-all-start.2 = ((bf16[256,32,512]{2,1,0:T(8,128)(2,1)}), bf16[256,32,512]{2,1,0:T(8,128)(2,1)}, u32[]{:S(2)}, u32[]{:S(2)}) async-start(bf16[256,32,512]{2,1,0:T(8,128)(2,1)} %copy.81), calls=%async_computation.2 | async-start | bytes 16777216 | tf_op jit(solution)/shard_map/all_to_all | solution.py:12
  496.9 416.1 %reduce-scatter.10.cloned.1.call-start = ((), (), s32[]{:S(2)}) async-start(), calls=%async_computation.9 | async-start | bytes 6291456
  701.9 187.1 %all-to-all-start.3 = ((bf16[256,32,512]{2,1,0:T(8,128)(2,1)}), bf16[256,32,512]{2,1,0:T(8,128)(2,1)}, u32[]{:S(2)}, u32[]{:S(2)}) async-start(bf16[256,32,512]{2,1,0:T(8,128)(2,1)} %copy.83), calls=%async_computation.3 | async-start | bytes 16777216 | tf_op jit(solution)/shard_map/all_to_all | solution.py:12
  706.9 235.7 %reduce-scatter.6.cloned.1.call-start = ((), (), s32[]{:S(2)}) async-start(), calls=%async_computation.7 | async-start | bytes 12582912 | tf_op jit(solution)/shard_map/reduce_scatter | solution.py:67
  721.9 290.5 %reduce-scatter.8.cloned.1.call-start = ((), (), s32[]{:S(2)}) async-start(), calls=%async_computation.8 | async-start | bytes 12582912 | tf_op jit(solution)/shard_map/reduce_scatter | solution.py:87
Sparse Core Ops, SparseCore 0:
  564.1 55.2 reduce-scatter.9
  722.0 100.2 reduce-scatter.5
  913.1 99.3 reduce-scatter.7

commit v2 on v1

--- a/solution.py
+++ b/solution.py
@@ -14,6 +14,22 @@
 
 def held(x):
     return lax.optimization_barrier(x)
+
+
+def dp_reduce_scatter(x, dim):
+    n = lax.axis_size("dp")
+    me = lax.axis_index("dp")
+    size = x.shape[dim] // n
+    total = lax.dynamic_slice_in_dim(x, me * size, size, axis=dim)
+    for shift in range(1, n):
+        target = lax.rem(me + shift, n)
+        part = lax.dynamic_slice_in_dim(x, target * size, size, axis=dim)
+        total = total + lax.ppermute(
+            part.astype(jnp.bfloat16),
+            "dp",
+            [(i, (i + shift) % n) for i in range(n)],
+        ).astype(jnp.float32)
+    return total.astype(jnp.bfloat16)
 
 
 def body(inputs, gate_logits, kernel, cotangent, block_one, block_two):
@@ -53,8 +69,28 @@
     third = jnp.einsum(
         "cef,ecd->fcd", block_two, filtered, preferred_element_type=f32
     ).astype(jnp.bfloat16)
-    third, grad_first_rows = held((third, grad_first_rows))
-    third_rows = to_rows(third)
+    n_seq = lax.axis_size("seq")
+    own = third.shape[0] // n_seq
+    half = own // 2
+    halves = ((0, half), (half, own)) if half else ((0, own),)
+    third_split = third.reshape((n_seq, own) + third.shape[1:])
+    third_split, grad_first_rows = held((third_split, grad_first_rows))
+
+    def finish(lo, hi, third_rows):
+        fourth = jnp.einsum(
+            "fch,fcd->fhd", block_one[lo:hi], third_rows, preferred_element_type=f32
+        ).astype(jnp.bfloat16)
+        fourth_wide = fourth.astype(f32)
+        opened_k = opened[lo:hi]
+        output = (opened_k * fourth_wide).astype(jnp.bfloat16)
+        grad_gate = (
+            incoming[lo:hi] * fourth_wide * opened_k * (1.0 - opened_k)
+        ).astype(jnp.bfloat16)
+        outer_one = jnp.einsum(
+            "fhd,fcd->fch", grad_fourth[lo:hi], third_rows, preferred_element_type=f32
+        )
+        partial = (outer_one + outer_inputs[lo:hi]) * grad_scale
+        return output, grad_gate, dp_reduce_scatter(partial, 2)
 
     grad_kernel = (grad_filtered * second).astype(jnp.bfloat16)
     grad_block_two = (
@@ -74,17 +110,24 @@
         "acd,abd->acb", grad_first_rows, tokens, preferred_element_type=f32
     )
 
-    fourth = jnp.einsum(
-        "fch,fcd->fhd", block_one, third_rows, preferred_element_type=f32
-    ).astype(jnp.bfloat16)
-    fourth_wide = fourth.astype(f32)
-    output = (opened * fourth_wide).astype(jnp.bfloat16)
-    grad_gate = (incoming * fourth_wide * opened * (1.0 - opened)).astype(jnp.bfloat16)
-    outer_one = jnp.einsum(
-        "fhd,fcd->fch", grad_fourth, third_rows, preferred_element_type=f32
-    )
-    grad_block_one = ((outer_one + outer_inputs) * grad_scale).astype(jnp.bfloat16)
-    grad_block_one = lax.psum_scatter(grad_block_one, "dp", scatter_dimension=2, tiled=True)
+    outputs, grad_gates, grad_block_ones = [], [], []
+    pending = None
+    for lo, hi in halves:
+        piece = third_split[:, lo:hi].reshape((-1,) + third.shape[1:])
+        if pending is not None:
+            piece, arrived = held((piece, pending[2]))
+            outputs_k = finish(pending[0], pending[1], arrived)
+            outputs.append(outputs_k[0])
+            grad_gates.append(outputs_k[1])
+            grad_block_ones.append(outputs_k[2])
+        pending = (lo, hi, to_rows(piece))
+    outputs_k = finish(*pending)
+    outputs.append(outputs_k[0])
+    grad_gates.append(outputs_k[1])
+    grad_block_ones.append(outputs_k[2])
+    output = jnp.concatenate(outputs, axis=0)
+    grad_gate = jnp.concatenate(grad_gates, axis=0)
+    grad_block_one = jnp.concatenate(grad_block_ones, axis=0)
     return (
         output[None],
         grad_tokens[None],

time: 1030 us -> 1000 us (0.971)
  waiting for transfers between devices: 570 us -> 482 us
  other arithmetic: 26.3 us -> 63.2 us
  local copies, waits for them, and re-layouts: 198 us -> 211 us
    all_to_all x2 -> x3, waiting for transfers between devices: 251 us -> 180 us  [to_rows(): return lax.all_to_all(x, 'seq', split_axis=0, concat_axis=1, tiled=True)]
    reduce_scatter x1 -> x0, waiting for transfers between devices: 16.7 us -> none  [body(): lax.psum_scatter(grad_block_one, 'dp', scatter_dimension=2, tiled=True)]
    slice x0 -> x3, local copies, waits for them, and re-layouts: none -> 16.3 us  [body(): piece = third_split[:, lo:hi].reshape((-1,) + third.shape[1:])]
    div x0 -> x1, other arithmetic: none -> 15.8 us  [body(): opened = jax.nn.sigmoid(gate_logits[0].astype(f32))]
    optimization_barrier x4 -> x3, local copies, waits for them, and re-layouts: 56 us -> 41.3 us  [held(): return lax.optimization_barrier(x)]
    broadcast_in_dim x0 -> x1, other arithmetic: none -> 11.5 us  [body(): output[None]]
    unnamed x11 -> x21, local copies, waits for them, and re-layouts: 105 us -> 113 us
    dot_general x2 -> x4, matrix products: 36.3 us -> 43 us  [the longest x2 28.6 us: finish(): jnp.einsum('fch,fcd->fhd', block_one[lo:hi], third_rows, preferred_elemen...]
  transfers between devices with their start and end apart: 7 -> 9, of which waited for: 5 -> 5; matrix products, arithmetic and copies ran while one was open for 30% -> 33% of each run, Pallas kernels for 0% -> 0%
where the time goes in v2:
time: 1000 us; the launch traced here: 996 us
  waiting for transfers between devices  482 us (48%)
  local copies, waits for them, and re-layouts  211 us (21%)
  matrix products  196 us (20%)
  other arithmetic  63.2 us (6%)
  starting transfers between devices  30.1 us (3%)
  between operations  14.4 us (1%)
    all_to_all x2, waiting for transfers between devices, to_cols(): return lax.all_to_all(x, 'seq', split_axis=1, concat_axis=0, tiled=True)  302 us
    all_to_all x3, waiting for transfers between devices, to_rows(): return lax.all_to_all(x, 'seq', split_axis=0, concat_axis=1, tiled=True)  180 us
    unnamed x21, local copies, waits for them, and re-layouts  113 us
    optimization_barrier x3, local copies, waits for them, and re-layouts, held(): return lax.optimization_barrier(x)  41.3 us
    dot_general x2, matrix products, finish(): jnp.einsum('fch,fcd->fhd', block_one[lo:hi], third_rows, preferred_elemen...  28.6 us
    dot_general x1, matrix products, body(): jnp.einsum('fcd,ecd->cef', grad_third_cols, filtered, preferred_element_t...  21.1 us
    all_to_all x2, local copies, waits for them, and re-layouts, to_cols(): return lax.all_to_all(x, 'seq', split_axis=1, concat_axis=0, tiled=True)  20.6 us
    dot_general x1, matrix products, body(): jnp.einsum('cef,fcd->ecd', block_two, grad_third_cols, preferred_element_...  20.4 us
  transfers between devices with their start and end apart: 9, of which 5 were waited for; matrix products, arithmetic and copies ran while one was open for 33% of the time, Pallas kernels for 0%

profile of v2, /device:TPU:10, one launch (start us, length us, event | category | flops | bytes accessed | tf_op | source)
XLA Modules:
  0.0 995.8 jit_solution(5992362893387498019)
XLA Ops:
  7.2 12.3 %copy.87 = bf16[1,16,512,512]{2,3,1,0:T(8,128)(2,1)} copy(bf16[1,16,512,512]{3,2,1,0:T(8,128)(2,1)} %param.9) | data formatting | bytes 16777216 | tf_op args[3]
  19.4 12.3 %copy.85 = bf16[1,16,512,512]{2,3,1,0:T(8,128)(2,1)} copy(bf16[1,16,512,512]{3,2,1,0:T(8,128)(2,1)} %param.7) | data formatting | bytes 16777216 | tf_op args[1]
  31.7 15.8 %add_divide_fusion = (f32[1,16,512,512]{2,3,1,0:T(8,128)}, bf16[16,512,512]{1,2,0:T(8,128)(2,1)}) fusion(bf16[1,16,512,512]{2,3,1,0:T(8,128)(2,1)} %copy.85, bf16[1,16,512,512]{2,3,1,0:T(8,128)(2,1)} %copy.87), kind=kLoop, calls=%fused_computation.6 | loop fusion | flops 29360128 | bytes 41943040 | tf_op jit(solution)/shard_map/div | solution.py:41
  47.5 11.5 %convert_bitcast_fusion.2 = bf16[16,512,512]{1,2,0:T(8,128)(2,1)} fusion(bf16[16,512,512]{1,2,0:T(8,128)(2,1)} %get-tuple-element.51, bf16[16,512,512]{2,1,0:T(8,128)(2,1)} %param.10), kind=kOutput, calls=%fused_computation.39 | convolution fusion | flops 4299161600 | bytes 25165824 | tf_op jit(solution)/shard_map/fch,fhd->fcd/dot_general | solution.py:44
  59.0 14.9 %copy.88 = bf16[16,512,512]{2,0,1:T(8,128)(2,1)} copy(bf16[16,512,512]{1,2,0:T(8,128)(2,1)} %convert_bitcast_fusion.2) | data formatting | bytes 16777216 | tf_op jit(solution)/shard_map/optimization_barrier | solution.py:16
  80.2 13.7 %fusion.22 = bf16[16,512,512]{2,1,0:T(8,128)(2,1)} fusion(bf16[16,512,512]{2,1,0:T(8,128)(2,1)} %param.10, bf16[1,16,512,512]{3,2,1,0:T(8,128)(2,1)} %param.6), kind=kOutput, calls=%fused_computation.43 | convolution fusion | flops 4299161600 | bytes 25165824 | tf_op jit(solution)/shard_map/acb,abd->acd/dot_general | solution.py:49
  93.9 168.2 %all-to-all-done = bf16[16,512,512]{2,0,1:T(8,128)(2,1)} async-done(((bf16[16,512,512]{2,0,1:T(8,128)(2,1)}), bf16[16,512,512]{2,0,1:T(8,128)(2,1)}, u32[]{:S(2)}, u32[]{:S(2)}) %all-to-all-start) | async-done | bytes 8388640 | tf_op jit(solution)/shard_map/all_to_all | solution.py:8
  262.2 12.3 %copy.90 = bf16[16,16,32,512]{3,2,1,0:T(8,128)(2,1)} copy(bf16[16,16,32,512]{3,1,2,0:T(8,128)(2,1)} %bitcast.6) | data formatting | bytes 16777216 | tf_op jit(solution)/shard_map/all_to_all | solution.py:8
  274.5 11.7 %copy.92 = bf16[16,512,512]{2,0,1:T(8,128)(2,1)} copy(bf16[16,512,512]{2,1,0:T(8,128)(2,1)} %fusion.22) | data formatting | bytes 16777216 | tf_op jit(solution)/shard_map/optimization_barrier | solution.py:16
  291.3 13.7 %copy.86 = bf16[256,32,512]{0,2,1:T(8,128)(2,1)} copy(bf16[256,32,512]{2,1,0:T(8,128)(2,1)} %param.8) | data formatting | bytes 16777216 | tf_op args[2]
  305.0 20.4 %convolution_bitcast_fusion.1 = f32[256,32,512]{0,2,1:T(8,128)} fusion(bf16[32,256,256]{2,1,0:T(8,128)(2,1)} %param.11, bf16[256,32,512]{2,1,0:T(8,128)(2,1)} %bitcast.117), kind=kOutput, calls=%fused_computation.8 | convolution fusion | flops 2147483648 | bytes 29360128 | tf_op jit(solution)/shard_map/cef,fcd->ecd/dot_general | solution.py:56
  325.4 14.3 %convert_bitcast_fusion.1 = bf16[256,32,512]{0,2,1:T(8,128)(2,1)} fusion(bf16[32,256,256]{2,1,0:T(8,128)(2,1)} %param.11, f32[256,32,512]{0,2,1:T(8,128)} %convolution_bitcast_fusion.1, bf16[256,32,512]{0,2,1:T(8,128)(2,1)} %copy.86), kind=kOutput, calls=%fused_computation.38 | convolution fusion | flops 2164260864 | bytes 37748736 | tf_op jit(solution)/shard_map/cea,ecd->acd/dot_general | solution.py:59
  339.7 133.7 %all-to-all-done.1 = bf16[16,512,512]{2,0,1:T(8,128)(2,1)} async-done(((bf16[16,512,512]{2,0,1:T(8,128)(2,1)}), bf16[16,512,512]{2,0,1:T(8,128)(2,1)}, u32[]{:S(2)}, u32[]{:S(2)}) %all-to-all-start.1) | async-done | bytes 8388640 | tf_op jit(solution)/shard_map/all_to_all | solution.py:8
  481.6 14.6 %copy.97 = bf16[256,32,512]{2,1,0:T(8,128)(2,1)} copy(bf16[256,32,512]{0,2,1:T(8,128)(2,1)} %convert_bitcast_fusion.1) | data formatting | bytes 16777216 | tf_op jit(solution)/shard_map/optimization_barrier | solution.py:16
  501.3 12.8 %convolution_bitcast_fusion = f32[256,32,512]{0,2,1:T(8,128)} fusion(bf16[256,32,512]{2,0,1:T(8,128)(2,1)} %bitcast.115, bf16[32,256,256]{2,1,0:T(8,128)(2,1)} %param.11), kind=kOutput, calls=%fused_computation.7 | convolution fusion | flops 2147483648 | bytes 29360128 | tf_op jit(solution)/shard_map/cea,acd->ecd/dot_general | solution.py:66
  514.1 21.1 %fusion.20 = f32[32,256,256]{2,1,0:T(8,128)} fusion(bf16[256,32,512]{2,1,0:T(8,128)(2,1)} %bitcast.118, f32[256,32,512]{0,2,1:T(8,128)} %convolution_bitcast_fusion, bf16[256,32,512]{0,2,1:T(8,128)(2,1)} %copy.86), kind=kOutput, calls=%fused_computation.41 | convolution fusion | flops 2160066560 | bytes 41943040 | tf_op jit(solution)/shard_map/fcd,ecd->cef/dot_general | solution.py:98
  535.2 16.5 %multiply_convert_fusion.2 = bf16[32,256,256]{2,1,0:T(8,128)(2,1)} fusion(f32[32,256,256]{2,1,0:T(8,128)} %fusion.20, bf16[256,32,512]{2,0,1:T(8,128)(2,1)} %bitcast.116, f32[256,32,512]{0,2,1:T(8,128)} %convolution_bitcast_fusion.1, bf16[256,32,512]{0,2,1:T(8,128)(2,1)} %copy.86), kind=kOutput, calls=%fused_computation.36 | convolution fusion | flops 2166358016 | bytes 46137344 | tf_op jit(solution)/shard_map/ecd,acd->cea/dot_general | solution.py:99
  559.9 8.4 copy.128
  568.4 15.4 %multiply_convert_fusion.1 = bf16[256,32,512]{0,2,1:T(8,128)(2,1)} fusion(f32[256,32,512]{0,2,1:T(8,128)} %convolution_bitcast_fusion.1, f32[256,32,512]{0,2,1:T(8,128)} %convolution_bitcast_fusion), kind=kLoop, calls=%fused_computation.5 | loop fusion | flops 8388608 | bytes 41943040 | tf_op jit(solution)/shard_map/convert_element_type | solution.py:95
  583.8 15.3 %convolution_convert_fusion = bf16[32,512,256]{1,2,0:T(8,128)(2,1)} fusion(bf16[32,256,256]{2,1,0:T(8,128)(2,1)} %param.11, f32[256,32,512]{0,2,1:T(8,128)} %convolution_bitcast_fusion, bf16[256,32,512]{0,2,1:T(8,128)(2,1)} %copy.86), kind=kOutput, calls=%fused_computation.44 | convolution fusion | flops 2164260864 | bytes 37748736 | tf_op jit(solution)/shard_map/cef,ecd->fcd/dot_general | solution.py:69
  599.1 84.2 %all-to-all-done.2 = bf16[256,32,512]{2,1,0:T(8,128)(2,1)} async-done(((bf16[256,32,512]{2,1,0:T(8,128)(2,1)}), bf16[256,32,512]{2,1,0:T(8,128)(2,1)}, u32[]{:S(2)}, u32[]{:S(2)}) %all-to-all-start.2) | async-done | bytes 8388640 | tf_op jit(solution)/shard_map/all_to_all | solution.py:12
  683.3 8.3 copy.98
  713.4 85.5 %all-to-all-done.3 = bf16[128,32,512]{2,1,0:T(8,128)(2,1)} async-done(((bf16[128,32,512]{2,1,0:T(8,128)(2,1)}), bf16[128,32,512]{2,1,0:T(8,128)(2,1)}, u32[]{:S(2)}, u32[]{:S(2)}) %all-to-all-start.3) | async-done | bytes 4194336 | tf_op jit(solution)/shard_map/all_to_all | solution.py:12
  808.7 16.1 %fusion.15 = f32[16,512,512]{2,1,0:T(8,128)} fusion(bf16[16,512,512]{2,1,0:T(8,128)(2,1)} %bitcast.119, bf16[1,16,512,512]{3,2,1,0:T(8,128)(2,1)} %param.6), kind=kOutput, calls=%fused_computation.32 | convolution fusion | flops 4294967296 | bytes 33554432 | tf_op jit(solution)/shard_map/acd,abd->acb/dot_general | solution.py:109
  839.3 11.4 %convert_element_type.108 = f32[1,16,512,512]{2,3,1,0:T(8,128)} convert(bf16[1,16,512,512]{2,3,1,0:T(8,128)(2,1)} %copy.87) | non-fusion elementwise | flops 4194304 | bytes 25165824 | tf_op jit(solution)/shard_map/convert_element_type | solution.py:42
  856.0 11.5 %convert_bitcast_fusion = bf16[1,16,512,512]{2,3,1,0:T(8,128)(2,1)} fusion(bf16[16,512,512]{2,1,0:T(8,128)(2,1)} %bitcast.120, bf16[16,512,512]{2,1,0:T(8,128)(2,1)} %param.10), kind=kOutput, calls=%fused_computation.37 | convolution fusion | flops 4299161600 | bytes 25165824 | tf_op jit(solution)/shard_map/acb,acd->abd/dot_general | solution.py:106
  867.5 12.3 %copy.112 = bf16[1,16,512,512]{3,2,1,0:T(8,128)(2,1)} copy(bf16[1,16,512,512]{2,3,1,0:T(8,128)(2,1)} %convert_bitcast_fusion) | data formatting | bytes 16777216
  891.1 9.8 all-to-all-done.4
  925.1 21.9 %fusion.12 = (bf16[8,512,512]{1,2,0:T(8,128)(2,1)}, bf16[8,512,512]{1,2,0:T(8,128)(2,1)}, bf16[8,512,512]{1,2,0:T(8,128)(2,1)}, bf16[8,512,512]{1,2,0:T(8,128)(2,1)}) fusion(f32[1,16,512,512]{2,3,1,0:T(8,128)} %convert_element_type.108, f32[1,16,512,512]{2,3,1,0:T(8,128)} %get-tuple-element.50, bf16[8,512,512]{2,1,0:T(8,128)(2,1)} %fusion.36, ...), kind=kOutput, calls=%fused_computation.23 | convolution fusion | flops 2183135232 | bytes 62914560 | tf_op jit(solution)/shard_map/fch,fcd->fhd/dot_general | solution.py:80
  947.0 11.5 %maximum_bitcast_fusion = (bf16[1,16,512,512]{2,3,1,0:T(8,128)(2,1)}, bf16[1,16,512,512]{2,3,1,0:T(8,128)(2,1)}) fusion(bf16[8,512,512]{1,2,0:T(8,128)(2,1)} %get-tuple-element.48, bf16[8,512,512]{1,2,0:T(8,128)(2,1)} %get-tuple-element.49, bf16[8,512,512]{1,2,0:T(8,128)(2,1)} %get-tuple-element.47, bf16[8,512,512]{1,2,0:T(8,128)(2,1)} %get-tuple-element.46), kind=kLoop, calls=%fused_computation.26 | loop fusion | flops 8388608 | bytes 33554432 | tf_op jit(solution)/shard_map/broadcast_in_dim | solution.py:132
  958.5 12.3 %copy.111 = bf16[1,16,512,512]{3,2,1,0:T(8,128)(2,1)} copy(bf16[1,16,512,512]{2,3,1,0:T(8,128)(2,1)} %get-tuple-element.54) | data formatting | bytes 16777216
  970.8 12.3 %copy.113 = bf16[1,16,512,512]{3,2,1,0:T(8,128)(2,1)} copy(bf16[1,16,512,512]{2,3,1,0:T(8,128)(2,1)} %get-tuple-element.55) | data formatting | bytes 16777216
  (44 shorter events, 125.6 us)
Async XLA Ops:
  73.8 188.3 %all-to-all-start = ((bf16[16,512,512]{2,0,1:T(8,128)(2,1)}), bf16[16,512,512]{2,0,1:T(8,128)(2,1)}, u32[]{:S(2)}, u32[]{:S(2)}) async-start(bf16[16,512,512]{2,0,1:T(8,128)(2,1)} %copy.88), calls=%async_computation | async-start | bytes 16777216 | tf_op jit(solution)/shard_map/all_to_all | solution.py:8
  286.2 187.1 %all-to-all-start.1 = ((bf16[16,512,512]{2,0,1:T(8,128)(2,1)}), bf16[16,512,512]{2,0,1:T(8,128)(2,1)}, u32[]{:S(2)}, u32[]{:S(2)}) async-start(bf16[16,512,512]{2,0,1:T(8,128)(2,1)} %copy.92), calls=%async_computation.1 | async-start | bytes 16777216 | tf_op jit(solution)/shard_map/all_to_all | solution.py:8
  496.2 187.1 %all-to-all-start.2 = ((bf16[256,32,512]{2,1,0:T(8,128)(2,1)}), bf16[256,32,512]{2,1,0:T(8,128)(2,1)}, u32[]{:S(2)}, u32[]{:S(2)}) async-start(bf16[256,32,512]{2,1,0:T(8,128)(2,1)} %copy.97), calls=%async_computation.2 | async-start | bytes 16777216 | tf_op jit(solution)/shard_map/all_to_all | solution.py:12
  501.3 349.5 %reduce-scatter.7.cloned.1.call-start = ((), (), s32[]{:S(2)}) async-start(), calls=%async_computation.8 | async-start | bytes 6291456
  568.3 311.4 %reduce-scatter.5.cloned.1.call-start = ((), (), s32[]{:S(2)}) async-start(), calls=%async_computation.7 | async-start | bytes 12582912 | tf_op jit(solution)/shard_map/reduce_scatter | solution.py:103
  701.4 97.5 %all-to-all-start.3 = ((bf16[128,32,512]{2,1,0:T(8,128)(2,1)}), bf16[128,32,512]{2,1,0:T(8,128)(2,1)}, u32[]{:S(2)}, u32[]{:S(2)}) async-start(bf16[128,32,512]{2,1,0:T(8,128)(2,1)} %bitcast.126), calls=%async_computation.3 | async-start | bytes 8388608 | tf_op jit(solution)/shard_map/all_to_all | solution.py:12
  803.7 97.2 %all-to-all-start.4 = ((bf16[128,32,512]{2,1,0:T(8,128)(2,1)}), bf16[128,32,512]{2,1,0:T(8,128)(2,1)}, u32[]{:S(2)}, u32[]{:S(2)}) async-start(bf16[128,32,512]{2,1,0:T(8,128)(2,1)} %bitcast.125), calls=%async_computation.4 | async-start | bytes 8388608 | tf_op jit(solution)/shard_map/all_to_all | solution.py:12
  833.0 3.2 copy-start
  837.8 49.9 %collective-permute-start = (bf16[8,512,256]{2,1,0:T(8,128)(2,1)}, bf16[8,512,256]{2,1,0:T(8,128)(2,1)}, u32[]{:S(2)}, u32[]{:S(2)}) collective-permute-start(bf16[8,512,256]{2,1,0:T(8,128)(2,1)} %dynamic-slice_convert_fusion.1), channel_id=1, source_target_pairs={{0,16},{16,0},{1,17},{17,1},{2,18},{18,2},{3,19},{19,3},{4,20},{20... | collective-permute-start | bytes 6291464 | tf_op jit(solution)/shard_map/ppermute | solution.py:27
  900.9 11.6 %slice-start = ((s8[8388608]{0:T(1024)(128)(4,1)}), s8[4194304]{0:T(1024)(128)(4,1)S(1)}, s32[]{:S(2)}) async-start(s8[8388608]{0:T(1024)(128)(4,1)} %bitcast.121), calls=%async_computation.9 | async-start | bytes 8388608
  903.8 2.0 copy-start.2
  905.8 6.7 slice-start.1
  918.7 3.2 copy-start.1
  923.6 59.4 %collective-permute-start.1 = (bf16[8,512,256]{2,1,0:T(8,128)(2,1)}, bf16[8,512,256]{2,1,0:T(8,128)(2,1)}, u32[]{:S(2)}, u32[]{:S(2)}) collective-permute-start(bf16[8,512,256]{2,1,0:T(8,128)(2,1)} %dynamic-slice_convert_fusion), channel_id=1, source_target_pairs={{0,16},{16,0},{1,17},{17,1},{2,18},{18,2},{3,19},{19,3},{4,20},{20... | collective-permute-start | bytes 6291464 | tf_op jit(solution)/shard_map/ppermute | solution.py:27
Sparse Core Ops, SparseCore 0:
  568.5 55.2 reduce-scatter.6
  626.1 99.2 reduce-scatter.4

commit v3 on v2

--- a/solution.py
+++ b/solution.py
@@ -4,12 +4,31 @@
 from jax.sharding import PartitionSpec as P
 
 
-def to_cols(x):
-    return lax.all_to_all(x, "seq", split_axis=1, concat_axis=0, tiled=True)
+def cols_send(x):
+    n = lax.axis_size("seq")
+    a, c, d = x.shape
+    return x.reshape(a, n, c // n, d).transpose(1, 0, 2, 3)
 
 
-def to_rows(x):
-    return lax.all_to_all(x, "seq", split_axis=0, concat_axis=1, tiled=True)
+def cols_recv(x):
+    return lax.all_to_all(x, "seq", split_axis=0, concat_axis=0, tiled=True).reshape(
+        (-1,) + x.shape[2:]
+    )
+
+
+def to_cols(x):
+    return cols_recv(cols_send(x))
+
+
+def rows_send(x):
+    n = lax.axis_size("seq")
+    return x.reshape((n, x.shape[0] // n) + x.shape[1:])
+
+
+def rows_recv(x):
+    n, f, c, d = x.shape
+    moved = lax.all_to_all(x, "seq", split_axis=0, concat_axis=0, tiled=True)
+    return moved.transpose(1, 0, 2, 3).reshape(f, n * c, d)
 
 
 def held(x):
@@ -44,13 +63,13 @@
     grad_third = jnp.einsum(
         "fch,fhd->fcd", block_one, grad_fourth, preferred_element_type=f32
     ).astype(jnp.bfloat16)
-    grad_third_cols = to_cols(held(grad_third))
+    grad_third_cols = cols_recv(held(cols_send(grad_third)))
 
     first = jnp.einsum(
         "acb,abd->acd", block_one, tokens, preferred_element_type=f32
     ).astype(jnp.bfloat16)
-    first, grad_third_cols = held((first, grad_third_cols))
-    first_cols = to_cols(first)
+    first_send, grad_third_cols = held((cols_send(first), grad_third_cols))
+    first_cols = cols_recv(first_send)
 
     grad_filtered = held(
         jnp.einsum("cef,fcd->ecd", block_two, grad_third_cols, preferred_element_type=f32)
@@ -59,8 +78,8 @@
     grad_first = jnp.einsum(
         "cea,ecd->acd", block_two, grad_second, preferred_element_type=f32
     ).astype(jnp.bfloat16)
-    grad_first, first_cols = held((grad_first, first_cols))
-    grad_first_rows = to_rows(grad_first)
+    grad_first_send, first_cols = held((rows_send(grad_first), first_cols))
+    grad_first_rows = rows_recv(grad_first_send)
 
     second = held(
         jnp.einsum("cea,acd->ecd", block_two, first_cols, preferred_element_type=f32)
@@ -73,8 +92,9 @@
     own = third.shape[0] // n_seq
     half = own // 2
     halves = ((0, half), (half, own)) if half else ((0, own),)
-    third_split = third.reshape((n_seq, own) + third.shape[1:])
-    third_split, grad_first_rows = held((third_split, grad_first_rows))
+    third_split = rows_send(third)
+    pieces = [third_split[:, lo:hi] for lo, hi in halves]
+    pieces, grad_first_rows = held((pieces, grad_first_rows))
 
     def finish(lo, hi, third_rows):
         fourth = jnp.einsum(
@@ -112,15 +132,14 @@
 
     outputs, grad_gates, grad_block_ones = [], [], []
     pending = None
-    for lo, hi in halves:
-        piece = third_split[:, lo:hi].reshape((-1,) + third.shape[1:])
+    for (lo, hi), piece in zip(halves, pieces):
         if pending is not None:
             piece, arrived = held((piece, pending[2]))
             outputs_k = finish(pending[0], pending[1], arrived)
             outputs.append(outputs_k[0])
             grad_gates.append(outputs_k[1])
             grad_block_ones.append(outputs_k[2])
-        pending = (lo, hi, to_rows(piece))
+        pending = (lo, hi, rows_recv(piece))
     outputs_k = finish(*pending)
     outputs.append(outputs_k[0])
     grad_gates.append(outputs_k[1])

time: 1000 us -> 936 us (0.936)
  waiting for transfers between devices: 482 us -> 353 us
  blocking collectives: 0 us -> 97.1 us
  local copies, waits for them, and re-layouts: 211 us -> 152 us
  matrix products: 196 us -> 224 us
    all_to_all x5 -> x4, waiting for transfers between devices: 481 us -> 353 us  [the longest x2 293 us: cols_recv(): lax.all_to_all(x, 'seq', split_axis=0, concat_axis=0, tiled=True)]
    all_to_all x0 -> x1, blocking collectives: none -> 97.1 us  [rows_recv(): moved = lax.all_to_all(x, 'seq', split_axis=0, concat_axis=0, tiled=True)]
    all_to_all x5 -> x1, local copies, waits for them, and re-layouts: 36.5 us -> 2.84 us  [rows_recv(): moved = lax.all_to_all(x, 'seq', split_axis=0, concat_axis=0, tiled=True)]
    optimization_barrier x3, local copies, waits for them, and re-layouts: 41.3 us -> 15 us  [held(): return lax.optimization_barrier(x)]
    reshape x0 -> x2, local copies, waits for them, and re-layouts: none -> 16.7 us  [cols_send(): return x.reshape(a, n, c // n, d).transpose(1, 0, 2, 3)]
    slice x3 -> x1, local copies, waits for them, and re-layouts: 16.3 us -> 4.14 us  [body(): pieces = [third_split[:, lo:hi] for lo, hi in halves]]
    all_to_all x5 -> x4, starting transfers between devices: 27 us -> 22.7 us  [the longest x2 11.7 us: cols_recv(): lax.all_to_all(x, 'seq', split_axis=0, concat_axis=0, tiled=True)]
  transfers between devices with their start and end apart: 9 -> 8, of which waited for: 5 -> 3; matrix products, arithmetic and copies ran while one was open for 33% -> 36% of each run, Pallas kernels for 0% -> 0%
where the time goes in v3:
time: 936 us; the launch traced here: 925 us
  waiting for transfers between devices  353 us (38%)
  matrix products  224 us (24%)
  local copies, waits for them, and re-layouts  152 us (16%)
  blocking collectives  97.1 us (10%)
  other arithmetic  59.7 us (6%)
  starting transfers between devices  24.8 us (3%)
  between operations  14.4 us (2%)
    all_to_all x2, waiting for transfers between devices, cols_recv(): lax.all_to_all(x, 'seq', split_axis=0, concat_axis=0, tiled=True)  293 us
    unnamed x21, local copies, waits for them, and re-layouts  108 us
    all_to_all x1, blocking collectives, rows_recv(): moved = lax.all_to_all(x, 'seq', split_axis=0, concat_axis=0, tiled=True)  97.1 us
    all_to_all x2, waiting for transfers between devices, rows_recv(): moved = lax.all_to_all(x, 'seq', split_axis=0, concat_axis=0, tiled=True)  60.1 us
    dot_general x2, matrix products, finish(): jnp.einsum('fch,fcd->fhd', block_one[lo:hi], third_rows, preferred_elemen...  26.8 us
    dot_general x1, matrix products, body(): jnp.einsum('fcd,ecd->cef', grad_third_cols, filtered, preferred_element_t...  22 us
    dot_general x1, matrix products, body(): jnp.einsum('ecd,acd->cea', grad_second, first_cols, preferred_element_typ...  21.4 us
    dot_general x1, matrix products, body(): jnp.einsum('acd,abd->acb', grad_first_rows, tokens, preferred_element_typ...  20.7 us
  transfers between devices with their start and end apart: 8, of which 3 were waited for; matrix products, arithmetic and copies ran while one was open for 36% of the time, Pallas kernels for 0%

profile of v3, /device:TPU:10, one launch (start us, length us, event | category | flops | bytes accessed | tf_op | source)
XLA Modules:
  0.0 925.1 jit_solution(10969912772151458215)
XLA Ops:
  7.2 12.3 %copy.67 = bf16[1,16,512,512]{2,3,1,0:T(8,128)(2,1)} copy(bf16[1,16,512,512]{3,2,1,0:T(8,128)(2,1)} %param.9) | data formatting | bytes 16777216 | tf_op args[3]
  19.4 12.3 %copy.64 = bf16[1,16,512,512]{2,3,1,0:T(8,128)(2,1)} copy(bf16[1,16,512,512]{3,2,1,0:T(8,128)(2,1)} %param.7) | data formatting | bytes 16777216 | tf_op args[1]
  31.7 13.4 %add_divide_fusion = (f32[1,16,512,512]{2,3,1,0:T(8,128)}, bf16[16,512,512]{1,2,0:T(8,128)(2,1)S(1)}) fusion(bf16[1,16,512,512]{2,3,1,0:T(8,128)(2,1)} %copy.64, bf16[1,16,512,512]{2,3,1,0:T(8,128)(2,1)} %copy.67), kind=kLoop, calls=%fused_computation.6 | loop fusion | flops 29360128 | bytes 41943040 | tf_op jit(solution)/shard_map/div | solution.py:60
  45.1 13.3 %convolution_convert_fusion.2 = bf16[16,512,512]{1,2,0:T(8,128)(2,1)} fusion(bf16[16,512,512]{1,2,0:T(8,128)(2,1)S(1)} %get-tuple-element.47, bf16[16,512,512]{2,1,0:T(8,128)(2,1)} %param.10), kind=kOutput, calls=%fused_computation.52 | convolution fusion | flops 4299161600 | bytes 25165824 | tf_op jit(solution)/shard_map/fch,fhd->fcd/dot_general | solution.py:63
  58.4 8.3 copy.139
  72.9 13.7 %fusion.30 = bf16[16,512,512]{2,1,0:T(8,128)(2,1)} fusion(bf16[16,512,512]{2,1,0:T(8,128)(2,1)} %param.10, bf16[1,16,512,512]{3,2,1,0:T(8,128)(2,1)} %param.6), kind=kOutput, calls=%fused_computation.49 | convolution fusion | flops 4299161600 | bytes 25165824 | tf_op jit(solution)/shard_map/acb,abd->acd/dot_general | solution.py:68
  86.6 8.4 copy.140
  95.0 159.9 %all-to-all-done = bf16[16,16,32,512]{3,2,1,0:T(8,128)(2,1)} async-done(((bf16[16,16,32,512]{3,2,1,0:T(8,128)(2,1)}), bf16[16,16,32,512]{3,2,1,0:T(8,128)(2,1)}, u32[]{:S(2)}, u32[]{:S(2)}) %all-to-all-start) | async-done | bytes 8388640 | tf_op jit(solution)/shard_map/all_to_all | solution.py:14
  260.4 13.7 %copy.65 = bf16[256,32,512]{0,2,1:T(8,128)(2,1)} copy(bf16[256,32,512]{2,1,0:T(8,128)(2,1)} %param.8) | data formatting | bytes 16777216 | tf_op args[2]
  274.1 20.4 %convolution_bitcast_fusion.1 = f32[256,32,512]{0,2,1:T(8,128)} fusion(bf16[32,256,256]{2,1,0:T(8,128)(2,1)} %param.11, bf16[256,32,512]{2,1,0:T(8,128)(2,1)} %bitcast.8), kind=kOutput, calls=%fused_computation.8 | convolution fusion | flops 2147483648 | bytes 29360128 | tf_op jit(solution)/shard_map/cef,fcd->ecd/dot_general | solution.py:75
  294.5 15.1 %convolution_convert_fusion.1 = bf16[32,512,256]{1,2,0:T(8,128)(2,1)} fusion(bf16[32,256,256]{2,1,0:T(8,128)(2,1)} %param.11, f32[256,32,512]{0,2,1:T(8,128)} %convolution_bitcast_fusion.1, bf16[256,32,512]{0,2,1:T(8,128)(2,1)} %copy.65), kind=kOutput, calls=%fused_computation.51 | convolution fusion | flops 2164260864 | bytes 37748736 | tf_op jit(solution)/shard_map/cea,ecd->acd/dot_general | solution.py:78
  309.6 132.7 %all-to-all-done.1 = bf16[16,16,32,512]{3,2,1,0:T(8,128)(2,1)} async-done(((bf16[16,16,32,512]{3,2,1,0:T(8,128)(2,1)}), bf16[16,16,32,512]{3,2,1,0:T(8,128)(2,1)}, u32[]{:S(2)}, u32[]{:S(2)}) %all-to-all-start.1) | async-done | bytes 8388640 | tf_op jit(solution)/shard_map/all_to_all | solution.py:14
  442.3 8.1 copy.78
  455.5 20.4 %convolution_bitcast_fusion = f32[256,32,512]{0,2,1:T(8,128)} fusion(bf16[32,256,256]{2,1,0:T(8,128)(2,1)} %param.11, bf16[256,32,512]{2,1,0:T(8,128)(2,1)} %bitcast.12), kind=kOutput, calls=%fused_computation.7 | convolution fusion | flops 2147483648 | bytes 29360128 | tf_op jit(solution)/shard_map/cea,acd->ecd/dot_general | solution.py:85
  475.9 21.4 %fusion.20 = f32[32,256,256]{2,1,0:T(8,128)} fusion(bf16[256,32,512]{2,1,0:T(8,128)(2,1)} %bitcast.12, f32[256,32,512]{0,2,1:T(8,128)} %convolution_bitcast_fusion.1, bf16[256,32,512]{0,2,1:T(8,128)(2,1)} %copy.65), kind=kOutput, calls=%fused_computation.41 | convolution fusion | flops 2160066560 | bytes 41943040 | tf_op jit(solution)/shard_map/ecd,acd->cea/dot_general | solution.py:119
  497.2 22.0 %multiply_convert_fusion.2 = bf16[32,256,256]{2,1,0:T(8,128)(2,1)} fusion(f32[32,256,256]{2,1,0:T(8,128)} %fusion.20, bf16[256,32,512]{2,1,0:T(8,128)(2,1)} %bitcast.8, f32[256,32,512]{0,2,1:T(8,128)} %convolution_bitcast_fusion, bf16[256,32,512]{0,2,1:T(8,128)(2,1)} %copy.65), kind=kOutput, calls=%fused_computation.38 | convolution fusion | flops 2166358016 | bytes 46137344 | tf_op jit(solution)/shard_map/fcd,ecd->cef/dot_general | solution.py:118
  519.2 8.0 copy.105
  527.3 8.4 copy.109
  535.8 15.3 %multiply_convert_fusion.1 = bf16[256,32,512]{0,2,1:T(8,128)(2,1)} fusion(f32[256,32,512]{0,2,1:T(8,128)} %convolution_bitcast_fusion.1, f32[256,32,512]{0,2,1:T(8,128)} %convolution_bitcast_fusion), kind=kLoop, calls=%fused_computation.5 | loop fusion | flops 8388608 | bytes 41943040 | tf_op jit(solution)/shard_map/convert_element_type | solution.py:115
  551.1 15.3 %convolution_convert_fusion = bf16[32,512,256]{1,2,0:T(8,128)(2,1)} fusion(bf16[32,256,256]{2,1,0:T(8,128)(2,1)} %param.11, f32[256,32,512]{0,2,1:T(8,128)} %convolution_bitcast_fusion, bf16[256,32,512]{0,2,1:T(8,128)(2,1)} %copy.65), kind=kOutput, calls=%fused_computation.50 | convolution fusion | flops 2164260864 | bytes 37748736 | tf_op jit(solution)/shard_map/cef,ecd->fcd/dot_general | solution.py:88
  577.5 60.1 %all-to-all-done.2 = bf16[16,16,32,512]{3,1,2,0:T(8,128)(2,1)} async-done(((bf16[16,16,32,512]{3,1,2,0:T(8,128)(2,1)}), bf16[16,16,32,512]{3,1,2,0:T(8,128)(2,1)}, u32[]{:S(2)}, u32[]{:S(2)}) %all-to-all-start.2) | async-done | bytes 8388640 | tf_op jit(solution)/shard_map/all_to_all | solution.py:30
  637.5 97.1 %all_to_all.25 = bf16[16,8,32,512]{3,1,2,0:T(8,128)(2,1)} all-to-all(bf16[16,8,32,512]{3,1,2,0:T(8,128)(2,1)} %copy.107), channel_id=1, replica_groups=mesh['dp'=2,'seq'=16] {'seq'}, dimensions={0} | all-to-all | bytes 8388608 | tf_op jit(solution)/shard_map/all_to_all | solution.py:30
  740.7 20.7 %fusion.15 = f32[16,512,512]{2,1,0:T(8,128)} fusion(bf16[1,16,512,512]{3,2,1,0:T(8,128)(2,1)} %param.6, bf16[16,512,512]{2,0,1:T(8,128)(2,1)} %bitcast.18), kind=kOutput, calls=%fused_computation.32 | convolution fusion | flops 4294967296 | bytes 33554432 | tf_op jit(solution)/shard_map/acd,abd->acb/dot_general | solution.py:129
  761.4 9.2 fusion.4
  777.1 11.4 %convert_element_type.108 = f32[1,16,512,512]{2,3,1,0:T(8,128)} convert(bf16[1,16,512,512]{2,3,1,0:T(8,128)(2,1)} %copy.67) | non-fusion elementwise | flops 4194304 | bytes 25165824 | tf_op jit(solution)/shard_map/convert_element_type | solution.py:61
  793.9 16.9 %convert_bitcast_fusion = bf16[1,16,512,512]{2,3,1,0:T(8,128)(2,1)} fusion(bf16[16,512,512]{2,1,0:T(8,128)(2,1)} %param.10, bf16[16,512,512]{2,0,1:T(8,128)(2,1)} %bitcast.18), kind=kOutput, calls=%fused_computation.39 | convolution fusion | flops 4299161600 | bytes 25165824 | tf_op jit(solution)/shard_map/acb,acd->abd/dot_general | solution.py:126
  810.8 12.3 %copy.92 = bf16[1,16,512,512]{3,2,1,0:T(8,128)(2,1)} copy(bf16[1,16,512,512]{2,3,1,0:T(8,128)(2,1)} %convert_bitcast_fusion) | data formatting | bytes 16777216
  843.9 9.1 fusion.3
  857.3 20.0 %fusion.12 = (bf16[8,512,512]{1,2,0:T(8,128)(2,1)S(1)}, bf16[8,512,512]{1,2,0:T(8,128)(2,1)}, bf16[8,512,512]{1,2,0:T(8,128)(2,1)}, bf16[8,512,512]{1,2,0:T(8,128)(2,1)}) fusion(f32[1,16,512,512]{2,3,1,0:T(8,128)} %convert_element_type.108, f32[1,16,512,512]{2,3,1,0:T(8,128)} %get-tuple-element.46, bf16[8,512,512]{2,1,0:T(8,128)(2,1)} %fusion.48, ...), kind=kOutput, calls=%fused_computation.23 | convolution fusion | flops 2183135232 | bytes 62914560 | tf_op jit(solution)/shard_map/fch,fcd->fhd/dot_general | solution.py:100
  877.3 10.5 %maximum_bitcast_fusion = (bf16[1,16,512,512]{2,3,1,0:T(8,128)(2,1)}, bf16[1,16,512,512]{2,3,1,0:T(8,128)(2,1)}) fusion(bf16[8,512,512]{1,2,0:T(8,128)(2,1)} %get-tuple-element.44, bf16[8,512,512]{1,2,0:T(8,128)(2,1)} %get-tuple-element.45, bf16[8,512,512]{1,2,0:T(8,128)(2,1)} %get-tuple-element.43, bf16[8,512,512]{1,2,0:T(8,128)(2,1)S(1)} %get-tuple-element.42), kind=kLoop, calls=%fused_computation.26 | loop fusion | flops 8388608 | bytes 33554432 | tf_op jit(solution)/shard_map/broadcast_in_dim | solution.py:151
  887.8 12.3 %copy.91 = bf16[1,16,512,512]{3,2,1,0:T(8,128)(2,1)} copy(bf16[1,16,512,512]{2,3,1,0:T(8,128)(2,1)} %get-tuple-element.50) | data formatting | bytes 16777216
  900.1 12.3 %copy.93 = bf16[1,16,512,512]{3,2,1,0:T(8,128)(2,1)} copy(bf16[1,16,512,512]{2,3,1,0:T(8,128)(2,1)} %get-tuple-element.51) | data formatting | bytes 16777216
  (39 shorter events, 76.5 us)
Async XLA Ops:
  45.1 13.3 %copy-start.1 = (bf16[16,512,512]{1,2,0:T(8,128)(2,1)}, bf16[16,512,512]{1,2,0:T(8,128)(2,1)S(1)}, u32[]{:S(2)}) copy-start(bf16[16,512,512]{1,2,0:T(8,128)(2,1)S(1)} %get-tuple-element.47) | copy-start | bytes 25165828
  66.6 188.3 %all-to-all-start = ((bf16[16,16,32,512]{3,2,1,0:T(8,128)(2,1)}), bf16[16,16,32,512]{3,2,1,0:T(8,128)(2,1)}, u32[]{:S(2)}, u32[]{:S(2)}) async-start(bf16[16,16,32,512]{3,2,1,0:T(8,128)(2,1)} %bitcast.110), calls=%async_computation | async-start | bytes 16777216 | tf_op jit(solution)/shard_map/all_to_all | solution.py:14
  255.0 187.3 %all-to-all-start.1 = ((bf16[16,16,32,512]{3,2,1,0:T(8,128)(2,1)}), bf16[16,16,32,512]{3,2,1,0:T(8,128)(2,1)}, u32[]{:S(2)}, u32[]{:S(2)}) async-start(bf16[16,16,32,512]{3,2,1,0:T(8,128)(2,1)} %bitcast.109), calls=%async_computation.1 | async-start | bytes 16777216 | tf_op jit(solution)/shard_map/all_to_all | solution.py:14
  450.4 187.1 %all-to-all-start.2 = ((bf16[16,16,32,512]{3,1,2,0:T(8,128)(2,1)}), bf16[16,16,32,512]{3,1,2,0:T(8,128)(2,1)}, u32[]{:S(2)}, u32[]{:S(2)}) async-start(bf16[16,16,32,512]{3,1,2,0:T(8,128)(2,1)} %copy.78), calls=%async_computation.2 | async-start | bytes 16777216 | tf_op jit(solution)/shard_map/all_to_all | solution.py:30
  455.4 333.0 %reduce-scatter.7.cloned.1.call-start = ((), (), s32[]{:S(2)}) async-start(), calls=%async_computation.8 | async-start | bytes 6291456
  535.7 287.4 %reduce-scatter.5.cloned.1.call-start = ((), (), s32[]{:S(2)}) async-start(), calls=%async_computation.7 | async-start | bytes 12582912 | tf_op jit(solution)/shard_map/reduce_scatter | solution.py:123
  734.6 99.6 %all-to-all-start.4 = ((bf16[16,8,32,512]{3,2,1,0:T(8,128)(2,1)}), bf16[16,8,32,512]{3,2,1,0:T(8,128)(2,1)}, u32[]{:S(2)}, u32[]{:S(2)}) async-start(bf16[16,8,32,512]{3,2,1,0:T(8,128)(2,1)} %copy.108), calls=%async_computation.4 | async-start | bytes 8388608 | tf_op jit(solution)/shard_map/all_to_all | solution.py:30
  770.5 3.4 copy-start
  775.5 55.4 %collective-permute-start = (bf16[8,512,256]{2,1,0:T(8,128)(2,1)}, bf16[8,512,256]{2,1,0:T(8,128)(2,1)}, u32[]{:S(2)}, u32[]{:S(2)}) collective-permute-start(bf16[8,512,256]{2,1,0:T(8,128)(2,1)} %dynamic-slice_convert_fusion.1), channel_id=1, source_target_pairs={{0,16},{16,0},{1,17},{17,1},{2,18},{18,2},{3,19},{19,3},{4,20},{20... | collective-permute-start | bytes 6291464 | tf_op jit(solution)/shard_map/ppermute | solution.py:46
  834.3 9.6 %slice-start = ((s8[8388608]{0:T(1024)(128)(4,1)}), s8[4194304]{0:T(1024)(128)(4,1)S(1)}, s32[]{:S(2)}) async-start(s8[8388608]{0:T(1024)(128)(4,1)} %bitcast.107), calls=%async_computation.9 | async-start | bytes 8388608
  837.1 6.8 slice-start.1
  843.9 13.4 %copy-start.2 = (bf16[16,8,32,512]{3,1,2,0:T(8,128)(2,1)S(1)}, bf16[16,8,32,512]{3,1,2,0:T(8,128)(2,1)}, u32[]{:S(2)}) copy-start(bf16[16,8,32,512]{3,1,2,0:T(8,128)(2,1)} %all_to_all.25) | copy-start | bytes 12582916
  856.8 55.5 %collective-permute-start.1 = (bf16[8,512,256]{2,1,0:T(8,128)(2,1)}, bf16[8,512,256]{2,1,0:T(8,128)(2,1)}, u32[]{:S(2)}, u32[]{:S(2)}) collective-permute-start(bf16[8,512,256]{2,1,0:T(8,128)(2,1)} %dynamic-slice_convert_fusion), channel_id=1, source_target_pairs={{0,16},{16,0},{1,17},{17,1},{2,18},{18,2},{3,19},{19,3},{4,20},{20... | collective-permute-start | bytes 6291464 | tf_op jit(solution)/shard_map/ppermute | solution.py:46
Sparse Core Ops, SparseCore 0:
  535.8 55.2 reduce-scatter.6
  593.5 99.2 reduce-scatter.4

commit v4 on v3

--- a/solution.py
+++ b/solution.py
@@ -2,6 +2,11 @@
 import jax.numpy as jnp
 from jax import lax
 from jax.sharding import PartitionSpec as P
+from jax.experimental.layout import Layout, with_layout_constraint
+
+
+def natural(x):
+    return with_layout_constraint(x, Layout(tuple(range(x.ndim))))
 
 
 def cols_send(x):
@@ -100,7 +105,7 @@
         fourth = jnp.einsum(
             "fch,fcd->fhd", block_one[lo:hi], third_rows, preferred_element_type=f32
         ).astype(jnp.bfloat16)
-        fourth_wide = fourth.astype(f32)
+        fourth_wide = natural(fourth).astype(f32)
         opened_k = opened[lo:hi]
         output = (opened_k * fourth_wide).astype(jnp.bfloat16)
         grad_gate = (

time: 936 us -> 904 us (0.966)
  local copies, waits for them, and re-layouts: 152 us -> 102 us
  waiting for transfers between devices: 353 us -> 368 us
    unnamed x21 -> x17, local copies, waits for them, and re-layouts: 108 us -> 61.1 us
    convert_element_type x0 -> x1, other arithmetic: none -> 15.8 us  [body(): grad_fourth = held((incoming * opened).astype(jnp.bfloat16))]
    div x1 -> x0, other arithmetic: 13.4 us -> none  [body(): opened = jax.nn.sigmoid(gate_logits[0].astype(f32))]
    ppermute x2, waiting for transfers between devices: 0.01 us -> 13.4 us  [dp_reduce_scatter(): lax.ppermute(part.astype(jnp.bfloat16), 'dp', [(i, (i + shift) % n) for i...]
  transfers between devices with their start and end apart: 8 -> 8, of which waited for: 3 -> 4; matrix products, arithmetic and copies ran while one was open for 36% -> 35% of each run, Pallas kernels for 0% -> 0%
where the time goes in v4:
time: 904 us; the launch traced here: 894 us
  waiting for transfers between devices  368 us (41%)
  matrix products  225 us (25%)
  local copies, waits for them, and re-layouts  102 us (11%)
  blocking collectives  97.1 us (11%)
  other arithmetic  62.5 us (7%)
  starting transfers between devices  24.9 us (3%)
  between operations  14.6 us (2%)
    all_to_all x2, waiting for transfers between devices, cols_recv(): lax.all_to_all(x, 'seq', split_axis=0, concat_axis=0, tiled=True)  293 us
    all_to_all x1, blocking collectives, rows_recv(): moved = lax.all_to_all(x, 'seq', split_axis=0, concat_axis=0, tiled=True)  97.1 us
    all_to_all x2, waiting for transfers between devices, rows_recv(): moved = lax.all_to_all(x, 'seq', split_axis=0, concat_axis=0, tiled=True)  61.8 us
    unnamed x17, local copies, waits for them, and re-layouts  61.1 us
    dot_general x2, matrix products, finish(): jnp.einsum('fch,fcd->fhd', block_one[lo:hi], third_rows, preferred_elemen...  30 us
    dot_general x1, matrix products, body(): jnp.einsum('fcd,ecd->cef', grad_third_cols, filtered, preferred_element_t...  22 us
    dot_general x1, matrix products, body(): jnp.einsum('ecd,acd->cea', grad_second, first_cols, preferred_element_typ...  21.4 us
    dot_general x1, matrix products, body(): jnp.einsum('acd,abd->acb', grad_first_rows, tokens, preferred_element_typ...  20.7 us
  transfers between devices with their start and end apart: 8, of which 4 were waited for; matrix products, arithmetic and copies ran while one was open for 35% of the time, Pallas kernels for 0%

profile of v4, /device:TPU:10, one launch (start us, length us, event | category | flops | bytes accessed | tf_op | source)
XLA Modules:
  0.0 894.0 jit_solution(9050105584161929036)
XLA Ops:
  7.2 15.8 %fusion.10 = (bf16[16,512,512]{2,1,0:T(8,128)(2,1)}, f32[1,16,512,512]{3,2,1,0:T(8,128)}) fusion(bf16[1,16,512,512]{3,2,1,0:T(8,128)(2,1)} %param.9, bf16[1,16,512,512]{3,2,1,0:T(8,128)(2,1)} %param.7), kind=kLoop, calls=%fused_computation.21 | loop fusion | flops 29360128 | bytes 41943040 | tf_op jit(solution)/shard_map/convert_element_type | solution.py:67
  23.0 13.7 %convolution_convert_fusion.2 = bf16[16,512,512]{1,2,0:T(8,128)(2,1)} fusion(bf16[16,512,512]{2,1,0:T(8,128)(2,1)} %param.10, bf16[16,512,512]{2,1,0:T(8,128)(2,1)} %get-tuple-element.42), kind=kOutput, calls=%fused_computation.52 | convolution fusion | flops 4299161600 | bytes 25165824 | tf_op jit(solution)/shard_map/fch,fhd->fcd/dot_general | solution.py:68
  36.7 8.3 copy.98
  45.0 6.2 all-to-all-start
  51.2 13.7 %fusion.28 = bf16[16,512,512]{2,1,0:T(8,128)(2,1)} fusion(bf16[16,512,512]{2,1,0:T(8,128)(2,1)} %param.10, bf16[1,16,512,512]{3,2,1,0:T(8,128)(2,1)} %param.6), kind=kOutput, calls=%fused_computation.49 | convolution fusion | flops 4299161600 | bytes 25165824 | tf_op jit(solution)/shard_map/acb,abd->acd/dot_general | solution.py:73
  64.9 8.4 copy.99
  73.3 159.9 %all-to-all-done = bf16[16,16,32,512]{3,2,1,0:T(8,128)(2,1)} async-done(((bf16[16,16,32,512]{3,2,1,0:T(8,128)(2,1)}), bf16[16,16,32,512]{3,2,1,0:T(8,128)(2,1)}, u32[]{:S(2)}, u32[]{:S(2)}) %all-to-all-start) | async-done | bytes 8388640 | tf_op jit(solution)/shard_map/all_to_all | solution.py:19
  239.0 13.7 %copy.31 = bf16[256,32,512]{0,2,1:T(8,128)(2,1)} copy(bf16[256,32,512]{2,1,0:T(8,128)(2,1)} %param.8) | data formatting | bytes 16777216 | tf_op args[2]
  252.7 20.4 %convolution_bitcast_fusion.1 = f32[256,32,512]{0,2,1:T(8,128)} fusion(bf16[32,256,256]{2,1,0:T(8,128)(2,1)} %param.11, bf16[256,32,512]{2,1,0:T(8,128)(2,1)} %bitcast.8), kind=kOutput, calls=%fused_computation.12 | convolution fusion | flops 2147483648 | bytes 29360128 | tf_op jit(solution)/shard_map/cef,fcd->ecd/dot_general | solution.py:80
  273.0 15.0 %convolution_convert_fusion.1 = bf16[32,512,256]{1,2,0:T(8,128)(2,1)} fusion(bf16[32,256,256]{2,1,0:T(8,128)(2,1)} %param.11, f32[256,32,512]{0,2,1:T(8,128)} %convolution_bitcast_fusion.1, bf16[256,32,512]{0,2,1:T(8,128)(2,1)} %copy.31), kind=kOutput, calls=%fused_computation.51 | convolution fusion | flops 2164260864 | bytes 37748736 | tf_op jit(solution)/shard_map/cea,ecd->acd/dot_general | solution.py:83
  288.0 132.9 %all-to-all-done.1 = bf16[16,16,32,512]{3,2,1,0:T(8,128)(2,1)} async-done(((bf16[16,16,32,512]{3,2,1,0:T(8,128)(2,1)}), bf16[16,16,32,512]{3,2,1,0:T(8,128)(2,1)}, u32[]{:S(2)}, u32[]{:S(2)}) %all-to-all-start.1) | async-done | bytes 8388640 | tf_op jit(solution)/shard_map/all_to_all | solution.py:19
  420.9 8.0 copy.42
  434.0 20.4 %convolution_bitcast_fusion = f32[256,32,512]{0,2,1:T(8,128)} fusion(bf16[32,256,256]{2,1,0:T(8,128)(2,1)} %param.11, bf16[256,32,512]{2,1,0:T(8,128)(2,1)} %bitcast.12), kind=kOutput, calls=%fused_computation.11 | convolution fusion | flops 2147483648 | bytes 29360128 | tf_op jit(solution)/shard_map/cea,acd->ecd/dot_general | solution.py:90
  454.3 21.4 %fusion.18 = f32[32,256,256]{2,1,0:T(8,128)} fusion(bf16[256,32,512]{2,1,0:T(8,128)(2,1)} %bitcast.12, f32[256,32,512]{0,2,1:T(8,128)} %convolution_bitcast_fusion.1, bf16[256,32,512]{0,2,1:T(8,128)(2,1)} %copy.31), kind=kOutput, calls=%fused_computation.41 | convolution fusion | flops 2160066560 | bytes 41943040 | tf_op jit(solution)/shard_map/ecd,acd->cea/dot_general | solution.py:124
  475.7 22.0 %multiply_convert_fusion.2 = bf16[32,256,256]{2,1,0:T(8,128)(2,1)} fusion(f32[32,256,256]{2,1,0:T(8,128)} %fusion.18, bf16[256,32,512]{2,1,0:T(8,128)(2,1)} %bitcast.8, f32[256,32,512]{0,2,1:T(8,128)} %convolution_bitcast_fusion, bf16[256,32,512]{0,2,1:T(8,128)(2,1)} %copy.31), kind=kOutput, calls=%fused_computation.38 | convolution fusion | flops 2166358016 | bytes 46137344 | tf_op jit(solution)/shard_map/fcd,ecd->cef/dot_general | solution.py:123
  497.8 8.2 copy.62
  506.0 8.4 copy.68
  514.5 15.3 %multiply_convert_fusion.1 = bf16[256,32,512]{0,2,1:T(8,128)(2,1)} fusion(f32[256,32,512]{0,2,1:T(8,128)} %convolution_bitcast_fusion.1, f32[256,32,512]{0,2,1:T(8,128)} %convolution_bitcast_fusion), kind=kLoop, calls=%fused_computation.5 | loop fusion | flops 8388608 | bytes 41943040 | tf_op jit(solution)/shard_map/convert_element_type | solution.py:120
  529.8 15.3 %convolution_convert_fusion = bf16[32,512,256]{1,2,0:T(8,128)(2,1)} fusion(bf16[32,256,256]{2,1,0:T(8,128)(2,1)} %param.11, f32[256,32,512]{0,2,1:T(8,128)} %convolution_bitcast_fusion, bf16[256,32,512]{0,2,1:T(8,128)(2,1)} %copy.31), kind=kOutput, calls=%fused_computation.50 | convolution fusion | flops 2164260864 | bytes 37748736 | tf_op jit(solution)/shard_map/cef,ecd->fcd/dot_general | solution.py:93
  554.2 61.8 %all-to-all-done.2 = bf16[16,16,32,512]{3,1,2,0:T(8,128)(2,1)} async-done(((bf16[16,16,32,512]{3,1,2,0:T(8,128)(2,1)}), bf16[16,16,32,512]{3,1,2,0:T(8,128)(2,1)}, u32[]{:S(2)}, u32[]{:S(2)}) %all-to-all-start.2) | async-done | bytes 8388640 | tf_op jit(solution)/shard_map/all_to_all | solution.py:35
  616.0 97.1 %all_to_all.25 = bf16[16,8,32,512]{3,1,2,0:T(8,128)(2,1)} all-to-all(bf16[16,8,32,512]{3,1,2,0:T(8,128)(2,1)} %copy.65), channel_id=1, replica_groups=mesh['dp'=2,'seq'=16] {'seq'}, dimensions={0} | all-to-all | bytes 8388608 | tf_op jit(solution)/shard_map/all_to_all | solution.py:35
  718.9 20.7 %fusion.13 = f32[16,512,512]{2,1,0:T(8,128)} fusion(bf16[1,16,512,512]{3,2,1,0:T(8,128)(2,1)} %param.6, bf16[16,512,512]{2,0,1:T(8,128)(2,1)} %bitcast.18), kind=kOutput, calls=%fused_computation.32 | convolution fusion | flops 4294967296 | bytes 33554432 | tf_op jit(solution)/shard_map/acd,abd->acb/dot_general | solution.py:134
  739.6 9.2 %fusion.12 = f32[8,512,512]{2,1,0:T(8,128)S(1)} fusion(f32[16,512,512]{2,1,0:T(8,128)} %fusion.13, bf16[16,512,512]{2,1,0:T(8,128)(2,1)} %get-tuple-element.42, bf16[8,512,512]{2,0,1:T(8,128)(2,1)} %bitcast.98), kind=kOutput, calls=%fused_computation.25 | convolution fusion | flops 2151677952 | bytes 25165824 | tf_op jit(solution)/shard_map/fhd,fcd->fch/dot_general | solution.py:114
  755.2 11.4 %convert_element_type.106 = f32[1,16,512,512]{3,2,1,0:T(8,128)} convert(bf16[1,16,512,512]{3,2,1,0:T(8,128)(2,1)} %param.9) | non-fusion elementwise | flops 4194304 | bytes 25165824 | tf_op jit(solution)/shard_map/convert_element_type | solution.py:66
  772.0 16.9 %convert_bitcast_fusion = bf16[1,16,512,512]{2,3,1,0:T(8,128)(2,1)} fusion(bf16[16,512,512]{2,1,0:T(8,128)(2,1)} %param.10, bf16[16,512,512]{2,0,1:T(8,128)(2,1)} %bitcast.18), kind=kOutput, calls=%fused_computation.39 | convolution fusion | flops 4299161600 | bytes 25165824 | tf_op jit(solution)/shard_map/acb,acd->abd/dot_general | solution.py:131
  789.0 12.3 %copy.54 = bf16[1,16,512,512]{3,2,1,0:T(8,128)(2,1)} copy(bf16[1,16,512,512]{2,3,1,0:T(8,128)(2,1)} %convert_bitcast_fusion) | data formatting | bytes 16777216
  801.2 7.8 copy.55
  819.5 6.8 fusion.46
  826.2 6.3 fusion.11
  834.7 23.3 %fusion.5 = (bf16[8,512,512]{2,1,0:T(8,128)(2,1)S(1)}, bf16[8,512,512]{2,1,0:T(8,128)(2,1)}, bf16[8,512,512]{2,1,0:T(8,128)(2,1)}, bf16[8,512,512]{2,1,0:T(8,128)(2,1)}) fusion(f32[1,16,512,512]{3,2,1,0:T(8,128)} %convert_element_type.106, f32[1,16,512,512]{3,2,1,0:T(8,128)} %get-tuple-element.43, bf16[8,512,512]{1,2,0:T(8,128)(2,1)} %fusion.46, ...), kind=kOutput, calls=%fused_computation.16 | convolution fusion | flops 2183135232 | bytes 62914560 | tf_op jit(solution)/shard_map/fch,fcd->fhd/dot_general | solution.py:105
  858.0 10.5 %maximum_bitcast_fusion = (bf16[1,16,512,512]{3,2,1,0:T(8,128)(2,1)}, bf16[1,16,512,512]{3,2,1,0:T(8,128)(2,1)}) fusion(bf16[8,512,512]{2,1,0:T(8,128)(2,1)} %get-tuple-element.38, bf16[8,512,512]{2,1,0:T(8,128)(2,1)} %get-tuple-element.39, bf16[8,512,512]{2,1,0:T(8,128)(2,1)} %get-tuple-element.37, bf16[8,512,512]{2,1,0:T(8,128)(2,1)S(1)} %get-tuple-element.36), kind=kLoop, calls=%fused_computation.30 | loop fusion | flops 8388608 | bytes 33554432 | tf_op jit(solution)/shard_map/broadcast_in_dim | solution.py:156
  868.6 13.4 %collective-permute-done.1 = bf16[8,512,256]{2,1,0:T(8,128)(2,1)} collective-permute-done((bf16[8,512,256]{2,1,0:T(8,128)(2,1)}, bf16[8,512,256]{2,1,0:T(8,128)(2,1)}, u32[]{:S(2)}, u32[]{:S(2)}) %collective-permute-start.1) | collective-permute-done | bytes 2097184 | tf_op jit(solution)/shard_map/ppermute | solution.py:51
  (35 shorter events, 54.9 us)
Async XLA Ops:
  45.0 188.3 %all-to-all-start = ((bf16[16,16,32,512]{3,2,1,0:T(8,128)(2,1)}), bf16[16,16,32,512]{3,2,1,0:T(8,128)(2,1)}, u32[]{:S(2)}, u32[]{:S(2)}) async-start(bf16[16,16,32,512]{3,2,1,0:T(8,128)(2,1)} %bitcast.93), calls=%async_computation | async-start | bytes 16777216 | tf_op jit(solution)/shard_map/all_to_all | solution.py:19
  233.3 187.6 %all-to-all-start.1 = ((bf16[16,16,32,512]{3,2,1,0:T(8,128)(2,1)}), bf16[16,16,32,512]{3,2,1,0:T(8,128)(2,1)}, u32[]{:S(2)}, u32[]{:S(2)}) async-start(bf16[16,16,32,512]{3,2,1,0:T(8,128)(2,1)} %bitcast.92), calls=%async_computation.1 | async-start | bytes 16777216 | tf_op jit(solution)/shard_map/all_to_all | solution.py:19
  428.9 187.1 %all-to-all-start.2 = ((bf16[16,16,32,512]{3,1,2,0:T(8,128)(2,1)}), bf16[16,16,32,512]{3,1,2,0:T(8,128)(2,1)}, u32[]{:S(2)}, u32[]{:S(2)}) async-start(bf16[16,16,32,512]{3,1,2,0:T(8,128)(2,1)} %copy.42), calls=%async_computation.2 | async-start | bytes 16777216 | tf_op jit(solution)/shard_map/all_to_all | solution.py:35
  433.9 332.7 %reduce-scatter.7.cloned.1.call-start = ((), (), s32[]{:S(2)}) async-start(), calls=%async_computation.8 | async-start | bytes 6291456
  514.4 286.8 %reduce-scatter.5.cloned.1.call-start = ((), (), s32[]{:S(2)}) async-start(), calls=%async_computation.7 | async-start | bytes 12582912 | tf_op jit(solution)/shard_map/reduce_scatter | solution.py:128
  713.1 100.6 %all-to-all-start.4 = ((bf16[16,8,32,512]{3,1,2,0:T(8,128)(2,1)}), bf16[16,8,32,512]{3,1,2,0:T(8,128)(2,1)}, u32[]{:S(2)}, u32[]{:S(2)}) async-start(bf16[16,8,32,512]{3,1,2,0:T(8,128)(2,1)} %copy.66), calls=%async_computation.4 | async-start | bytes 8388608 | tf_op jit(solution)/shard_map/all_to_all | solution.py:35
  748.8 3.2 copy-start
  753.7 55.4 %collective-permute-start = (bf16[8,512,256]{2,1,0:T(8,128)(2,1)}, bf16[8,512,256]{2,1,0:T(8,128)(2,1)}, u32[]{:S(2)}, u32[]{:S(2)}) collective-permute-start(bf16[8,512,256]{2,1,0:T(8,128)(2,1)} %dynamic-slice_convert_fusion.1), channel_id=1, source_target_pairs={{0,16},{16,0},{1,17},{17,1},{2,18},{18,2},{3,19},{19,3},{4,20},{20... | collective-permute-start | bytes 6291464 | tf_op jit(solution)/shard_map/ppermute | solution.py:51
  813.7 12.5 %slice-start = ((s8[8388608]{0:T(1024)(128)(4,1)}), s8[4194304]{0:T(1024)(128)(4,1)S(1)}, s32[]{:S(2)}) async-start(s8[8388608]{0:T(1024)(128)(4,1)} %bitcast.90), calls=%async_computation.9 | async-start | bytes 8388608
  817.5 2.0 copy-start.1
  819.5 6.8 slice-start.1
  834.2 47.7 %collective-permute-start.1 = (bf16[8,512,256]{2,1,0:T(8,128)(2,1)}, bf16[8,512,256]{2,1,0:T(8,128)(2,1)}, u32[]{:S(2)}, u32[]{:S(2)}) collective-permute-start(bf16[8,512,256]{2,1,0:T(8,128)(2,1)} %dynamic-slice_convert_fusion), channel_id=1, source_target_pairs={{0,16},{16,0},{1,17},{17,1},{2,18},{18,2},{3,19},{19,3},{4,20},{20... | collective-permute-start | bytes 6291464 | tf_op jit(solution)/shard_map/ppermute | solution.py:51
  868.6 15.8 %copy-start.2 = (bf16[8,512,256]{2,1,0:T(8,128)(2,1)S(1)}, bf16[8,512,256]{2,1,0:T(8,128)(2,1)}, u32[]{:S(2)}) copy-start(bf16[8,512,256]{2,1,0:T(8,128)(2,1)} %add_convert_fusion.1) | copy-start | bytes 6291460
Sparse Core Ops, SparseCore 0:
  514.6 55.2 reduce-scatter.6
  572.2 99.2 reduce-scatter.4

commit v5 on v4

--- a/solution.py
+++ b/solution.py
@@ -61,6 +61,12 @@
     kernel_wide = kernel.astype(jnp.float32)
     grad_scale = (lax.axis_size("dp") * tokens.shape[2]) ** (-0.5)
     f32 = jnp.float32
+    n_seq = lax.axis_size("seq")
+
+    first = jnp.einsum(
+        "acb,abd->acd", block_one, tokens, preferred_element_type=f32
+    ).astype(jnp.bfloat16)
+    first_cols = cols_recv(held(cols_send(first)))
 
     opened = jax.nn.sigmoid(gate_logits[0].astype(f32))
     incoming = cotangent[0].astype(f32)
@@ -68,13 +74,18 @@
     grad_third = jnp.einsum(
         "fch,fhd->fcd", block_one, grad_fourth, preferred_element_type=f32
     ).astype(jnp.bfloat16)
-    grad_third_cols = cols_recv(held(cols_send(grad_third)))
+    grad_third_send, first_cols = held((cols_send(grad_third), first_cols))
+    grad_third_cols = cols_recv(grad_third_send)
 
-    first = jnp.einsum(
-        "acb,abd->acd", block_one, tokens, preferred_element_type=f32
+    second = held(
+        jnp.einsum("cea,acd->ecd", block_two, first_cols, preferred_element_type=f32)
+    )
+    filtered = (kernel_wide * second).astype(jnp.bfloat16)
+    third = jnp.einsum(
+        "cef,ecd->fcd", block_two, filtered, preferred_element_type=f32
     ).astype(jnp.bfloat16)
-    first_send, grad_third_cols = held((cols_send(first), grad_third_cols))
-    first_cols = cols_recv(first_send)
+    third_send, grad_third_cols = held((rows_send(third), grad_third_cols))
+    third_rows = rows_recv(third_send)
 
     grad_filtered = held(
         jnp.einsum("cef,fcd->ecd", block_two, grad_third_cols, preferred_element_type=f32)
@@ -83,39 +94,6 @@
     grad_first = jnp.einsum(
         "cea,ecd->acd", block_two, grad_second, preferred_element_type=f32
     ).astype(jnp.bfloat16)
-    grad_first_send, first_cols = held((rows_send(grad_first), first_cols))
-    grad_first_rows = rows_recv(grad_first_send)
-
-    second = held(
-        jnp.einsum("cea,acd->ecd", block_two, first_cols, preferred_element_type=f32)
-    )
-    filtered = (kernel_wide * second).astype(jnp.bfloat16)
-    third = jnp.einsum(
-        "cef,ecd->fcd", block_two, filtered, preferred_element_type=f32
-    ).astype(jnp.bfloat16)
-    n_seq = lax.axis_size("seq")
-    own = third.shape[0] // n_seq
-    half = own // 2
-    halves = ((0, half), (half, own)) if half else ((0, own),)
-    third_split = rows_send(third)
-    pieces = [third_split[:, lo:hi] for lo, hi in halves]
-    pieces, grad_first_rows = held((pieces, grad_first_rows))
-
-    def finish(lo, hi, third_rows):
-        fourth = jnp.einsum(
-            "fch,fcd->fhd", block_one[lo:hi], third_rows, preferred_element_type=f32
-        ).astype(jnp.bfloat16)
-        fourth_wide = natural(fourth).astype(f32)
-        opened_k = opened[lo:hi]
-        output = (opened_k * fourth_wide).astype(jnp.bfloat16)
-        grad_gate = (
-            incoming[lo:hi] * fourth_wide * opened_k * (1.0 - opened_k)
-        ).astype(jnp.bfloat16)
-        outer_one = jnp.einsum(
-            "fhd,fcd->fch", grad_fourth[lo:hi], third_rows, preferred_element_type=f32
-        )
-        partial = (outer_one + outer_inputs[lo:hi]) * grad_scale
-        return output, grad_gate, dp_reduce_scatter(partial, 2)
 
     grad_kernel = (grad_filtered * second).astype(jnp.bfloat16)
     grad_block_two = (
@@ -128,29 +106,51 @@
     grad_kernel = lax.psum_scatter(grad_kernel, "dp", scatter_dimension=2, tiled=True)
     grad_block_two = lax.psum_scatter(grad_block_two, "dp", scatter_dimension=2, tiled=True)
 
-    grad_tokens = jnp.einsum(
-        "acb,acd->abd", block_one, grad_first_rows, preferred_element_type=f32
+    own = grad_first.shape[0] // n_seq
+    half = own // 2
+    halves = ((0, half), (half, own)) if half else ((0, own),)
+    grad_first_split = rows_send(grad_first)
+    pieces = [grad_first_split[:, lo:hi] for lo, hi in halves]
+    pieces, third_rows = held((pieces, third_rows))
+
+    fourth = jnp.einsum(
+        "fch,fcd->fhd", block_one, third_rows, preferred_element_type=f32
     ).astype(jnp.bfloat16)
-    outer_inputs = jnp.einsum(
-        "acd,abd->acb", grad_first_rows, tokens, preferred_element_type=f32
+    fourth_wide = natural(fourth).astype(f32)
+    output = (opened * fourth_wide).astype(jnp.bfloat16)
+    grad_gate = (incoming * fourth_wide * opened * (1.0 - opened)).astype(jnp.bfloat16)
+    outer_one = jnp.einsum(
+        "fhd,fcd->fch", grad_fourth, third_rows, preferred_element_type=f32
     )
 
-    outputs, grad_gates, grad_block_ones = [], [], []
+    def finish(lo, hi, grad_first_rows):
+        grad_tokens = natural(
+            jnp.einsum(
+                "acb,acd->abd", block_one[lo:hi], grad_first_rows, preferred_element_type=f32
+            ).astype(jnp.bfloat16)
+        )
+        outer_inputs = jnp.einsum(
+            "acd,abd->acb", grad_first_rows, tokens[lo:hi], preferred_element_type=f32
+        )
+        partial = (outer_one[lo:hi] + outer_inputs) * grad_scale
+        return grad_tokens, dp_reduce_scatter(partial, 2)
+
+    grad_tokens_parts, grad_block_ones = [], []
     pending = None
     for (lo, hi), piece in zip(halves, pieces):
         if pending is not None:
             piece, arrived = held((piece, pending[2]))
-            outputs_k = finish(pending[0], pending[1], arrived)
-            outputs.append(outputs_k[0])
-            grad_gates.append(outputs_k[1])
-            grad_block_ones.append(outputs_k[2])
+            done = finish(pending[0], pending[1], arrived)
+            grad_tokens_parts.append(done[0])
+            grad_block_ones.append(done[1])
         pending = (lo, hi, rows_recv(piece))
-    outputs_k = finish(*pending)
-    outputs.append(outputs_k[0])
-    grad_gates.append(outputs_k[1])
-    grad_block_ones.append(outputs_k[2])
-    output = jnp.concatenate(outputs, axis=0)
-    grad_gate = jnp.concatenate(grad_gates, axis=0)
+    arrived, grad_tokens_parts, output, grad_gate = held(
+        (pending[2], grad_tokens_parts, output, grad_gate)
+    )
+    done = finish(pending[0], pending[1], arrived)
+    grad_tokens_parts.append(done[0])
+    grad_block_ones.append(done[1])
+    grad_tokens = jnp.concatenate(grad_tokens_parts, axis=0)
     grad_block_one = jnp.concatenate(grad_block_ones, axis=0)
     return (
         output[None],

time: 904 us -> 879 us (0.972)
  waiting for transfers between devices: 368 us -> 472 us
  blocking collectives: 97.1 us -> 0 us
  other arithmetic: 62.5 us -> 42.9 us
  local copies, waits for them, and re-layouts: 102 us -> 87.6 us
    all_to_all x2 -> x3, waiting for transfers between devices: 61.8 us -> 176 us  [rows_recv(): moved = lax.all_to_all(x, 'seq', split_axis=0, concat_axis=0, tiled=True)]
    all_to_all x1 -> x0, blocking collectives: 97.1 us -> none  [rows_recv(): moved = lax.all_to_all(x, 'seq', split_axis=0, concat_axis=0, tiled=True)]
    convert_element_type x1 -> x0, other arithmetic: 11.4 us -> none  [body(): incoming = cotangent[0].astype(f32)]
    all_to_all x2, waiting for transfers between devices: 293 us -> 281 us  [cols_recv(): lax.all_to_all(x, 'seq', split_axis=0, concat_axis=0, tiled=True)]
    unnamed x17 -> x10, local copies, waits for them, and re-layouts: 61.1 us -> 50.2 us
  transfers between devices with their start and end apart: 8 -> 9, of which waited for: 4 -> 6; matrix products, arithmetic and copies ran while one was open for 35% -> 36% of each run, Pallas kernels for 0% -> 0%
where the time goes in v5:
time: 879 us; the launch traced here: 871 us
  waiting for transfers between devices  472 us (54%)
  matrix products  223 us (25%)
  local copies, waits for them, and re-layouts  87.6 us (10%)
  other arithmetic  42.9 us (5%)
  starting transfers between devices  30.4 us (3%)
  between operations  14.6 us (2%)
    all_to_all x2, waiting for transfers between devices, cols_recv(): lax.all_to_all(x, 'seq', split_axis=0, concat_axis=0, tiled=True)  281 us
    all_to_all x3, waiting for transfers between devices, rows_recv(): moved = lax.all_to_all(x, 'seq', split_axis=0, concat_axis=0, tiled=True)  176 us
    unnamed x10, local copies, waits for them, and re-layouts  50.2 us
    dot_general x1, matrix products, body(): jnp.einsum('fch,fcd->fhd', block_one, third_rows, preferred_element_type=...  25.3 us
    dot_general x1, matrix products, body(): jnp.einsum('fcd,ecd->cef', grad_third_cols, filtered, preferred_element_t...  22 us
    dot_general x1, matrix products, body(): jnp.einsum('ecd,acd->cea', grad_second, first_cols, preferred_element_typ...  21.4 us
    dot_general x1, matrix products, body(): jnp.einsum('fhd,fcd->fch', grad_fourth, third_rows, preferred_element_typ...  20.8 us
    dot_general x1, matrix products, body(): jnp.einsum('cea,acd->ecd', block_two, first_cols, preferred_element_type=...  20.4 us
  transfers between devices with their start and end apart: 9, of which 6 were waited for; matrix products, arithmetic and copies ran while one was open for 36% of the time, Pallas kernels for 0%

profile of v5, /device:TPU:10, one launch (start us, length us, event | category | flops | bytes accessed | tf_op | source)
XLA Modules:
  0.0 870.7 jit_solution(2900359897574918956)
XLA Ops:
  7.2 13.7 %fusion.24 = bf16[16,512,512]{2,1,0:T(8,128)(2,1)} fusion(bf16[16,512,512]{2,1,0:T(8,128)(2,1)} %param.10, bf16[1,16,512,512]{3,2,1,0:T(8,128)(2,1)} %param.6), kind=kOutput, calls=%fused_computation.38 | convolution fusion | flops 4299161600 | bytes 25165824 | tf_op jit(solution)/shard_map/acb,abd->acd/dot_general | solution.py:66
  20.9 8.4 copy.107
  29.3 6.2 all-to-all-start
  35.5 11.4 %fusion.3 = bf16[16,512,512]{2,1,0:T(8,128)(2,1)} fusion(bf16[1,16,512,512]{3,2,1,0:T(8,128)(2,1)} %param.9, bf16[1,16,512,512]{3,2,1,0:T(8,128)(2,1)} %param.7), kind=kLoop, calls=%fused_computation.8 | loop fusion | flops 29360128 | bytes 25165824 | tf_op jit(solution)/shard_map/convert_element_type | solution.py:73
  46.9 13.7 %convolution_convert_fusion.2 = bf16[16,512,512]{1,2,0:T(8,128)(2,1)} fusion(bf16[16,512,512]{2,1,0:T(8,128)(2,1)} %param.10, bf16[16,512,512]{2,1,0:T(8,128)(2,1)} %fusion.3), kind=kOutput, calls=%fused_computation.41 | convolution fusion | flops 4299161600 | bytes 25165824 | tf_op jit(solution)/shard_map/fch,fhd->fcd/dot_general | solution.py:74
  60.6 8.4 copy.108
  69.1 148.5 %all-to-all-done = bf16[16,16,32,512]{3,2,1,0:T(8,128)(2,1)} async-done(((bf16[16,16,32,512]{3,2,1,0:T(8,128)(2,1)}), bf16[16,16,32,512]{3,2,1,0:T(8,128)(2,1)}, u32[]{:S(2)}, u32[]{:S(2)}) %all-to-all-start) | async-done | bytes 8388640 | tf_op jit(solution)/shard_map/all_to_all | solution.py:19
  217.6 5.7 all-to-all-start.1
  223.3 13.7 %copy.30 = bf16[256,32,512]{0,2,1:T(8,128)(2,1)} copy(bf16[256,32,512]{2,1,0:T(8,128)(2,1)} %param.8) | data formatting | bytes 16777216 | tf_op args[2]
  237.0 20.4 %convolution_bitcast_fusion.1 = f32[256,32,512]{0,2,1:T(8,128)} fusion(bf16[32,256,256]{2,1,0:T(8,128)(2,1)} %param.11, bf16[256,32,512]{2,1,0:T(8,128)(2,1)} %bitcast.8), kind=kOutput, calls=%fused_computation.16 | convolution fusion | flops 2147483648 | bytes 29360128 | tf_op jit(solution)/shard_map/cea,acd->ecd/dot_general | solution.py:81
  257.4 14.9 %convolution_convert_fusion.1 = bf16[32,512,256]{1,2,0:T(8,128)(2,1)} fusion(bf16[32,256,256]{2,1,0:T(8,128)(2,1)} %param.11, f32[256,32,512]{0,2,1:T(8,128)} %convolution_bitcast_fusion.1, bf16[256,32,512]{0,2,1:T(8,128)(2,1)} %copy.30), kind=kOutput, calls=%fused_computation.40 | convolution fusion | flops 2164260864 | bytes 37748736 | tf_op jit(solution)/shard_map/cef,ecd->fcd/dot_general | solution.py:84
  272.3 132.9 %all-to-all-done.1 = bf16[16,16,32,512]{3,2,1,0:T(8,128)(2,1)} async-done(((bf16[16,16,32,512]{3,2,1,0:T(8,128)(2,1)}), bf16[16,16,32,512]{3,2,1,0:T(8,128)(2,1)}, u32[]{:S(2)}, u32[]{:S(2)}) %all-to-all-start.1) | async-done | bytes 8388640 | tf_op jit(solution)/shard_map/all_to_all | solution.py:19
  405.2 8.2 copy.41
  418.5 20.4 %convolution_bitcast_fusion = f32[256,32,512]{0,2,1:T(8,128)} fusion(bf16[32,256,256]{2,1,0:T(8,128)(2,1)} %param.11, bf16[256,32,512]{2,1,0:T(8,128)(2,1)} %bitcast.12), kind=kOutput, calls=%fused_computation.15 | convolution fusion | flops 2147483648 | bytes 29360128 | tf_op jit(solution)/shard_map/cef,fcd->ecd/dot_general | solution.py:91
  438.9 21.4 %fusion.12 = f32[32,256,256]{2,1,0:T(8,128)} fusion(bf16[256,32,512]{2,1,0:T(8,128)(2,1)} %bitcast.8, f32[256,32,512]{0,2,1:T(8,128)} %convolution_bitcast_fusion, bf16[256,32,512]{0,2,1:T(8,128)(2,1)} %copy.30), kind=kOutput, calls=%fused_computation.28 | convolution fusion | flops 2160066560 | bytes 41943040 | tf_op jit(solution)/shard_map/ecd,acd->cea/dot_general | solution.py:102
  460.3 22.0 %multiply_convert_fusion.1 = bf16[32,256,256]{2,1,0:T(8,128)(2,1)} fusion(f32[32,256,256]{2,1,0:T(8,128)} %fusion.12, bf16[256,32,512]{2,1,0:T(8,128)(2,1)} %bitcast.12, f32[256,32,512]{0,2,1:T(8,128)} %convolution_bitcast_fusion.1, bf16[256,32,512]{0,2,1:T(8,128)(2,1)} %copy.30), kind=kOutput, calls=%fused_computation.26 | convolution fusion | flops 2166358016 | bytes 46137344 | tf_op jit(solution)/shard_map/fcd,ecd->cef/dot_general | solution.py:101
  482.3 8.2 copy.63
  490.5 8.5 copy.69
  499.1 15.4 %convolution_convert_fusion = bf16[32,512,256]{1,2,0:T(8,128)(2,1)} fusion(bf16[32,256,256]{2,1,0:T(8,128)(2,1)} %param.11, f32[256,32,512]{0,2,1:T(8,128)} %convolution_bitcast_fusion, bf16[256,32,512]{0,2,1:T(8,128)(2,1)} %copy.30), kind=kOutput, calls=%fused_computation.39 | convolution fusion | flops 2164260864 | bytes 37748736 | tf_op jit(solution)/shard_map/cea,ecd->acd/dot_general | solution.py:94
  523.6 77.0 %all-to-all-done.2 = bf16[16,16,32,512]{3,1,2,0:T(8,128)(2,1)} async-done(((bf16[16,16,32,512]{3,1,2,0:T(8,128)(2,1)}), bf16[16,16,32,512]{3,1,2,0:T(8,128)(2,1)}, u32[]{:S(2)}, u32[]{:S(2)}) %all-to-all-start.2) | async-done | bytes 8388640 | tf_op jit(solution)/shard_map/all_to_all | solution.py:35
  605.6 14.9 %multiply_convert_fusion = bf16[256,32,512]{0,2,1:T(8,128)(2,1)} fusion(f32[256,32,512]{0,2,1:T(8,128)} %convolution_bitcast_fusion, f32[256,32,512]{0,2,1:T(8,128)} %convolution_bitcast_fusion.1), kind=kLoop, calls=%fused_computation.13 | loop fusion | flops 8388608 | bytes 41943040 | tf_op jit(solution)/shard_map/convert_element_type | solution.py:98
  620.6 77.2 %all-to-all-done.3 = bf16[16,8,32,512]{3,1,2,0:T(8,128)(2,1)} async-done(((bf16[16,8,32,512]{3,1,2,0:T(8,128)(2,1)}), bf16[16,8,32,512]{3,1,2,0:T(8,128)(2,1)}, u32[]{:S(2)}, u32[]{:S(2)}) %all-to-all-start.3) | async-done | bytes 4194336 | tf_op jit(solution)/shard_map/all_to_all | solution.py:35
  703.2 20.8 %fusion.17 = f32[16,512,512]{2,1,0:T(8,128)} fusion(bf16[16,512,512]{2,1,0:T(8,128)(2,1)} %fusion.3, bf16[16,512,512]{2,0,1:T(8,128)(2,1)} %bitcast.18), kind=kOutput, calls=%fused_computation.33 | convolution fusion | flops 4294967296 | bytes 33554432 | tf_op jit(solution)/shard_map/fhd,fcd->fch/dot_general | solution.py:122
  723.9 25.3 %fusion.6 = (bf16[16,512,512]{2,1,0:T(8,128)(2,1)}, bf16[16,512,512]{2,1,0:T(8,128)(2,1)}) fusion(bf16[1,16,512,512]{3,2,1,0:T(8,128)(2,1)} %param.9, bf16[1,16,512,512]{3,2,1,0:T(8,128)(2,1)} %param.7, bf16[16,512,512]{2,1,0:T(8,128)(2,1)} %param.10, bf16[16,512,512]{2,0,1:T(8,128)(2,1)} %bitcast.18), kind=kOutput, calls=%fused_computation.11 | convolution fusion | flops 4353687552 | bytes 50331648 | tf_op jit(solution)/shard_map/fch,fcd->fhd/dot_general | solution.py:116
  749.3 9.2 %fusion.8 = f32[8,512,512]{2,1,0:T(8,128)S(1)} fusion(f32[16,512,512]{2,1,0:T(8,128)} %fusion.17, bf16[1,16,512,512]{3,2,1,0:T(8,128)(2,1)} %param.6, bf16[8,512,512]{2,0,1:T(8,128)(2,1)} %bitcast.20), kind=kOutput, calls=%fused_computation.20 | convolution fusion | flops 2151677952 | bytes 25165824 | tf_op jit(solution)/shard_map/acd,abd->acb/dot_general | solution.py:132
  764.8 8.5 convert_bitcast_fusion.1
  773.3 21.9 %all-to-all-done.4 = bf16[16,8,32,512]{3,1,2,0:T(8,128)(2,1)} async-done(((bf16[16,8,32,512]{3,1,2,0:T(8,128)(2,1)}), bf16[16,8,32,512]{3,1,2,0:T(8,128)(2,1)}, u32[]{:S(2)}, u32[]{:S(2)}) %all-to-all-start.4) | async-done | bytes 4194336 | tf_op jit(solution)/shard_map/all_to_all | solution.py:35
  795.2 9.2 %fusion.7 = f32[8,512,512]{2,1,0:T(8,128)S(1)} fusion(f32[16,512,512]{2,1,0:T(8,128)} %fusion.17, bf16[1,16,512,512]{3,2,1,0:T(8,128)(2,1)} %param.6, bf16[8,512,512]{2,0,1:T(8,128)(2,1)} %bitcast.22), kind=kOutput, calls=%fused_computation.18 | convolution fusion | flops 2151677952 | bytes 25165824 | tf_op jit(solution)/shard_map/acd,abd->acb/dot_general | solution.py:132
  816.0 8.1 copy.55
  827.4 8.5 convert_bitcast_fusion
  835.9 7.6 maximum_bitcast_fusion
  843.5 14.3 %collective-permute-done.1 = bf16[8,512,256]{2,1,0:T(8,128)(2,1)} collective-permute-done((bf16[8,512,256]{2,1,0:T(8,128)(2,1)}, bf16[8,512,256]{2,1,0:T(8,128)(2,1)}, u32[]{:S(2)}, u32[]{:S(2)}) %collective-permute-start.1) | collective-permute-done | bytes 2097184 | tf_op jit(solution)/shard_map/ppermute | solution.py:51
  (26 shorter events, 51.6 us)
Async XLA Ops:
  29.3 188.3 %all-to-all-start = ((bf16[16,16,32,512]{3,2,1,0:T(8,128)(2,1)}), bf16[16,16,32,512]{3,2,1,0:T(8,128)(2,1)}, u32[]{:S(2)}, u32[]{:S(2)}) async-start(bf16[16,16,32,512]{3,2,1,0:T(8,128)(2,1)} %bitcast.85), calls=%async_computation | async-start | bytes 16777216 | tf_op jit(solution)/shard_map/all_to_all | solution.py:19
  217.6 187.6 %all-to-all-start.1 = ((bf16[16,16,32,512]{3,2,1,0:T(8,128)(2,1)}), bf16[16,16,32,512]{3,2,1,0:T(8,128)(2,1)}, u32[]{:S(2)}, u32[]{:S(2)}) async-start(bf16[16,16,32,512]{3,2,1,0:T(8,128)(2,1)} %bitcast.84), calls=%async_computation.1 | async-start | bytes 16777216 | tf_op jit(solution)/shard_map/all_to_all | solution.py:19
  413.4 187.1 %all-to-all-start.2 = ((bf16[16,16,32,512]{3,1,2,0:T(8,128)(2,1)}), bf16[16,16,32,512]{3,1,2,0:T(8,128)(2,1)}, u32[]{:S(2)}, u32[]{:S(2)}) async-start(bf16[16,16,32,512]{3,1,2,0:T(8,128)(2,1)} %copy.41), calls=%async_computation.2 | async-start | bytes 16777216 | tf_op jit(solution)/shard_map/all_to_all | solution.py:35
  418.5 392.3 %reduce-scatter.7.cloned.1.call-start = ((), (), s32[]{:S(2)}) async-start(), calls=%async_computation.8 | async-start | bytes 6291456
  600.5 97.2 %all-to-all-start.3 = ((bf16[16,8,32,512]{3,1,2,0:T(8,128)(2,1)}), bf16[16,8,32,512]{3,1,2,0:T(8,128)(2,1)}, u32[]{:S(2)}, u32[]{:S(2)}) async-start(bf16[16,8,32,512]{3,1,2,0:T(8,128)(2,1)} %copy.65), calls=%async_computation.3 | async-start | bytes 8388608 | tf_op jit(solution)/shard_map/all_to_all | solution.py:35
  605.6 210.4 %reduce-scatter.5.cloned.1.call-start = ((), (), s32[]{:S(2)}) async-start(), calls=%async_computation.7 | async-start | bytes 12582912 | tf_op jit(solution)/shard_map/reduce_scatter | solution.py:106
  697.8 97.4 %all-to-all-start.4 = ((bf16[16,8,32,512]{3,1,2,0:T(8,128)(2,1)}), bf16[16,8,32,512]{3,1,2,0:T(8,128)(2,1)}, u32[]{:S(2)}, u32[]{:S(2)}) async-start(bf16[16,8,32,512]{3,1,2,0:T(8,128)(2,1)} %copy.66), calls=%async_computation.4 | async-start | bytes 8388608 | tf_op jit(solution)/shard_map/all_to_all | solution.py:35
  758.5 3.2 copy-start
  763.3 60.7 %collective-permute-start = (bf16[8,512,256]{2,1,0:T(8,128)(2,1)}, bf16[8,512,256]{2,1,0:T(8,128)(2,1)}, u32[]{:S(2)}, u32[]{:S(2)}) collective-permute-start(bf16[8,512,256]{2,1,0:T(8,128)(2,1)} %dynamic-slice_convert_fusion.1), channel_id=1, source_target_pairs={{0,16},{16,0},{1,17},{17,1},{2,18},{18,2},{3,19},{19,3},{4,20},{20... | collective-permute-start | bytes 6291464 | tf_op jit(solution)/shard_map/ppermute | solution.py:51
  804.4 3.2 copy-start.1
  809.2 48.5 %collective-permute-start.1 = (bf16[8,512,256]{2,1,0:T(8,128)(2,1)}, bf16[8,512,256]{2,1,0:T(8,128)(2,1)}, u32[]{:S(2)}, u32[]{:S(2)}) collective-permute-start(bf16[8,512,256]{2,1,0:T(8,128)(2,1)} %dynamic-slice_convert_fusion), channel_id=1, source_target_pairs={{0,16},{16,0},{1,17},{17,1},{2,18},{18,2},{3,19},{19,3},{4,20},{20... | collective-permute-start | bytes 6291464 | tf_op jit(solution)/shard_map/ppermute | solution.py:51
Sparse Core Ops, SparseCore 0:
  499.2 55.2 reduce-scatter.6
  620.7 100.2 reduce-scatter.4

commit v6 on v5

--- a/solution.py
+++ b/solution.py
@@ -139,7 +139,9 @@
     pending = None
     for (lo, hi), piece in zip(halves, pieces):
         if pending is not None:
-            piece, arrived = held((piece, pending[2]))
+            piece, arrived, (output, grad_gate, outer_one) = held(
+                (piece, pending[2], (output, grad_gate, outer_one))
+            )
             done = finish(pending[0], pending[1], arrived)
             grad_tokens_parts.append(done[0])
             grad_block_ones.append(done[1])

time: 879 us -> 879 us (level)
  no operation moved by 1% of the time
where the time goes in v6:
time: 879 us; the launch traced here: 871 us
  waiting for transfers between devices  471 us (54%)
  matrix products  224 us (25%)
  local copies, waits for them, and re-layouts  87.6 us (10%)
  other arithmetic  43.1 us (5%)
  starting transfers between devices  30.5 us (3%)
  between operations  14.6 us (2%)
    all_to_all x2, waiting for transfers between devices, cols_recv(): lax.all_to_all(x, 'seq', split_axis=0, concat_axis=0, tiled=True)  281 us
    all_to_all x3, waiting for transfers between devices, rows_recv(): moved = lax.all_to_all(x, 'seq', split_axis=0, concat_axis=0, tiled=True)  175 us
    unnamed x10, local copies, waits for them, and re-layouts  50.2 us
    dot_general x1, matrix products, body(): jnp.einsum('fch,fcd->fhd', block_one, third_rows, preferred_element_type=...  25.7 us
    dot_general x1, matrix products, body(): jnp.einsum('fcd,ecd->cef', grad_third_cols, filtered, preferred_element_t...  22 us
    dot_general x1, matrix products, body(): jnp.einsum('ecd,acd->cea', grad_second, first_cols, preferred_element_typ...  21.4 us
    dot_general x1, matrix products, body(): jnp.einsum('fhd,fcd->fch', grad_fourth, third_rows, preferred_element_typ...  20.7 us
    dot_general x1, matrix products, body(): jnp.einsum('cea,acd->ecd', block_two, first_cols, preferred_element_type=...  20.4 us
  transfers between devices with their start and end apart: 9, of which 6 were waited for; matrix products, arithmetic and copies ran while one was open for 36% of the time, Pallas kernels for 0%

profile of v6, /device:TPU:10, one launch (start us, length us, event | category | flops | bytes accessed | tf_op | source)
XLA Modules:
  0.0 870.5 jit_solution(14281090042024625533)
XLA Ops:
  7.2 13.7 %fusion.22 = bf16[16,512,512]{2,1,0:T(8,128)(2,1)} fusion(bf16[16,512,512]{2,1,0:T(8,128)(2,1)} %param.10, bf16[1,16,512,512]{3,2,1,0:T(8,128)(2,1)} %param.6), kind=kOutput, calls=%fused_computation.36 | convolution fusion | flops 4299161600 | bytes 25165824 | tf_op jit(solution)/shard_map/acb,abd->acd/dot_general | solution.py:66
  20.9 8.4 copy.107
  29.3 6.2 all-to-all-start
  35.5 11.4 %fusion.3 = bf16[16,512,512]{2,1,0:T(8,128)(2,1)} fusion(bf16[1,16,512,512]{3,2,1,0:T(8,128)(2,1)} %param.9, bf16[1,16,512,512]{3,2,1,0:T(8,128)(2,1)} %param.7), kind=kLoop, calls=%fused_computation.8 | loop fusion | flops 29360128 | bytes 25165824 | tf_op jit(solution)/shard_map/convert_element_type | solution.py:73
  46.9 13.7 %convolution_convert_fusion.2 = bf16[16,512,512]{1,2,0:T(8,128)(2,1)} fusion(bf16[16,512,512]{2,1,0:T(8,128)(2,1)} %param.10, bf16[16,512,512]{2,1,0:T(8,128)(2,1)} %fusion.3), kind=kOutput, calls=%fused_computation.39 | convolution fusion | flops 4299161600 | bytes 25165824 | tf_op jit(solution)/shard_map/fch,fhd->fcd/dot_general | solution.py:74
  60.6 8.4 copy.108
  69.1 148.5 %all-to-all-done = bf16[16,16,32,512]{3,2,1,0:T(8,128)(2,1)} async-done(((bf16[16,16,32,512]{3,2,1,0:T(8,128)(2,1)}), bf16[16,16,32,512]{3,2,1,0:T(8,128)(2,1)}, u32[]{:S(2)}, u32[]{:S(2)}) %all-to-all-start) | async-done | bytes 8388640 | tf_op jit(solution)/shard_map/all_to_all | solution.py:19
  217.6 5.7 all-to-all-start.1
  223.3 13.7 %copy.30 = bf16[256,32,512]{0,2,1:T(8,128)(2,1)} copy(bf16[256,32,512]{2,1,0:T(8,128)(2,1)} %param.8) | data formatting | bytes 16777216 | tf_op args[2]
  237.0 20.4 %convolution_bitcast_fusion.1 = f32[256,32,512]{0,2,1:T(8,128)} fusion(bf16[32,256,256]{2,1,0:T(8,128)(2,1)} %param.11, bf16[256,32,512]{2,1,0:T(8,128)(2,1)} %bitcast.8), kind=kOutput, calls=%fused_computation.16 | convolution fusion | flops 2147483648 | bytes 29360128 | tf_op jit(solution)/shard_map/cea,acd->ecd/dot_general | solution.py:81
  257.4 14.9 %convolution_convert_fusion.1 = bf16[32,512,256]{1,2,0:T(8,128)(2,1)} fusion(bf16[32,256,256]{2,1,0:T(8,128)(2,1)} %param.11, f32[256,32,512]{0,2,1:T(8,128)} %convolution_bitcast_fusion.1, bf16[256,32,512]{0,2,1:T(8,128)(2,1)} %copy.30), kind=kOutput, calls=%fused_computation.38 | convolution fusion | flops 2164260864 | bytes 37748736 | tf_op jit(solution)/shard_map/cef,ecd->fcd/dot_general | solution.py:84
  272.3 132.9 %all-to-all-done.1 = bf16[16,16,32,512]{3,2,1,0:T(8,128)(2,1)} async-done(((bf16[16,16,32,512]{3,2,1,0:T(8,128)(2,1)}), bf16[16,16,32,512]{3,2,1,0:T(8,128)(2,1)}, u32[]{:S(2)}, u32[]{:S(2)}) %all-to-all-start.1) | async-done | bytes 8388640 | tf_op jit(solution)/shard_map/all_to_all | solution.py:19
  405.2 8.2 copy.41
  418.5 20.4 %convolution_bitcast_fusion = f32[256,32,512]{0,2,1:T(8,128)} fusion(bf16[32,256,256]{2,1,0:T(8,128)(2,1)} %param.11, bf16[256,32,512]{2,1,0:T(8,128)(2,1)} %bitcast.12), kind=kOutput, calls=%fused_computation.15 | convolution fusion | flops 2147483648 | bytes 29360128 | tf_op jit(solution)/shard_map/cef,fcd->ecd/dot_general | solution.py:91
  438.9 21.4 %fusion.10 = f32[32,256,256]{2,1,0:T(8,128)} fusion(bf16[256,32,512]{2,1,0:T(8,128)(2,1)} %bitcast.8, f32[256,32,512]{0,2,1:T(8,128)} %convolution_bitcast_fusion, bf16[256,32,512]{0,2,1:T(8,128)(2,1)} %copy.30), kind=kOutput, calls=%fused_computation.26 | convolution fusion | flops 2160066560 | bytes 41943040 | tf_op jit(solution)/shard_map/ecd,acd->cea/dot_general | solution.py:102
  460.3 22.0 %multiply_convert_fusion.1 = bf16[32,256,256]{2,1,0:T(8,128)(2,1)} fusion(f32[32,256,256]{2,1,0:T(8,128)} %fusion.10, bf16[256,32,512]{2,1,0:T(8,128)(2,1)} %bitcast.12, f32[256,32,512]{0,2,1:T(8,128)} %convolution_bitcast_fusion.1, bf16[256,32,512]{0,2,1:T(8,128)(2,1)} %copy.30), kind=kOutput, calls=%fused_computation.22 | convolution fusion | flops 2166358016 | bytes 46137344 | tf_op jit(solution)/shard_map/fcd,ecd->cef/dot_general | solution.py:101
  482.3 8.2 copy.63
  490.5 8.5 copy.69
  499.1 15.4 %convolution_convert_fusion = bf16[32,512,256]{1,2,0:T(8,128)(2,1)} fusion(bf16[32,256,256]{2,1,0:T(8,128)(2,1)} %param.11, f32[256,32,512]{0,2,1:T(8,128)} %convolution_bitcast_fusion, bf16[256,32,512]{0,2,1:T(8,128)(2,1)} %copy.30), kind=kOutput, calls=%fused_computation.37 | convolution fusion | flops 2164260864 | bytes 37748736 | tf_op jit(solution)/shard_map/cea,ecd->acd/dot_general | solution.py:94
  523.6 77.0 %all-to-all-done.2 = bf16[16,16,32,512]{3,1,2,0:T(8,128)(2,1)} async-done(((bf16[16,16,32,512]{3,1,2,0:T(8,128)(2,1)}), bf16[16,16,32,512]{3,1,2,0:T(8,128)(2,1)}, u32[]{:S(2)}, u32[]{:S(2)}) %all-to-all-start.2) | async-done | bytes 8388640 | tf_op jit(solution)/shard_map/all_to_all | solution.py:35
  605.6 15.1 %multiply_convert_fusion = bf16[256,32,512]{0,2,1:T(8,128)(2,1)} fusion(f32[256,32,512]{0,2,1:T(8,128)} %convolution_bitcast_fusion, f32[256,32,512]{0,2,1:T(8,128)} %convolution_bitcast_fusion.1), kind=kLoop, calls=%fused_computation.13 | loop fusion | flops 8388608 | bytes 41943040 | tf_op jit(solution)/shard_map/convert_element_type | solution.py:98
  620.7 20.7 %fusion.15 = f32[16,512,512]{2,1,0:T(8,128)} fusion(bf16[16,512,512]{2,1,0:T(8,128)(2,1)} %fusion.3, bf16[16,512,512]{2,0,1:T(8,128)(2,1)} %bitcast.18), kind=kOutput, calls=%fused_computation.31 | convolution fusion | flops 4294967296 | bytes 33554432 | tf_op jit(solution)/shard_map/fhd,fcd->fch/dot_general | solution.py:122
  641.4 25.7 %fusion.6 = (bf16[16,512,512]{2,1,0:T(8,128)(2,1)}, bf16[16,512,512]{2,1,0:T(8,128)(2,1)}) fusion(bf16[1,16,512,512]{3,2,1,0:T(8,128)(2,1)} %param.9, bf16[1,16,512,512]{3,2,1,0:T(8,128)(2,1)} %param.7, bf16[16,512,512]{2,1,0:T(8,128)(2,1)} %param.10, bf16[16,512,512]{2,0,1:T(8,128)(2,1)} %bitcast.18), kind=kOutput, calls=%fused_computation.11 | convolution fusion | flops 4353687552 | bytes 50331648 | tf_op jit(solution)/shard_map/fch,fcd->fhd/dot_general | solution.py:116
  667.1 30.6 %all-to-all-done.3 = bf16[16,8,32,512]{3,1,2,0:T(8,128)(2,1)} async-done(((bf16[16,8,32,512]{3,1,2,0:T(8,128)(2,1)}), bf16[16,8,32,512]{3,1,2,0:T(8,128)(2,1)}, u32[]{:S(2)}, u32[]{:S(2)}) %all-to-all-start.3) | async-done | bytes 4194336 | tf_op jit(solution)/shard_map/all_to_all | solution.py:35
  703.2 9.3 %add_multiply_fusion.1 = f32[8,512,512]{2,1,0:T(8,128)S(1)} fusion(f32[16,512,512]{2,1,0:T(8,128)} %fusion.15, bf16[1,16,512,512]{3,2,1,0:T(8,128)(2,1)} %param.6, bf16[8,512,512]{2,0,1:T(8,128)(2,1)} %bitcast.20), kind=kOutput, calls=%fused_computation.24 | convolution fusion | flops 2151677952 | bytes 25165824 | tf_op jit(solution)/shard_map/acd,abd->acb/dot_general | solution.py:132
  718.8 8.6 convert_bitcast_fusion.1
  727.4 67.8 %all-to-all-done.4 = bf16[16,8,32,512]{3,1,2,0:T(8,128)(2,1)} async-done(((bf16[16,8,32,512]{3,1,2,0:T(8,128)(2,1)}), bf16[16,8,32,512]{3,1,2,0:T(8,128)(2,1)}, u32[]{:S(2)}, u32[]{:S(2)}) %all-to-all-start.4) | async-done | bytes 4194336 | tf_op jit(solution)/shard_map/all_to_all | solution.py:35
  795.2 9.2 %add_multiply_fusion = f32[8,512,512]{2,1,0:T(8,128)S(1)} fusion(f32[16,512,512]{2,1,0:T(8,128)} %fusion.15, bf16[1,16,512,512]{3,2,1,0:T(8,128)(2,1)} %param.6, bf16[8,512,512]{2,0,1:T(8,128)(2,1)} %bitcast.24), kind=kOutput, calls=%fused_computation.23 | convolution fusion | flops 2151677952 | bytes 25165824 | tf_op jit(solution)/shard_map/acd,abd->acb/dot_general | solution.py:132
  816.0 8.1 copy.55
  827.4 8.5 convert_bitcast_fusion
  836.0 7.6 maximum_bitcast_fusion
  843.5 14.0 %collective-permute-done.1 = bf16[8,512,256]{2,1,0:T(8,128)(2,1)} collective-permute-done((bf16[8,512,256]{2,1,0:T(8,128)(2,1)}, bf16[8,512,256]{2,1,0:T(8,128)(2,1)}, u32[]{:S(2)}, u32[]{:S(2)}) %collective-permute-start.1) | collective-permute-done | bytes 2097184 | tf_op jit(solution)/shard_map/ppermute | solution.py:51
  (26 shorter events, 51.7 us)
Async XLA Ops:
  29.3 188.3 %all-to-all-start = ((bf16[16,16,32,512]{3,2,1,0:T(8,128)(2,1)}), bf16[16,16,32,512]{3,2,1,0:T(8,128)(2,1)}, u32[]{:S(2)}, u32[]{:S(2)}) async-start(bf16[16,16,32,512]{3,2,1,0:T(8,128)(2,1)} %bitcast.85), calls=%async_computation | async-start | bytes 16777216 | tf_op jit(solution)/shard_map/all_to_all | solution.py:19
  217.6 187.6 %all-to-all-start.1 = ((bf16[16,16,32,512]{3,2,1,0:T(8,128)(2,1)}), bf16[16,16,32,512]{3,2,1,0:T(8,128)(2,1)}, u32[]{:S(2)}, u32[]{:S(2)}) async-start(bf16[16,16,32,512]{3,2,1,0:T(8,128)(2,1)} %bitcast.84), calls=%async_computation.1 | async-start | bytes 16777216 | tf_op jit(solution)/shard_map/all_to_all | solution.py:19
  413.4 187.1 %all-to-all-start.2 = ((bf16[16,16,32,512]{3,1,2,0:T(8,128)(2,1)}), bf16[16,16,32,512]{3,1,2,0:T(8,128)(2,1)}, u32[]{:S(2)}, u32[]{:S(2)}) async-start(bf16[16,16,32,512]{3,1,2,0:T(8,128)(2,1)} %copy.41), calls=%async_computation.2 | async-start | bytes 16777216 | tf_op jit(solution)/shard_map/all_to_all | solution.py:35
  418.5 392.3 %reduce-scatter.7.cloned.1.call-start = ((), (), s32[]{:S(2)}) async-start(), calls=%async_computation.8 | async-start | bytes 6291456
  600.5 97.2 %all-to-all-start.3 = ((bf16[16,8,32,512]{3,1,2,0:T(8,128)(2,1)}), bf16[16,8,32,512]{3,1,2,0:T(8,128)(2,1)}, u32[]{:S(2)}, u32[]{:S(2)}) async-start(bf16[16,8,32,512]{3,1,2,0:T(8,128)(2,1)} %copy.65), calls=%async_computation.3 | async-start | bytes 8388608 | tf_op jit(solution)/shard_map/all_to_all | solution.py:35
  605.6 210.4 %reduce-scatter.5.cloned.1.call-start = ((), (), s32[]{:S(2)}) async-start(), calls=%async_computation.7 | async-start | bytes 12582912 | tf_op jit(solution)/shard_map/reduce_scatter | solution.py:106
  697.8 97.5 %all-to-all-start.4 = ((bf16[16,8,32,512]{3,1,2,0:T(8,128)(2,1)}), bf16[16,8,32,512]{3,1,2,0:T(8,128)(2,1)}, u32[]{:S(2)}, u32[]{:S(2)}) async-start(bf16[16,8,32,512]{3,1,2,0:T(8,128)(2,1)} %copy.66), calls=%async_computation.4 | async-start | bytes 8388608 | tf_op jit(solution)/shard_map/all_to_all | solution.py:35
  712.5 3.2 copy-start
  717.3 106.7 %collective-permute-start = (bf16[8,512,256]{2,1,0:T(8,128)(2,1)}, bf16[8,512,256]{2,1,0:T(8,128)(2,1)}, u32[]{:S(2)}, u32[]{:S(2)}) collective-permute-start(bf16[8,512,256]{2,1,0:T(8,128)(2,1)} %dynamic-slice_convert_fusion.1), channel_id=1, source_target_pairs={{0,16},{16,0},{1,17},{17,1},{2,18},{18,2},{3,19},{19,3},{4,20},{20... | collective-permute-start | bytes 6291464 | tf_op jit(solution)/shard_map/ppermute | solution.py:51
  804.4 3.2 copy-start.1
  809.2 48.3 %collective-permute-start.1 = (bf16[8,512,256]{2,1,0:T(8,128)(2,1)}, bf16[8,512,256]{2,1,0:T(8,128)(2,1)}, u32[]{:S(2)}, u32[]{:S(2)}) collective-permute-start(bf16[8,512,256]{2,1,0:T(8,128)(2,1)} %dynamic-slice_convert_fusion), channel_id=1, source_target_pairs={{0,16},{16,0},{1,17},{17,1},{2,18},{18,2},{3,19},{19,3},{4,20},{20... | collective-permute-start | bytes 6291464 | tf_op jit(solution)/shard_map/ppermute | solution.py:51
Sparse Core Ops, SparseCore 0:
  499.2 55.2 reduce-scatter.6
  620.8 100.2 reduce-scatter.4

commit v7 on v6

--- a/solution.py
+++ b/solution.py
@@ -107,8 +107,8 @@
     grad_block_two = lax.psum_scatter(grad_block_two, "dp", scatter_dimension=2, tiled=True)
 
     own = grad_first.shape[0] // n_seq
-    half = own // 2
-    halves = ((0, half), (half, own)) if half else ((0, own),)
+    cut = 3 * own // 4 if own % 4 == 0 else own // 2
+    halves = ((0, cut), (cut, own)) if cut else ((0, own),)
     grad_first_split = rows_send(grad_first)
     pieces = [grad_first_split[:, lo:hi] for lo, hi in halves]
     pieces, third_rows = held((pieces, third_rows))

time: 879 us -> 890 us (1.013)
    ppermute x2, waiting for transfers between devices: 14 us -> 40.3 us  [dp_reduce_scatter(): lax.ppermute(part.astype(jnp.bfloat16), 'dp', [(i, (i + shift) % n) for i...]
    all_to_all x3, waiting for transfers between devices: 175 us -> 149 us  [rows_recv(): moved = lax.all_to_all(x, 'seq', split_axis=0, concat_axis=0, tiled=True)]
  transfers between devices with their start and end apart: 9 -> 9, of which waited for: 6 -> 7; matrix products, arithmetic and copies ran while one was open for 36% -> 37% of each run, Pallas kernels for 0% -> 0%
where the time goes in v7:
time: 890 us; the launch traced here: 881 us
  waiting for transfers between devices  471 us (53%)
  matrix products  225 us (25%)
  local copies, waits for them, and re-layouts  95.7 us (11%)
  other arithmetic  43.3 us (5%)
  starting transfers between devices  31.1 us (3%)
  between operations  14.3 us (2%)
    all_to_all x2, waiting for transfers between devices, cols_recv(): lax.all_to_all(x, 'seq', split_axis=0, concat_axis=0, tiled=True)  281 us
    all_to_all x3, waiting for transfers between devices, rows_recv(): moved = lax.all_to_all(x, 'seq', split_axis=0, concat_axis=0, tiled=True)  149 us
    unnamed x10, local copies, waits for them, and re-layouts  45.2 us
    ppermute x2, waiting for transfers between devices, dp_reduce_scatter(): lax.ppermute(part.astype(jnp.bfloat16), 'dp', [(i, (i + shift) % n) for i...  40.3 us
    dot_general x1, matrix products, body(): jnp.einsum('fch,fcd->fhd', block_one, third_rows, preferred_element_type=...  25.5 us
    dot_general x1, matrix products, body(): jnp.einsum('fcd,ecd->cef', grad_third_cols, filtered, preferred_element_t...  22 us
    dot_general x1, matrix products, body(): jnp.einsum('ecd,acd->cea', grad_second, first_cols, preferred_element_typ...  21.6 us
    dot_general x2, matrix products, finish(): jnp.einsum('acd,abd->acb', grad_first_rows, tokens[lo:hi], preferred_elem...  21 us
  transfers between devices with their start and end apart: 9, of which 7 were waited for; matrix products, arithmetic and copies ran while one was open for 37% of the time, Pallas kernels for 0%

profile of v7, /device:TPU:10, one launch (start us, length us, event | category | flops | bytes accessed | tf_op | source)
XLA Modules:
  0.0 880.6 jit_solution(11661821989344883562)
XLA Ops:
  7.2 13.7 %fusion.22 = bf16[16,512,512]{2,1,0:T(8,128)(2,1)} fusion(bf16[16,512,512]{2,1,0:T(8,128)(2,1)} %param.10, bf16[1,16,512,512]{3,2,1,0:T(8,128)(2,1)} %param.6), kind=kOutput, calls=%fused_computation.35 | convolution fusion | flops 4299161600 | bytes 25165824 | tf_op jit(solution)/shard_map/acb,abd->acd/dot_general | solution.py:66
  20.9 8.4 copy.118
  29.3 6.2 all-to-all-start
  35.5 11.4 %fusion.3 = bf16[16,512,512]{2,1,0:T(8,128)(2,1)} fusion(bf16[1,16,512,512]{3,2,1,0:T(8,128)(2,1)} %param.9, bf16[1,16,512,512]{3,2,1,0:T(8,128)(2,1)} %param.7), kind=kLoop, calls=%fused_computation.8 | loop fusion | flops 29360128 | bytes 25165824 | tf_op jit(solution)/shard_map/convert_element_type | solution.py:73
  46.9 13.7 %convolution_convert_fusion.2 = bf16[16,512,512]{1,2,0:T(8,128)(2,1)} fusion(bf16[16,512,512]{2,1,0:T(8,128)(2,1)} %param.10, bf16[16,512,512]{2,1,0:T(8,128)(2,1)} %fusion.3), kind=kOutput, calls=%fused_computation.38 | convolution fusion | flops 4299161600 | bytes 25165824 | tf_op jit(solution)/shard_map/fch,fhd->fcd/dot_general | solution.py:74
  60.6 8.4 copy.119
  69.1 148.6 %all-to-all-done = bf16[16,16,32,512]{3,2,1,0:T(8,128)(2,1)} async-done(((bf16[16,16,32,512]{3,2,1,0:T(8,128)(2,1)}), bf16[16,16,32,512]{3,2,1,0:T(8,128)(2,1)}, u32[]{:S(2)}, u32[]{:S(2)}) %all-to-all-start) | async-done | bytes 8388640 | tf_op jit(solution)/shard_map/all_to_all | solution.py:19
  217.6 5.7 all-to-all-start.1
  223.3 13.7 %copy.54 = bf16[256,32,512]{0,2,1:T(8,128)(2,1)} copy(bf16[256,32,512]{2,1,0:T(8,128)(2,1)} %param.8) | data formatting | bytes 16777216 | tf_op args[2]
  237.0 20.4 %convolution_bitcast_fusion.1 = f32[256,32,512]{0,2,1:T(8,128)} fusion(bf16[32,256,256]{2,1,0:T(8,128)(2,1)} %param.11, bf16[256,32,512]{2,1,0:T(8,128)(2,1)} %bitcast.8), kind=kOutput, calls=%fused_computation.17 | convolution fusion | flops 2147483648 | bytes 29360128 | tf_op jit(solution)/shard_map/cea,acd->ecd/dot_general | solution.py:81
  257.4 14.9 %convolution_convert_fusion.1 = bf16[32,512,256]{1,2,0:T(8,128)(2,1)} fusion(bf16[32,256,256]{2,1,0:T(8,128)(2,1)} %param.11, f32[256,32,512]{0,2,1:T(8,128)} %convolution_bitcast_fusion.1, bf16[256,32,512]{0,2,1:T(8,128)(2,1)} %copy.54), kind=kOutput, calls=%fused_computation.37 | convolution fusion | flops 2164260864 | bytes 37748736 | tf_op jit(solution)/shard_map/cef,ecd->fcd/dot_general | solution.py:84
  272.3 132.9 %all-to-all-done.1 = bf16[16,16,32,512]{3,2,1,0:T(8,128)(2,1)} async-done(((bf16[16,16,32,512]{3,2,1,0:T(8,128)(2,1)}), bf16[16,16,32,512]{3,2,1,0:T(8,128)(2,1)}, u32[]{:S(2)}, u32[]{:S(2)}) %all-to-all-start.1) | async-done | bytes 8388640 | tf_op jit(solution)/shard_map/all_to_all | solution.py:19
  405.2 8.2 copy.65
  418.5 20.4 %convolution_bitcast_fusion = f32[256,32,512]{0,2,1:T(8,128)} fusion(bf16[32,256,256]{2,1,0:T(8,128)(2,1)} %param.11, bf16[256,32,512]{2,1,0:T(8,128)(2,1)} %bitcast.12), kind=kOutput, calls=%fused_computation.16 | convolution fusion | flops 2147483648 | bytes 29360128 | tf_op jit(solution)/shard_map/cef,fcd->ecd/dot_general | solution.py:91
  438.9 21.6 %fusion.10 = f32[32,256,256]{2,1,0:T(8,128)} fusion(bf16[256,32,512]{2,1,0:T(8,128)(2,1)} %bitcast.8, f32[256,32,512]{0,2,1:T(8,128)} %convolution_bitcast_fusion, bf16[256,32,512]{0,2,1:T(8,128)(2,1)} %copy.54), kind=kOutput, calls=%fused_computation.25 | convolution fusion | flops 2160066560 | bytes 41943040 | tf_op jit(solution)/shard_map/ecd,acd->cea/dot_general | solution.py:102
  460.5 22.0 %multiply_convert_fusion.1 = bf16[32,256,256]{2,1,0:T(8,128)(2,1)} fusion(f32[32,256,256]{2,1,0:T(8,128)} %fusion.10, bf16[256,32,512]{2,1,0:T(8,128)(2,1)} %bitcast.12, f32[256,32,512]{0,2,1:T(8,128)} %convolution_bitcast_fusion.1, bf16[256,32,512]{0,2,1:T(8,128)(2,1)} %copy.54), kind=kOutput, calls=%fused_computation.23 | convolution fusion | flops 2166358016 | bytes 46137344 | tf_op jit(solution)/shard_map/fcd,ecd->cef/dot_general | solution.py:101
  482.5 8.0 copy.86
  490.5 8.5 copy.92
  499.0 15.3 %multiply_convert_fusion = bf16[256,32,512]{0,2,1:T(8,128)(2,1)} fusion(f32[256,32,512]{0,2,1:T(8,128)} %convolution_bitcast_fusion, f32[256,32,512]{0,2,1:T(8,128)} %convolution_bitcast_fusion.1), kind=kLoop, calls=%fused_computation.13 | loop fusion | flops 8388608 | bytes 41943040 | tf_op jit(solution)/shard_map/convert_element_type | solution.py:98
  514.4 15.3 %convolution_convert_fusion = bf16[32,512,256]{1,2,0:T(8,128)(2,1)} fusion(bf16[32,256,256]{2,1,0:T(8,128)(2,1)} %param.11, f32[256,32,512]{0,2,1:T(8,128)} %convolution_bitcast_fusion, bf16[256,32,512]{0,2,1:T(8,128)(2,1)} %copy.54), kind=kOutput, calls=%fused_computation.36 | convolution fusion | flops 2164260864 | bytes 37748736 | tf_op jit(solution)/shard_map/cea,ecd->acd/dot_general | solution.py:94
  535.6 7.0 copy.88
  542.5 58.0 %all-to-all-done.2 = bf16[16,16,32,512]{3,1,2,0:T(8,128)(2,1)} async-done(((bf16[16,16,32,512]{3,1,2,0:T(8,128)(2,1)}), bf16[16,16,32,512]{3,1,2,0:T(8,128)(2,1)}, u32[]{:S(2)}, u32[]{:S(2)}) %all-to-all-start.2) | async-done | bytes 8388640 | tf_op jit(solution)/shard_map/all_to_all | solution.py:35
  600.5 5.6 all-to-all-start.3
  606.1 20.7 %fusion.15 = f32[16,512,512]{2,1,0:T(8,128)} fusion(bf16[16,512,512]{2,1,0:T(8,128)(2,1)} %fusion.3, bf16[16,512,512]{2,0,1:T(8,128)(2,1)} %bitcast.18), kind=kOutput, calls=%fused_computation.30 | convolution fusion | flops 4294967296 | bytes 33554432 | tf_op jit(solution)/shard_map/fhd,fcd->fch/dot_general | solution.py:122
  626.9 25.5 %fusion.6 = (bf16[16,512,512]{2,1,0:T(8,128)(2,1)}, bf16[16,512,512]{2,1,0:T(8,128)(2,1)}) fusion(bf16[1,16,512,512]{3,2,1,0:T(8,128)(2,1)} %param.9, bf16[1,16,512,512]{3,2,1,0:T(8,128)(2,1)} %param.7, bf16[16,512,512]{2,1,0:T(8,128)(2,1)} %param.10, bf16[16,512,512]{2,0,1:T(8,128)(2,1)} %bitcast.18), kind=kOutput, calls=%fused_computation.11 | convolution fusion | flops 4353687552 | bytes 50331648 | tf_op jit(solution)/shard_map/fch,fcd->fhd/dot_general | solution.py:116
  652.4 90.7 %all-to-all-done.3 = bf16[16,12,32,512]{3,2,1,0:T(8,128)(2,1)} async-done(((bf16[16,12,32,512]{3,2,1,0:T(8,128)(2,1)}), bf16[16,12,32,512]{3,2,1,0:T(8,128)(2,1)}, u32[]{:S(2)}, u32[]{:S(2)}) %all-to-all-start.3) | async-done | bytes 6291488 | tf_op jit(solution)/shard_map/all_to_all | solution.py:35
  743.1 6.6 copy.66
  755.1 16.2 %add_multiply_fusion = f32[12,512,512]{2,1,0:T(8,128)} fusion(f32[16,512,512]{2,1,0:T(8,128)} %fusion.15, bf16[12,512,512]{2,1,0:T(8,128)(2,1)} %bitcast.90, bf16[1,16,512,512]{3,2,1,0:T(8,128)(2,1)} %param.6), kind=kOutput, calls=%fused_computation.15 | convolution fusion | flops 3227516928 | bytes 37748736 | tf_op jit(solution)/shard_map/acd,abd->acb/dot_general | solution.py:132
  782.9 7.8 copy.78
  790.7 10.7 %convert_bitcast_fusion = bf16[12,512,512]{2,1,0:T(8,128)(2,1)} fusion(bf16[12,512,512]{2,1,0:T(8,128)(2,1)} %bitcast.91, bf16[16,512,512]{2,1,0:T(8,128)(2,1)} %param.10), kind=kOutput, calls=%fused_computation.44 | convolution fusion | flops 3224371200 | bytes 18874368 | tf_op jit(solution)/shard_map/acb,acd->abd/dot_general | solution.py:128
  811.6 35.7 %collective-permute-done = bf16[12,512,256]{2,1,0:T(8,128)(2,1)} collective-permute-done((bf16[12,512,256]{2,1,0:T(8,128)(2,1)}, bf16[12,512,256]{2,1,0:T(8,128)(2,1)}, u32[]{:S(2)}, u32[]{:S(2)}) %collective-permute-start) | collective-permute-done | bytes 3145760 | tf_op jit(solution)/shard_map/ppermute | solution.py:51
  856.9 7.5 maximum_bitcast_fusion
  (27 shorter events, 56.8 us)
Async XLA Ops:
  29.3 188.3 %all-to-all-start = ((bf16[16,16,32,512]{3,2,1,0:T(8,128)(2,1)}), bf16[16,16,32,512]{3,2,1,0:T(8,128)(2,1)}, u32[]{:S(2)}, u32[]{:S(2)}) async-start(bf16[16,16,32,512]{3,2,1,0:T(8,128)(2,1)} %bitcast.88), calls=%async_computation | async-start | bytes 16777216 | tf_op jit(solution)/shard_map/all_to_all | solution.py:19
  217.6 187.6 %all-to-all-start.1 = ((bf16[16,16,32,512]{3,2,1,0:T(8,128)(2,1)}), bf16[16,16,32,512]{3,2,1,0:T(8,128)(2,1)}, u32[]{:S(2)}, u32[]{:S(2)}) async-start(bf16[16,16,32,512]{3,2,1,0:T(8,128)(2,1)} %bitcast.87), calls=%async_computation.1 | async-start | bytes 16777216 | tf_op jit(solution)/shard_map/all_to_all | solution.py:19
  413.4 187.1 %all-to-all-start.2 = ((bf16[16,16,32,512]{3,1,2,0:T(8,128)(2,1)}), bf16[16,16,32,512]{3,1,2,0:T(8,128)(2,1)}, u32[]{:S(2)}, u32[]{:S(2)}) async-start(bf16[16,16,32,512]{3,1,2,0:T(8,128)(2,1)} %copy.65), calls=%async_computation.2 | async-start | bytes 16777216 | tf_op jit(solution)/shard_map/all_to_all | solution.py:35
  418.5 359.2 %reduce-scatter.7.cloned.1.call-start = ((), (), s32[]{:S(2)}) async-start(), calls=%async_computation.8 | async-start | bytes 6291456
  499.0 283.9 %reduce-scatter.5.cloned.1.call-start = ((), (), s32[]{:S(2)}) async-start(), calls=%async_computation.7 | async-start | bytes 12582912 | tf_op jit(solution)/shard_map/reduce_scatter | solution.py:106
  529.7 5.9 copy-start
  600.5 142.6 %all-to-all-start.3 = ((bf16[16,12,32,512]{3,2,1,0:T(8,128)(2,1)}), bf16[16,12,32,512]{3,2,1,0:T(8,128)(2,1)}, u32[]{:S(2)}, u32[]{:S(2)}) async-start(bf16[16,12,32,512]{3,2,1,0:T(8,128)(2,1)} %copy.88), calls=%async_computation.3 | async-start | bytes 12582912 | tf_op jit(solution)/shard_map/all_to_all | solution.py:35
  749.7 52.4 %all-to-all-start.4 = ((bf16[16,4,32,512]{3,1,2,0:T(4,128)(2,1)}), bf16[16,4,32,512]{3,1,2,0:T(4,128)(2,1)}, u32[]{:S(2)}, u32[]{:S(2)}) async-start(bf16[16,4,32,512]{3,1,2,0:T(4,128)(2,1)} %copy.89), calls=%async_computation.4 | async-start | bytes 4194304 | tf_op jit(solution)/shard_map/all_to_all | solution.py:35
  776.1 71.3 %collective-permute-start = (bf16[12,512,256]{2,1,0:T(8,128)(2,1)}, bf16[12,512,256]{2,1,0:T(8,128)(2,1)}, u32[]{:S(2)}, u32[]{:S(2)}) collective-permute-start(bf16[12,512,256]{2,1,0:T(8,128)(2,1)} %dynamic-slice_convert_fusion), channel_id=1, source_target_pairs={{0,16},{16,0},{1,17},{17,1},{2,18},{18,2},{3,19},{19,3},{4,20},{20... | collective-permute-start | bytes 9437192 | tf_op jit(solution)/shard_map/ppermute | solution.py:51
  807.0 2.0 copy-start.1
  810.1 58.9 %collective-permute-start.1 = (bf16[4,512,256]{2,1,0:T(8,128)(2,1)}, bf16[4,512,256]{2,1,0:T(8,128)(2,1)}, u32[]{:S(2)}, u32[]{:S(2)}) collective-permute-start(bf16[4,512,256]{2,1,0:T(8,128)(2,1)} %dynamic-slice_convert_fusion.1), channel_id=1, source_target_pairs={{0,16},{16,0},{1,17},{17,1},{2,18},{18,2},{3,19},{19,3},{4,20},{20... | collective-permute-start | bytes 3145736 | tf_op jit(solution)/shard_map/ppermute | solution.py:51
Sparse Core Ops, SparseCore 0:
  499.1 55.2 reduce-scatter.6
  556.7 99.2 reduce-scatter.4

commit v8 on v6

--- a/solution.py
+++ b/solution.py
@@ -30,10 +30,13 @@
     return x.reshape((n, x.shape[0] // n) + x.shape[1:])
 
 
-def rows_recv(x):
+def rows_move(x):
+    return lax.all_to_all(x, "seq", split_axis=0, concat_axis=0, tiled=True)
+
+
+def rows_order(x):
     n, f, c, d = x.shape
-    moved = lax.all_to_all(x, "seq", split_axis=0, concat_axis=0, tiled=True)
-    return moved.transpose(1, 0, 2, 3).reshape(f, n * c, d)
+    return x.transpose(1, 0, 2, 3).reshape(f, n * c, d)
 
 
 def held(x):
@@ -84,8 +87,8 @@
     third = jnp.einsum(
         "cef,ecd->fcd", block_two, filtered, preferred_element_type=f32
     ).astype(jnp.bfloat16)
-    third_send, grad_third_cols = held((rows_send(third), grad_third_cols))
-    third_rows = rows_recv(third_send)
+    third_send, grad_third_cols = held((natural(rows_send(third)), grad_third_cols))
+    third_arrived = rows_move(third_send)
 
     grad_filtered = held(
         jnp.einsum("cef,fcd->ecd", block_two, grad_third_cols, preferred_element_type=f32)
@@ -111,7 +114,8 @@
     halves = ((0, half), (half, own)) if half else ((0, own),)
     grad_first_split = rows_send(grad_first)
     pieces = [grad_first_split[:, lo:hi] for lo, hi in halves]
-    pieces, third_rows = held((pieces, third_rows))
+    pieces, third_arrived = held((pieces, third_arrived))
+    third_rows = rows_order(third_arrived)
 
     fourth = jnp.einsum(
         "fch,fcd->fhd", block_one, third_rows, preferred_element_type=f32
@@ -142,14 +146,14 @@
             piece, arrived, (output, grad_gate, outer_one) = held(
                 (piece, pending[2], (output, grad_gate, outer_one))
             )
-            done = finish(pending[0], pending[1], arrived)
+            done = finish(pending[0], pending[1], rows_order(arrived))
             grad_tokens_parts.append(done[0])
             grad_block_ones.append(done[1])
-        pending = (lo, hi, rows_recv(piece))
+        pending = (lo, hi, rows_move(piece))
     arrived, grad_tokens_parts, output, grad_gate = held(
         (pending[2], grad_tokens_parts, output, grad_gate)
     )
-    done = finish(pending[0], pending[1], arrived)
+    done = finish(pending[0], pending[1], rows_order(arrived))
     grad_tokens_parts.append(done[0])
     grad_block_ones.append(done[1])
     grad_tokens = jnp.concatenate(grad_tokens_parts, axis=0)

time: 879 us -> 871 us (level)
  waiting for transfers between devices: 471 us -> 456 us
  local copies, waits for them, and re-layouts: 87.6 us -> 99.3 us
    all_to_all x2, waiting for transfers between devices: 281 us -> 270 us  [cols_recv(): lax.all_to_all(x, 'seq', split_axis=0, concat_axis=0, tiled=True)]
    convert_element_type x0 -> x1, local copies, waits for them, and re-layouts: none -> 11.5 us  [body(): third = jnp.einsum('cef,ecd->fcd', block_two, filtered, preferred_element...]
  transfers between devices with their start and end apart: 9 -> 9, of which waited for: 6 -> 6; matrix products, arithmetic and copies ran while one was open for 36% -> 38% of each run, Pallas kernels for 0% -> 0%
where the time goes in v8:
time: 871 us; the launch traced here: 862 us
  waiting for transfers between devices  456 us (52%)
  matrix products  218 us (25%)
  local copies, waits for them, and re-layouts  99.3 us (11%)
  other arithmetic  43.1 us (5%)
  starting transfers between devices  30.4 us (3%)
  between operations  14.6 us (2%)
    all_to_all x2, waiting for transfers between devices, cols_recv(): lax.all_to_all(x, 'seq', split_axis=0, concat_axis=0, tiled=True)  270 us
    all_to_all x3, waiting for transfers between devices, rows_move(): return lax.all_to_all(x, 'seq', split_axis=0, concat_axis=0, tiled=True)  172 us
    unnamed x10, local copies, waits for them, and re-layouts  50.2 us
    dot_general x1, matrix products, body(): jnp.einsum('fch,fcd->fhd', block_one, third_rows, preferred_element_type=...  24.5 us
    dot_general x1, matrix products, body(): jnp.einsum('fcd,ecd->cef', grad_third_cols, filtered, preferred_element_t...  22 us
    dot_general x1, matrix products, body(): jnp.einsum('ecd,acd->cea', grad_second, first_cols, preferred_element_typ...  21.4 us
    dot_general x1, matrix products, body(): jnp.einsum('cea,acd->ecd', block_two, first_cols, preferred_element_type=...  20.4 us
    dot_general x1, matrix products, body(): jnp.einsum('cef,fcd->ecd', block_two, grad_third_cols, preferred_element_...  20.4 us
  transfers between devices with their start and end apart: 9, of which 6 were waited for; matrix products, arithmetic and copies ran while one was open for 38% of the time, Pallas kernels for 0%

profile of v8, /device:TPU:10, one launch (start us, length us, event | category | flops | bytes accessed | tf_op | source)
XLA Modules:
  0.0 862.0 jit_solution(10295003681780315098)
XLA Ops:
  7.2 13.7 %fusion.15 = bf16[16,512,512]{2,1,0:T(8,128)(2,1)} fusion(bf16[16,512,512]{2,1,0:T(8,128)(2,1)} %param.10, bf16[1,16,512,512]{3,2,1,0:T(8,128)(2,1)} %param.6), kind=kOutput, calls=%fused_computation.32 | convolution fusion | flops 4299161600 | bytes 25165824 | tf_op jit(solution)/shard_map/acb,abd->acd/dot_general | solution.py:69
  20.9 8.4 copy.117
  29.3 6.2 all-to-all-start
  35.5 11.4 %fusion.3 = bf16[16,512,512]{2,1,0:T(8,128)(2,1)} fusion(bf16[1,16,512,512]{3,2,1,0:T(8,128)(2,1)} %param.9, bf16[1,16,512,512]{3,2,1,0:T(8,128)(2,1)} %param.7), kind=kLoop, calls=%fused_computation.8 | loop fusion | flops 29360128 | bytes 25165824 | tf_op jit(solution)/shard_map/convert_element_type | solution.py:76
  46.9 13.7 %convolution_convert_fusion.1 = bf16[16,512,512]{1,2,0:T(8,128)(2,1)} fusion(bf16[16,512,512]{2,1,0:T(8,128)(2,1)} %param.10, bf16[16,512,512]{2,1,0:T(8,128)(2,1)} %fusion.3), kind=kOutput, calls=%fused_computation.34 | convolution fusion | flops 4299161600 | bytes 25165824 | tf_op jit(solution)/shard_map/fch,fhd->fcd/dot_general | solution.py:77
  60.6 8.3 copy.118
  68.9 148.7 %all-to-all-done = bf16[16,16,32,512]{3,2,1,0:T(8,128)(2,1)} async-done(((bf16[16,16,32,512]{3,2,1,0:T(8,128)(2,1)}), bf16[16,16,32,512]{3,2,1,0:T(8,128)(2,1)}, u32[]{:S(2)}, u32[]{:S(2)}) %all-to-all-start) | async-done | bytes 8388640 | tf_op jit(solution)/shard_map/all_to_all | solution.py:19
  223.0 13.7 %copy.49 = bf16[256,32,512]{0,2,1:T(8,128)(2,1)} copy(bf16[256,32,512]{2,1,0:T(8,128)(2,1)} %param.8) | data formatting | bytes 16777216 | tf_op args[2]
  236.7 20.4 %convolution_bitcast_fusion.1 = f32[256,32,512]{0,2,1:T(8,128)} fusion(bf16[32,256,256]{2,1,0:T(8,128)(2,1)} %param.11, bf16[256,32,512]{2,1,0:T(8,128)(2,1)} %bitcast.8), kind=kOutput, calls=%fused_computation.16 | convolution fusion | flops 2147483648 | bytes 29360128 | tf_op jit(solution)/shard_map/cea,acd->ecd/dot_general | solution.py:84
  257.1 15.1 %convert_bitcast_fusion = bf16[256,32,512]{2,0,1:T(8,128)(2,1)} fusion(bf16[32,256,256]{2,1,0:T(8,128)(2,1)} %param.11, f32[256,32,512]{0,2,1:T(8,128)} %convolution_bitcast_fusion.1, bf16[256,32,512]{0,2,1:T(8,128)(2,1)} %copy.49), kind=kOutput, calls=%fused_computation.25 | convolution fusion | flops 2164260864 | bytes 37748736 | tf_op jit(solution)/shard_map/cef,ecd->fcd/dot_general | solution.py:87
  272.3 11.5 %copy.55 = bf16[256,32,512]{2,1,0:T(8,128)(2,1)} copy(bf16[256,32,512]{2,0,1:T(8,128)(2,1)} %convert_bitcast_fusion) | data formatting | bytes 16777216 | tf_op jit(solution)/shard_map/convert_element_type | solution.py:89
  283.8 121.2 %all-to-all-done.1 = bf16[16,16,32,512]{3,2,1,0:T(8,128)(2,1)} async-done(((bf16[16,16,32,512]{3,2,1,0:T(8,128)(2,1)}), bf16[16,16,32,512]{3,2,1,0:T(8,128)(2,1)}, u32[]{:S(2)}, u32[]{:S(2)}) %all-to-all-start.1) | async-done | bytes 8388640 | tf_op jit(solution)/shard_map/all_to_all | solution.py:19
  410.2 20.4 %convolution_bitcast_fusion = f32[256,32,512]{0,2,1:T(8,128)} fusion(bf16[32,256,256]{2,1,0:T(8,128)(2,1)} %param.11, bf16[256,32,512]{2,1,0:T(8,128)(2,1)} %bitcast.12), kind=kOutput, calls=%fused_computation.15 | convolution fusion | flops 2147483648 | bytes 29360128 | tf_op jit(solution)/shard_map/cef,fcd->ecd/dot_general | solution.py:94
  430.6 21.4 %fusion.10 = f32[32,256,256]{2,1,0:T(8,128)} fusion(bf16[256,32,512]{2,1,0:T(8,128)(2,1)} %bitcast.8, f32[256,32,512]{0,2,1:T(8,128)} %convolution_bitcast_fusion, bf16[256,32,512]{0,2,1:T(8,128)(2,1)} %copy.49), kind=kOutput, calls=%fused_computation.27 | convolution fusion | flops 2160066560 | bytes 41943040 | tf_op jit(solution)/shard_map/ecd,acd->cea/dot_general | solution.py:105
  452.0 22.0 %multiply_convert_fusion.1 = bf16[32,256,256]{2,1,0:T(8,128)(2,1)} fusion(f32[32,256,256]{2,1,0:T(8,128)} %fusion.10, bf16[256,32,512]{2,1,0:T(8,128)(2,1)} %bitcast.12, f32[256,32,512]{0,2,1:T(8,128)} %convolution_bitcast_fusion.1, bf16[256,32,512]{0,2,1:T(8,128)(2,1)} %copy.49), kind=kOutput, calls=%fused_computation.22 | convolution fusion | flops 2166358016 | bytes 46137344 | tf_op jit(solution)/shard_map/fcd,ecd->cef/dot_general | solution.py:104
  474.0 8.2 copy.81
  482.2 8.4 copy.87
  490.7 15.4 %convolution_convert_fusion = bf16[32,512,256]{1,2,0:T(8,128)(2,1)} fusion(bf16[32,256,256]{2,1,0:T(8,128)(2,1)} %param.11, f32[256,32,512]{0,2,1:T(8,128)} %convolution_bitcast_fusion, bf16[256,32,512]{0,2,1:T(8,128)(2,1)} %copy.49), kind=kOutput, calls=%fused_computation.33 | convolution fusion | flops 2164260864 | bytes 37748736 | tf_op jit(solution)/shard_map/cea,ecd->acd/dot_general | solution.py:97
  515.2 76.9 %all-to-all-done.2 = bf16[16,16,32,512]{3,2,1,0:T(8,128)(2,1)} async-done(((bf16[16,16,32,512]{3,2,1,0:T(8,128)(2,1)}), bf16[16,16,32,512]{3,2,1,0:T(8,128)(2,1)}, u32[]{:S(2)}, u32[]{:S(2)}) %all-to-all-start.2) | async-done | bytes 8388640 | tf_op jit(solution)/shard_map/all_to_all | solution.py:34
  597.2 15.1 %multiply_convert_fusion = bf16[256,32,512]{0,2,1:T(8,128)(2,1)} fusion(f32[256,32,512]{0,2,1:T(8,128)} %convolution_bitcast_fusion, f32[256,32,512]{0,2,1:T(8,128)} %convolution_bitcast_fusion.1), kind=kLoop, calls=%fused_computation.13 | loop fusion | flops 8388608 | bytes 41943040 | tf_op jit(solution)/shard_map/convert_element_type | solution.py:101
  612.3 8.5 copy.61
  620.8 16.1 %fusion.55 = f32[16,512,512]{2,1,0:T(8,128)} fusion(bf16[16,512,512]{2,1,0:T(8,128)(2,1)} %bitcast.85, bf16[16,512,512]{2,1,0:T(8,128)(2,1)} %fusion.3), kind=kOutput, calls=%fused_computation.58 | convolution fusion | flops 4294967296 | bytes 33554432 | tf_op jit(solution)/shard_map/fhd,fcd->fch/dot_general | solution.py:126
  636.9 24.5 %fusion.6 = (bf16[16,512,512]{2,1,0:T(8,128)(2,1)}, bf16[16,512,512]{2,1,0:T(8,128)(2,1)}) fusion(bf16[1,16,512,512]{3,2,1,0:T(8,128)(2,1)} %param.9, bf16[1,16,512,512]{3,2,1,0:T(8,128)(2,1)} %param.7, bf16[16,512,512]{2,1,0:T(8,128)(2,1)} %bitcast.86, bf16[16,512,512]{2,1,0:T(8,128)(2,1)} %param.10), kind=kOutput, calls=%fused_computation.11 | convolution fusion | flops 4353687552 | bytes 50331648 | tf_op jit(solution)/shard_map/fch,fcd->fhd/dot_general | solution.py:120
  661.4 27.9 %all-to-all-done.3 = bf16[16,8,32,512]{3,1,2,0:T(8,128)(2,1)} async-done(((bf16[16,8,32,512]{3,1,2,0:T(8,128)(2,1)}), bf16[16,8,32,512]{3,1,2,0:T(8,128)(2,1)}, u32[]{:S(2)}, u32[]{:S(2)}) %all-to-all-start.3) | async-done | bytes 4194336 | tf_op jit(solution)/shard_map/all_to_all | solution.py:34
  694.7 9.3 %add_multiply_fusion.1 = f32[8,512,512]{2,1,0:T(8,128)S(1)} fusion(f32[16,512,512]{2,1,0:T(8,128)} %fusion.55, bf16[1,16,512,512]{3,2,1,0:T(8,128)(2,1)} %param.6, bf16[8,512,512]{2,0,1:T(8,128)(2,1)} %bitcast.22), kind=kOutput, calls=%fused_computation.24 | convolution fusion | flops 2151677952 | bytes 25165824 | tf_op jit(solution)/shard_map/acd,abd->acb/dot_general | solution.py:136
  710.5 8.6 convert_bitcast_fusion.2
  719.1 67.7 %all-to-all-done.4 = bf16[16,8,32,512]{3,1,2,0:T(8,128)(2,1)} async-done(((bf16[16,8,32,512]{3,1,2,0:T(8,128)(2,1)}), bf16[16,8,32,512]{3,1,2,0:T(8,128)(2,1)}, u32[]{:S(2)}, u32[]{:S(2)}) %all-to-all-start.4) | async-done | bytes 4194336 | tf_op jit(solution)/shard_map/all_to_all | solution.py:34
  786.8 9.2 %add_multiply_fusion = f32[8,512,512]{2,1,0:T(8,128)S(1)} fusion(f32[16,512,512]{2,1,0:T(8,128)} %fusion.55, bf16[1,16,512,512]{3,2,1,0:T(8,128)(2,1)} %param.6, bf16[8,512,512]{2,0,1:T(8,128)(2,1)} %bitcast.26), kind=kOutput, calls=%fused_computation.23 | convolution fusion | flops 2151677952 | bytes 25165824 | tf_op jit(solution)/shard_map/acd,abd->acb/dot_general | solution.py:136
  807.5 8.1 copy.73
  818.9 8.5 convert_bitcast_fusion.1
  827.4 7.6 maximum_bitcast_fusion
  835.0 14.0 %collective-permute-done.1 = bf16[8,512,256]{2,1,0:T(8,128)(2,1)} collective-permute-done((bf16[8,512,256]{2,1,0:T(8,128)(2,1)}, bf16[8,512,256]{2,1,0:T(8,128)(2,1)}, u32[]{:S(2)}, u32[]{:S(2)}) %collective-permute-start.1) | collective-permute-done | bytes 2097184 | tf_op jit(solution)/shard_map/ppermute | solution.py:54
  (27 shorter events, 57.4 us)
Async XLA Ops:
  29.3 188.3 %all-to-all-start = ((bf16[16,16,32,512]{3,2,1,0:T(8,128)(2,1)}), bf16[16,16,32,512]{3,2,1,0:T(8,128)(2,1)}, u32[]{:S(2)}, u32[]{:S(2)}) async-start(bf16[16,16,32,512]{3,2,1,0:T(8,128)(2,1)} %bitcast.89), calls=%async_computation | async-start | bytes 16777216 | tf_op jit(solution)/shard_map/all_to_all | solution.py:19
  217.6 187.3 %all-to-all-start.1 = ((bf16[16,16,32,512]{3,2,1,0:T(8,128)(2,1)}), bf16[16,16,32,512]{3,2,1,0:T(8,128)(2,1)}, u32[]{:S(2)}, u32[]{:S(2)}) async-start(bf16[16,16,32,512]{3,2,1,0:T(8,128)(2,1)} %bitcast.88), calls=%async_computation.1 | async-start | bytes 16777216 | tf_op jit(solution)/shard_map/all_to_all | solution.py:19
  405.0 187.1 %all-to-all-start.2 = ((bf16[16,16,32,512]{3,2,1,0:T(8,128)(2,1)}), bf16[16,16,32,512]{3,2,1,0:T(8,128)(2,1)}, u32[]{:S(2)}, u32[]{:S(2)}) async-start(bf16[16,16,32,512]{3,2,1,0:T(8,128)(2,1)} %bitcast.87), calls=%async_computation.2 | async-start | bytes 16777216 | tf_op jit(solution)/shard_map/all_to_all | solution.py:34
  410.0 392.3 %reduce-scatter.7.cloned.1.call-start = ((), (), s32[]{:S(2)}) async-start(), calls=%async_computation.8 | async-start | bytes 6291456
  592.1 97.2 %all-to-all-start.3 = ((bf16[16,8,32,512]{3,1,2,0:T(8,128)(2,1)}), bf16[16,8,32,512]{3,1,2,0:T(8,128)(2,1)}, u32[]{:S(2)}, u32[]{:S(2)}) async-start(bf16[16,8,32,512]{3,1,2,0:T(8,128)(2,1)} %copy.83), calls=%async_computation.3 | async-start | bytes 8388608 | tf_op jit(solution)/shard_map/all_to_all | solution.py:34
  597.1 210.4 %reduce-scatter.5.cloned.1.call-start = ((), (), s32[]{:S(2)}) async-start(), calls=%async_computation.7 | async-start | bytes 12582912 | tf_op jit(solution)/shard_map/reduce_scatter | solution.py:109
  689.3 97.5 %all-to-all-start.4 = ((bf16[16,8,32,512]{3,1,2,0:T(8,128)(2,1)}), bf16[16,8,32,512]{3,1,2,0:T(8,128)(2,1)}, u32[]{:S(2)}, u32[]{:S(2)}) async-start(bf16[16,8,32,512]{3,1,2,0:T(8,128)(2,1)} %copy.84), calls=%async_computation.4 | async-start | bytes 8388608 | tf_op jit(solution)/shard_map/all_to_all | solution.py:34
  704.0 3.4 copy-start
  709.0 106.5 %collective-permute-start = (bf16[8,512,256]{2,1,0:T(8,128)(2,1)}, bf16[8,512,256]{2,1,0:T(8,128)(2,1)}, u32[]{:S(2)}, u32[]{:S(2)}) collective-permute-start(bf16[8,512,256]{2,1,0:T(8,128)(2,1)} %dynamic-slice_convert_fusion.1), channel_id=1, source_target_pairs={{0,16},{16,0},{1,17},{17,1},{2,18},{18,2},{3,19},{19,3},{4,20},{20... | collective-permute-start | bytes 6291464 | tf_op jit(solution)/shard_map/ppermute | solution.py:54
  795.9 3.2 copy-start.1
  800.7 48.3 %collective-permute-start.1 = (bf16[8,512,256]{2,1,0:T(8,128)(2,1)}, bf16[8,512,256]{2,1,0:T(8,128)(2,1)}, u32[]{:S(2)}, u32[]{:S(2)}) collective-permute-start(bf16[8,512,256]{2,1,0:T(8,128)(2,1)} %dynamic-slice_convert_fusion), channel_id=1, source_target_pairs={{0,16},{16,0},{1,17},{17,1},{2,18},{18,2},{3,19},{19,3},{4,20},{20... | collective-permute-start | bytes 6291464 | tf_op jit(solution)/shard_map/ppermute | solution.py:54
Sparse Core Ops, SparseCore 0:
  490.8 55.2 reduce-scatter.6
  612.4 100.2 reduce-scatter.4

commit v9 on v8

--- a/solution.py
+++ b/solution.py
@@ -110,8 +110,8 @@
     grad_block_two = lax.psum_scatter(grad_block_two, "dp", scatter_dimension=2, tiled=True)
 
     own = grad_first.shape[0] // n_seq
-    half = own // 2
-    halves = ((0, half), (half, own)) if half else ((0, own),)
+    cut = 3 * own // 4 if own % 4 == 0 else own // 2
+    halves = ((0, cut), (cut, own)) if cut else ((0, own),)
     grad_first_split = rows_send(grad_first)
     pieces = [grad_first_split[:, lo:hi] for lo, hi in halves]
     pieces, third_arrived = held((pieces, third_arrived))

time: 871 us -> 882 us (1.013)
    ppermute x2, waiting for transfers between devices: 14 us -> 41.9 us  [dp_reduce_scatter(): lax.ppermute(part.astype(jnp.bfloat16), 'dp', [(i, (i + shift) % n) for i...]
    all_to_all x3, waiting for transfers between devices: 172 us -> 145 us  [rows_move(): return lax.all_to_all(x, 'seq', split_axis=0, concat_axis=0, tiled=True)]
    optimization_barrier x2 -> x3, local copies, waits for them, and re-layouts: 4.94 us -> 15.8 us  [held(): return lax.optimization_barrier(x)]
  transfers between devices with their start and end apart: 9 -> 9, of which waited for: 6 -> 6; matrix products, arithmetic and copies ran while one was open for 38% -> 39% of each run, Pallas kernels for 0% -> 0%
where the time goes in v9:
time: 882 us; the launch traced here: 872 us
  waiting for transfers between devices  458 us (52%)
  matrix products  219 us (25%)
  local copies, waits for them, and re-layouts  107 us (12%)
  other arithmetic  43.3 us (5%)
  starting transfers between devices  30.3 us (3%)
  between operations  14.3 us (2%)
    all_to_all x2, waiting for transfers between devices, cols_recv(): lax.all_to_all(x, 'seq', split_axis=0, concat_axis=0, tiled=True)  270 us
    all_to_all x3, waiting for transfers between devices, rows_move(): return lax.all_to_all(x, 'seq', split_axis=0, concat_axis=0, tiled=True)  145 us
    unnamed x10, local copies, waits for them, and re-layouts  45.4 us
    ppermute x2, waiting for transfers between devices, dp_reduce_scatter(): lax.ppermute(part.astype(jnp.bfloat16), 'dp', [(i, (i + shift) % n) for i...  41.9 us
    dot_general x1, matrix products, body(): jnp.einsum('fch,fcd->fhd', block_one, third_rows, preferred_element_type=...  24.4 us
    dot_general x1, matrix products, body(): jnp.einsum('fcd,ecd->cef', grad_third_cols, filtered, preferred_element_t...  22 us
    dot_general x1, matrix products, body(): jnp.einsum('ecd,acd->cea', grad_second, first_cols, preferred_element_typ...  21.6 us
    dot_general x2, matrix products, finish(): jnp.einsum('acd,abd->acb', grad_first_rows, tokens[lo:hi], preferred_elem...  21 us
  transfers between devices with their start and end apart: 9, of which 6 were waited for; matrix products, arithmetic and copies ran while one was open for 39% of the time, Pallas kernels for 0%

profile of v9, /device:TPU:10, one launch (start us, length us, event | category | flops | bytes accessed | tf_op | source)
XLA Modules:
  0.0 872.4 jit_solution(10738444954337249461)
XLA Ops:
  7.2 13.7 %fusion.15 = bf16[16,512,512]{2,1,0:T(8,128)(2,1)} fusion(bf16[16,512,512]{2,1,0:T(8,128)(2,1)} %param.10, bf16[1,16,512,512]{3,2,1,0:T(8,128)(2,1)} %param.6), kind=kOutput, calls=%fused_computation.31 | convolution fusion | flops 4299161600 | bytes 25165824 | tf_op jit(solution)/shard_map/acb,abd->acd/dot_general | solution.py:69
  20.9 8.4 copy.127
  29.3 6.2 all-to-all-start
  35.5 11.4 %fusion.3 = bf16[16,512,512]{2,1,0:T(8,128)(2,1)} fusion(bf16[1,16,512,512]{3,2,1,0:T(8,128)(2,1)} %param.9, bf16[1,16,512,512]{3,2,1,0:T(8,128)(2,1)} %param.7), kind=kLoop, calls=%fused_computation.8 | loop fusion | flops 29360128 | bytes 25165824 | tf_op jit(solution)/shard_map/convert_element_type | solution.py:76
  46.9 13.7 %convolution_convert_fusion.1 = bf16[16,512,512]{1,2,0:T(8,128)(2,1)} fusion(bf16[16,512,512]{2,1,0:T(8,128)(2,1)} %param.10, bf16[16,512,512]{2,1,0:T(8,128)(2,1)} %fusion.3), kind=kOutput, calls=%fused_computation.33 | convolution fusion | flops 4299161600 | bytes 25165824 | tf_op jit(solution)/shard_map/fch,fhd->fcd/dot_general | solution.py:77
  60.6 8.3 copy.128
  68.9 148.7 %all-to-all-done = bf16[16,16,32,512]{3,2,1,0:T(8,128)(2,1)} async-done(((bf16[16,16,32,512]{3,2,1,0:T(8,128)(2,1)}), bf16[16,16,32,512]{3,2,1,0:T(8,128)(2,1)}, u32[]{:S(2)}, u32[]{:S(2)}) %all-to-all-start) | async-done | bytes 8388640 | tf_op jit(solution)/shard_map/all_to_all | solution.py:19
  217.6 5.7 all-to-all-start.1
  223.3 13.7 %copy.72 = bf16[256,32,512]{0,2,1:T(8,128)(2,1)} copy(bf16[256,32,512]{2,1,0:T(8,128)(2,1)} %param.8) | data formatting | bytes 16777216 | tf_op args[2]
  237.1 20.4 %convolution_bitcast_fusion.1 = f32[256,32,512]{0,2,1:T(8,128)} fusion(bf16[32,256,256]{2,1,0:T(8,128)(2,1)} %param.11, bf16[256,32,512]{2,1,0:T(8,128)(2,1)} %bitcast.8), kind=kOutput, calls=%fused_computation.17 | convolution fusion | flops 2147483648 | bytes 29360128 | tf_op jit(solution)/shard_map/cea,acd->ecd/dot_general | solution.py:84
  257.4 14.9 %convert_bitcast_fusion = bf16[256,32,512]{2,0,1:T(8,128)(2,1)} fusion(bf16[32,256,256]{2,1,0:T(8,128)(2,1)} %param.11, f32[256,32,512]{0,2,1:T(8,128)} %convolution_bitcast_fusion.1, bf16[256,32,512]{0,2,1:T(8,128)(2,1)} %copy.72), kind=kOutput, calls=%fused_computation.24 | convolution fusion | flops 2164260864 | bytes 37748736 | tf_op jit(solution)/shard_map/cef,ecd->fcd/dot_general | solution.py:87
  272.3 11.5 %copy.78 = bf16[256,32,512]{2,1,0:T(8,128)(2,1)} copy(bf16[256,32,512]{2,0,1:T(8,128)(2,1)} %convert_bitcast_fusion) | data formatting | bytes 16777216 | tf_op jit(solution)/shard_map/convert_element_type | solution.py:89
  283.9 121.4 %all-to-all-done.1 = bf16[16,16,32,512]{3,2,1,0:T(8,128)(2,1)} async-done(((bf16[16,16,32,512]{3,2,1,0:T(8,128)(2,1)}), bf16[16,16,32,512]{3,2,1,0:T(8,128)(2,1)}, u32[]{:S(2)}, u32[]{:S(2)}) %all-to-all-start.1) | async-done | bytes 8388640 | tf_op jit(solution)/shard_map/all_to_all | solution.py:19
  410.6 20.4 %convolution_bitcast_fusion = f32[256,32,512]{0,2,1:T(8,128)} fusion(bf16[32,256,256]{2,1,0:T(8,128)(2,1)} %param.11, bf16[256,32,512]{2,1,0:T(8,128)(2,1)} %bitcast.12), kind=kOutput, calls=%fused_computation.16 | convolution fusion | flops 2147483648 | bytes 29360128 | tf_op jit(solution)/shard_map/cef,fcd->ecd/dot_general | solution.py:94
  430.9 21.6 %fusion.10 = f32[32,256,256]{2,1,0:T(8,128)} fusion(bf16[256,32,512]{2,1,0:T(8,128)(2,1)} %bitcast.8, f32[256,32,512]{0,2,1:T(8,128)} %convolution_bitcast_fusion, bf16[256,32,512]{0,2,1:T(8,128)(2,1)} %copy.72), kind=kOutput, calls=%fused_computation.26 | convolution fusion | flops 2160066560 | bytes 41943040 | tf_op jit(solution)/shard_map/ecd,acd->cea/dot_general | solution.py:105
  452.5 22.0 %multiply_convert_fusion.1 = bf16[32,256,256]{2,1,0:T(8,128)(2,1)} fusion(f32[32,256,256]{2,1,0:T(8,128)} %fusion.10, bf16[256,32,512]{2,1,0:T(8,128)(2,1)} %bitcast.12, f32[256,32,512]{0,2,1:T(8,128)} %convolution_bitcast_fusion.1, bf16[256,32,512]{0,2,1:T(8,128)(2,1)} %copy.72), kind=kOutput, calls=%fused_computation.23 | convolution fusion | flops 2166358016 | bytes 46137344 | tf_op jit(solution)/shard_map/fcd,ecd->cef/dot_general | solution.py:104
  474.6 8.0 copy.103
  482.5 8.5 copy.109
  491.1 15.3 %multiply_convert_fusion = bf16[256,32,512]{0,2,1:T(8,128)(2,1)} fusion(f32[256,32,512]{0,2,1:T(8,128)} %convolution_bitcast_fusion, f32[256,32,512]{0,2,1:T(8,128)} %convolution_bitcast_fusion.1), kind=kLoop, calls=%fused_computation.13 | loop fusion | flops 8388608 | bytes 41943040 | tf_op jit(solution)/shard_map/convert_element_type | solution.py:101
  506.4 15.3 %convolution_convert_fusion = bf16[32,512,256]{1,2,0:T(8,128)(2,1)} fusion(bf16[32,256,256]{2,1,0:T(8,128)(2,1)} %param.11, f32[256,32,512]{0,2,1:T(8,128)} %convolution_bitcast_fusion, bf16[256,32,512]{0,2,1:T(8,128)(2,1)} %copy.72), kind=kOutput, calls=%fused_computation.32 | convolution fusion | flops 2164260864 | bytes 37748736 | tf_op jit(solution)/shard_map/cea,ecd->acd/dot_general | solution.py:97
  527.6 6.9 copy.105
  534.6 57.8 %all-to-all-done.2 = bf16[16,16,32,512]{3,2,1,0:T(8,128)(2,1)} async-done(((bf16[16,16,32,512]{3,2,1,0:T(8,128)(2,1)}), bf16[16,16,32,512]{3,2,1,0:T(8,128)(2,1)}, u32[]{:S(2)}, u32[]{:S(2)}) %all-to-all-start.2) | async-done | bytes 8388640 | tf_op jit(solution)/shard_map/all_to_all | solution.py:34
  597.8 8.5 copy.84
  606.3 16.4 %fusion.41 = f32[16,512,512]{2,1,0:T(8,128)} fusion(bf16[16,512,512]{2,1,0:T(8,128)(2,1)} %bitcast.86, bf16[16,512,512]{2,1,0:T(8,128)(2,1)} %fusion.3), kind=kOutput, calls=%fused_computation.54 | convolution fusion | flops 4294967296 | bytes 33554432 | tf_op jit(solution)/shard_map/fhd,fcd->fch/dot_general | solution.py:126
  622.7 24.4 %fusion.6 = (bf16[16,512,512]{2,1,0:T(8,128)(2,1)}, bf16[16,512,512]{2,1,0:T(8,128)(2,1)}) fusion(bf16[1,16,512,512]{3,2,1,0:T(8,128)(2,1)} %param.9, bf16[1,16,512,512]{3,2,1,0:T(8,128)(2,1)} %param.7, bf16[16,512,512]{2,1,0:T(8,128)(2,1)} %bitcast.87, bf16[16,512,512]{2,1,0:T(8,128)(2,1)} %param.10), kind=kOutput, calls=%fused_computation.11 | convolution fusion | flops 4353687552 | bytes 50331648 | tf_op jit(solution)/shard_map/fch,fcd->fhd/dot_general | solution.py:120
  647.1 87.7 %all-to-all-done.3 = bf16[16,12,32,512]{3,2,1,0:T(8,128)(2,1)} async-done(((bf16[16,12,32,512]{3,2,1,0:T(8,128)(2,1)}), bf16[16,12,32,512]{3,2,1,0:T(8,128)(2,1)}, u32[]{:S(2)}, u32[]{:S(2)}) %all-to-all-start.3) | async-done | bytes 6291488 | tf_op jit(solution)/shard_map/all_to_all | solution.py:34
  740.4 6.6 copy.86
  747.0 16.2 %add_multiply_fusion = f32[12,512,512]{2,1,0:T(8,128)} fusion(f32[16,512,512]{2,1,0:T(8,128)} %fusion.41, bf16[12,512,512]{2,1,0:T(8,128)(2,1)} %bitcast.93, bf16[1,16,512,512]{3,2,1,0:T(8,128)(2,1)} %param.6), kind=kOutput, calls=%fused_computation.15 | convolution fusion | flops 3227516928 | bytes 37748736 | tf_op jit(solution)/shard_map/acd,abd->acb/dot_general | solution.py:136
  774.7 8.0 copy.95
  782.7 10.7 %convert_bitcast_fusion.1 = bf16[12,512,512]{2,1,0:T(8,128)(2,1)} fusion(bf16[12,512,512]{2,1,0:T(8,128)(2,1)} %bitcast.94, bf16[16,512,512]{2,1,0:T(8,128)(2,1)} %param.10), kind=kOutput, calls=%fused_computation.40 | convolution fusion | flops 3224371200 | bytes 18874368 | tf_op jit(solution)/shard_map/acb,acd->abd/dot_general | solution.py:132
  801.9 37.4 %collective-permute-done = bf16[12,512,256]{2,1,0:T(8,128)(2,1)} collective-permute-done((bf16[12,512,256]{2,1,0:T(8,128)(2,1)}, bf16[12,512,256]{2,1,0:T(8,128)(2,1)}, u32[]{:S(2)}, u32[]{:S(2)}) %collective-permute-start) | collective-permute-done | bytes 3145760 | tf_op jit(solution)/shard_map/ppermute | solution.py:54
  848.8 7.5 maximum_bitcast_fusion
  (28 shorter events, 60.9 us)
Async XLA Ops:
  29.3 188.3 %all-to-all-start = ((bf16[16,16,32,512]{3,2,1,0:T(8,128)(2,1)}), bf16[16,16,32,512]{3,2,1,0:T(8,128)(2,1)}, u32[]{:S(2)}, u32[]{:S(2)}) async-start(bf16[16,16,32,512]{3,2,1,0:T(8,128)(2,1)} %bitcast.92), calls=%async_computation | async-start | bytes 16777216 | tf_op jit(solution)/shard_map/all_to_all | solution.py:19
  217.6 187.7 %all-to-all-start.1 = ((bf16[16,16,32,512]{3,2,1,0:T(8,128)(2,1)}), bf16[16,16,32,512]{3,2,1,0:T(8,128)(2,1)}, u32[]{:S(2)}, u32[]{:S(2)}) async-start(bf16[16,16,32,512]{3,2,1,0:T(8,128)(2,1)} %bitcast.91), calls=%async_computation.1 | async-start | bytes 16777216 | tf_op jit(solution)/shard_map/all_to_all | solution.py:19
  405.3 187.1 %all-to-all-start.2 = ((bf16[16,16,32,512]{3,2,1,0:T(8,128)(2,1)}), bf16[16,16,32,512]{3,2,1,0:T(8,128)(2,1)}, u32[]{:S(2)}, u32[]{:S(2)}) async-start(bf16[16,16,32,512]{3,2,1,0:T(8,128)(2,1)} %bitcast.90), calls=%async_computation.2 | async-start | bytes 16777216 | tf_op jit(solution)/shard_map/all_to_all | solution.py:34
  410.3 359.2 %reduce-scatter.7.cloned.1.call-start = ((), (), s32[]{:S(2)}) async-start(), calls=%async_computation.8 | async-start | bytes 6291456
  491.0 283.7 %reduce-scatter.5.cloned.1.call-start = ((), (), s32[]{:S(2)}) async-start(), calls=%async_computation.7 | async-start | bytes 12582912 | tf_op jit(solution)/shard_map/reduce_scatter | solution.py:109
  521.7 5.9 copy-start
  592.4 142.4 %all-to-all-start.3 = ((bf16[16,12,32,512]{3,2,1,0:T(8,128)(2,1)}), bf16[16,12,32,512]{3,2,1,0:T(8,128)(2,1)}, u32[]{:S(2)}, u32[]{:S(2)}) async-start(bf16[16,12,32,512]{3,2,1,0:T(8,128)(2,1)} %copy.105), calls=%async_computation.3 | async-start | bytes 12582912 | tf_op jit(solution)/shard_map/all_to_all | solution.py:34
  734.8 58.7 %all-to-all-start.4 = ((bf16[16,4,32,512]{3,1,2,0:T(4,128)(2,1)}), bf16[16,4,32,512]{3,1,2,0:T(4,128)(2,1)}, u32[]{:S(2)}, u32[]{:S(2)}) async-start(bf16[16,4,32,512]{3,1,2,0:T(4,128)(2,1)} %copy.106), calls=%async_computation.4 | async-start | bytes 4194304 | tf_op jit(solution)/shard_map/all_to_all | solution.py:34
  768.0 71.3 %collective-permute-start = (bf16[12,512,256]{2,1,0:T(8,128)(2,1)}, bf16[12,512,256]{2,1,0:T(8,128)(2,1)}, u32[]{:S(2)}, u32[]{:S(2)}) collective-permute-start(bf16[12,512,256]{2,1,0:T(8,128)(2,1)} %dynamic-slice_convert_fusion), channel_id=1, source_target_pairs={{0,16},{16,0},{1,17},{17,1},{2,18},{18,2},{3,19},{19,3},{4,20},{20... | collective-permute-start | bytes 9437192 | tf_op jit(solution)/shard_map/ppermute | solution.py:54
  798.3 2.0 copy-start.1
  801.4 59.5 %collective-permute-start.1 = (bf16[4,512,256]{2,1,0:T(8,128)(2,1)}, bf16[4,512,256]{2,1,0:T(8,128)(2,1)}, u32[]{:S(2)}, u32[]{:S(2)}) collective-permute-start(bf16[4,512,256]{2,1,0:T(8,128)(2,1)} %dynamic-slice_convert_fusion.1), channel_id=1, source_target_pairs={{0,16},{16,0},{1,17},{17,1},{2,18},{18,2},{3,19},{19,3},{4,20},{20... | collective-permute-start | bytes 3145736 | tf_op jit(solution)/shard_map/ppermute | solution.py:54
Sparse Core Ops, SparseCore 0:
  491.2 55.2 reduce-scatter.6
  548.8 99.3 reduce-scatter.4

commit v10 on v8

--- a/solution.py
+++ b/solution.py
@@ -133,11 +133,34 @@
                 "acb,acd->abd", block_one[lo:hi], grad_first_rows, preferred_element_type=f32
             ).astype(jnp.bfloat16)
         )
-        outer_inputs = jnp.einsum(
-            "acd,abd->acb", grad_first_rows, tokens[lo:hi], preferred_element_type=f32
-        )
-        partial = (outer_one[lo:hi] + outer_inputs) * grad_scale
-        return grad_tokens, dp_reduce_scatter(partial, 2)
+        n_dp = lax.axis_size("dp")
+        me = lax.axis_index("dp")
+        size = tokens.shape[1] // n_dp
+
+        def partial_for(owner):
+            columns = lax.dynamic_slice_in_dim(tokens[lo:hi], owner * size, size, axis=1)
+            known = lax.dynamic_slice_in_dim(outer_one[lo:hi], owner * size, size, axis=2)
+            return (
+                known
+                + jnp.einsum(
+                    "acd,abd->acb", grad_first_rows, columns, preferred_element_type=f32
+                )
+            ) * grad_scale
+
+        received = []
+        for shift in range(1, n_dp):
+            target = lax.rem(me + shift, n_dp)
+            received.append(
+                lax.ppermute(
+                    partial_for(target).astype(jnp.bfloat16),
+                    "dp",
+                    [(i, (i + shift) % n_dp) for i in range(n_dp)],
+                )
+            )
+        total = partial_for(me)
+        for part in received:
+            total = total + part.astype(f32)
+        return grad_tokens, total.astype(jnp.bfloat16)
 
     grad_tokens_parts, grad_block_ones = [], []
     pending = None

time: 871 us -> 867 us (level)
  waiting for transfers between devices: 456 us -> 444 us
    slice x0 -> x2, local copies, waits for them, and re-layouts: none -> 12.4 us  [the longest x1 7.15 us: partial_for(): outer_one[lo:hi]]
    all_to_all x3, waiting for transfers between devices: 172 us -> 163 us  [rows_move(): return lax.all_to_all(x, 'seq', split_axis=0, concat_axis=0, tiled=True)]
    dot_general x2 -> x4, matrix products: 18.4 us -> 26.4 us  [partial_for(): jnp.einsum('acd,abd->acb', grad_first_rows, columns, preferred_element_ty...]
  transfers between devices with their start and end apart: 9 -> 9, of which waited for: 6 -> 6; matrix products, arithmetic and copies ran while one was open for 38% -> 39% of each run, Pallas kernels for 0% -> 0%
where the time goes in v10:
time: 867 us; the launch traced here: 858 us
  waiting for transfers between devices  444 us (51%)
  matrix products  226 us (26%)
  local copies, waits for them, and re-layouts  106 us (12%)
  other arithmetic  36.7 us (4%)
  starting transfers between devices  31.2 us (4%)
  between operations  14.4 us (2%)
    all_to_all x2, waiting for transfers between devices, cols_recv(): lax.all_to_all(x, 'seq', split_axis=0, concat_axis=0, tiled=True)  270 us
    all_to_all x3, waiting for transfers between devices, rows_move(): return lax.all_to_all(x, 'seq', split_axis=0, concat_axis=0, tiled=True)  163 us
    unnamed x10, local copies, waits for them, and re-layouts  47.8 us
    dot_general x4, matrix products, partial_for(): jnp.einsum('acd,abd->acb', grad_first_rows, columns, preferred_element_ty...  26.4 us
    dot_general x1, matrix products, body(): jnp.einsum('fch,fcd->fhd', block_one, third_rows, preferred_element_type=...  24.4 us
    dot_general x1, matrix products, body(): jnp.einsum('fcd,ecd->cef', grad_third_cols, filtered, preferred_element_t...  22 us
    dot_general x1, matrix products, body(): jnp.einsum('ecd,acd->cea', grad_second, first_cols, preferred_element_typ...  21.4 us
    dot_general x1, matrix products, body(): jnp.einsum('cea,acd->ecd', block_two, first_cols, preferred_element_type=...  20.4 us
  transfers between devices with their start and end apart: 9, of which 6 were waited for; matrix products, arithmetic and copies ran while one was open for 39% of the time, Pallas kernels for 0%

profile of v10, /device:TPU:10, one launch (start us, length us, event | category | flops | bytes accessed | tf_op | source)
XLA Modules:
  0.0 858.2 jit_solution(9710027772012576253)
XLA Ops:
  7.2 13.7 %fusion.15 = bf16[16,512,512]{2,1,0:T(8,128)(2,1)} fusion(bf16[16,512,512]{2,1,0:T(8,128)(2,1)} %param.10, bf16[1,16,512,512]{3,2,1,0:T(8,128)(2,1)} %param.6), kind=kOutput, calls=%fused_computation.30 | convolution fusion | flops 4299161600 | bytes 25165824 | tf_op jit(solution)/shard_map/acb,abd->acd/dot_general | solution.py:69
  20.9 8.4 copy.127
  35.5 11.4 %fusion.3 = bf16[16,512,512]{2,1,0:T(8,128)(2,1)} fusion(bf16[1,16,512,512]{3,2,1,0:T(8,128)(2,1)} %param.9, bf16[1,16,512,512]{3,2,1,0:T(8,128)(2,1)} %param.7), kind=kLoop, calls=%fused_computation.8 | loop fusion | flops 29360128 | bytes 25165824 | tf_op jit(solution)/shard_map/convert_element_type | solution.py:76
  46.9 13.7 %convolution_convert_fusion.1 = bf16[16,512,512]{1,2,0:T(8,128)(2,1)} fusion(bf16[16,512,512]{2,1,0:T(8,128)(2,1)} %param.10, bf16[16,512,512]{2,1,0:T(8,128)(2,1)} %fusion.3), kind=kOutput, calls=%fused_computation.32 | convolution fusion | flops 4299161600 | bytes 25165824 | tf_op jit(solution)/shard_map/fch,fhd->fcd/dot_general | solution.py:77
  60.6 8.3 copy.128
  68.9 148.7 %all-to-all-done = bf16[16,16,32,512]{3,2,1,0:T(8,128)(2,1)} async-done(((bf16[16,16,32,512]{3,2,1,0:T(8,128)(2,1)}), bf16[16,16,32,512]{3,2,1,0:T(8,128)(2,1)}, u32[]{:S(2)}, u32[]{:S(2)}) %all-to-all-start) | async-done | bytes 8388640 | tf_op jit(solution)/shard_map/all_to_all | solution.py:19
  223.0 13.7 %copy.49 = bf16[256,32,512]{0,2,1:T(8,128)(2,1)} copy(bf16[256,32,512]{2,1,0:T(8,128)(2,1)} %param.8) | data formatting | bytes 16777216 | tf_op args[2]
  236.7 20.4 %convolution_bitcast_fusion.1 = f32[256,32,512]{0,2,1:T(8,128)} fusion(bf16[32,256,256]{2,1,0:T(8,128)(2,1)} %param.11, bf16[256,32,512]{2,1,0:T(8,128)(2,1)} %bitcast.8), kind=kOutput, calls=%fused_computation.16 | convolution fusion | flops 2147483648 | bytes 29360128 | tf_op jit(solution)/shard_map/cea,acd->ecd/dot_general | solution.py:84
  257.1 14.9 %convert_bitcast_fusion = bf16[256,32,512]{2,0,1:T(8,128)(2,1)} fusion(bf16[32,256,256]{2,1,0:T(8,128)(2,1)} %param.11, f32[256,32,512]{0,2,1:T(8,128)} %convolution_bitcast_fusion.1, bf16[256,32,512]{0,2,1:T(8,128)(2,1)} %copy.49), kind=kOutput, calls=%fused_computation.23 | convolution fusion | flops 2164260864 | bytes 37748736 | tf_op jit(solution)/shard_map/cef,ecd->fcd/dot_general | solution.py:87
  272.0 11.5 %copy.55 = bf16[256,32,512]{2,1,0:T(8,128)(2,1)} copy(bf16[256,32,512]{2,0,1:T(8,128)(2,1)} %convert_bitcast_fusion) | data formatting | bytes 16777216 | tf_op jit(solution)/shard_map/convert_element_type | solution.py:89
  283.5 121.4 %all-to-all-done.1 = bf16[16,16,32,512]{3,2,1,0:T(8,128)(2,1)} async-done(((bf16[16,16,32,512]{3,2,1,0:T(8,128)(2,1)}), bf16[16,16,32,512]{3,2,1,0:T(8,128)(2,1)}, u32[]{:S(2)}, u32[]{:S(2)}) %all-to-all-start.1) | async-done | bytes 8388640 | tf_op jit(solution)/shard_map/all_to_all | solution.py:19
  410.4 20.4 %convolution_bitcast_fusion = f32[256,32,512]{0,2,1:T(8,128)} fusion(bf16[32,256,256]{2,1,0:T(8,128)(2,1)} %param.11, bf16[256,32,512]{2,1,0:T(8,128)(2,1)} %bitcast.12), kind=kOutput, calls=%fused_computation.15 | convolution fusion | flops 2147483648 | bytes 29360128 | tf_op jit(solution)/shard_map/cef,fcd->ecd/dot_general | solution.py:94
  430.8 21.4 %fusion.10 = f32[32,256,256]{2,1,0:T(8,128)} fusion(bf16[256,32,512]{2,1,0:T(8,128)(2,1)} %bitcast.8, f32[256,32,512]{0,2,1:T(8,128)} %convolution_bitcast_fusion, bf16[256,32,512]{0,2,1:T(8,128)(2,1)} %copy.49), kind=kOutput, calls=%fused_computation.25 | convolution fusion | flops 2160066560 | bytes 41943040 | tf_op jit(solution)/shard_map/ecd,acd->cea/dot_general | solution.py:105
  452.1 22.0 %multiply_convert_fusion.1 = bf16[32,256,256]{2,1,0:T(8,128)(2,1)} fusion(f32[32,256,256]{2,1,0:T(8,128)} %fusion.10, bf16[256,32,512]{2,1,0:T(8,128)(2,1)} %bitcast.12, f32[256,32,512]{0,2,1:T(8,128)} %convolution_bitcast_fusion.1, bf16[256,32,512]{0,2,1:T(8,128)(2,1)} %copy.49), kind=kOutput, calls=%fused_computation.22 | convolution fusion | flops 2166358016 | bytes 46137344 | tf_op jit(solution)/shard_map/fcd,ecd->cef/dot_general | solution.py:104
  474.2 8.0 copy.83
  482.2 8.4 copy.89
  490.7 15.4 %multiply_convert_fusion = bf16[256,32,512]{0,2,1:T(8,128)(2,1)} fusion(f32[256,32,512]{0,2,1:T(8,128)} %convolution_bitcast_fusion, f32[256,32,512]{0,2,1:T(8,128)} %convolution_bitcast_fusion.1), kind=kLoop, calls=%fused_computation.13 | loop fusion | flops 8388608 | bytes 41943040 | tf_op jit(solution)/shard_map/convert_element_type | solution.py:101
  506.1 15.3 %convolution_convert_fusion = bf16[32,512,256]{1,2,0:T(8,128)(2,1)} fusion(bf16[32,256,256]{2,1,0:T(8,128)(2,1)} %param.11, f32[256,32,512]{0,2,1:T(8,128)} %convolution_bitcast_fusion, bf16[256,32,512]{0,2,1:T(8,128)(2,1)} %copy.49), kind=kOutput, calls=%fused_computation.31 | convolution fusion | flops 2164260864 | bytes 37748736 | tf_op jit(solution)/shard_map/cea,ecd->acd/dot_general | solution.py:97
  530.4 61.6 %all-to-all-done.2 = bf16[16,16,32,512]{3,2,1,0:T(8,128)(2,1)} async-done(((bf16[16,16,32,512]{3,2,1,0:T(8,128)(2,1)}), bf16[16,16,32,512]{3,2,1,0:T(8,128)(2,1)}, u32[]{:S(2)}, u32[]{:S(2)}) %all-to-all-start.2) | async-done | bytes 8388640 | tf_op jit(solution)/shard_map/all_to_all | solution.py:34
  597.6 8.5 copy.61
  606.1 16.4 %fusion.77 = f32[16,512,512]{2,1,0:T(8,128)} fusion(bf16[16,512,512]{2,1,0:T(8,128)(2,1)} %bitcast.95, bf16[16,512,512]{2,1,0:T(8,128)(2,1)} %fusion.3), kind=kOutput, calls=%fused_computation.70 | convolution fusion | flops 4294967296 | bytes 33554432 | tf_op jit(solution)/shard_map/fhd,fcd->fch/dot_general | solution.py:126
  622.5 24.4 %fusion.6 = (bf16[16,512,512]{2,1,0:T(8,128)(2,1)}, bf16[16,512,512]{2,1,0:T(8,128)(2,1)}) fusion(bf16[1,16,512,512]{3,2,1,0:T(8,128)(2,1)} %param.9, bf16[1,16,512,512]{3,2,1,0:T(8,128)(2,1)} %param.7, bf16[16,512,512]{2,1,0:T(8,128)(2,1)} %bitcast.96, bf16[16,512,512]{2,1,0:T(8,128)(2,1)} %param.10), kind=kOutput, calls=%fused_computation.11 | convolution fusion | flops 4353687552 | bytes 50331648 | tf_op jit(solution)/shard_map/fch,fcd->fhd/dot_general | solution.py:120
  646.9 42.8 %all-to-all-done.3 = bf16[16,8,32,512]{3,1,2,0:T(8,128)(2,1)} async-done(((bf16[16,8,32,512]{3,1,2,0:T(8,128)(2,1)}), bf16[16,8,32,512]{3,1,2,0:T(8,128)(2,1)}, u32[]{:S(2)}, u32[]{:S(2)}) %all-to-all-start.3) | async-done | bytes 4194336 | tf_op jit(solution)/shard_map/all_to_all | solution.py:34
  704.8 7.1 fusion.74
  712.0 6.5 multiply_convert_fusion.3
  720.0 8.4 convert_bitcast_fusion.2
  728.4 58.6 %all-to-all-done.4 = bf16[16,8,32,512]{3,1,2,0:T(8,128)(2,1)} async-done(((bf16[16,8,32,512]{3,1,2,0:T(8,128)(2,1)}), bf16[16,8,32,512]{3,1,2,0:T(8,128)(2,1)}, u32[]{:S(2)}, u32[]{:S(2)}) %all-to-all-start.4) | async-done | bytes 4194336 | tf_op jit(solution)/shard_map/all_to_all | solution.py:34
  787.1 7.0 multiply_convert_fusion.2
  800.9 8.0 copy.75
  815.3 8.5 convert_bitcast_fusion.1
  823.9 7.6 maximum_bitcast_fusion
  831.4 10.9 %collective-permute-done.1 = bf16[8,512,256]{2,1,0:T(8,128)(2,1)} collective-permute-done((bf16[8,512,256]{2,1,0:T(8,128)(2,1)}, bf16[8,512,256]{2,1,0:T(8,128)(2,1)}, u32[]{:S(2)}, u32[]{:S(2)}) %collective-permute-start.1) | collective-permute-done | bytes 2097184 | tf_op jit(solution)/shard_map/ppermute | solution.py:154
  (27 shorter events, 70.5 us)
Async XLA Ops:
  29.3 188.3 %all-to-all-start = ((bf16[16,16,32,512]{3,2,1,0:T(8,128)(2,1)}), bf16[16,16,32,512]{3,2,1,0:T(8,128)(2,1)}, u32[]{:S(2)}, u32[]{:S(2)}) async-start(bf16[16,16,32,512]{3,2,1,0:T(8,128)(2,1)} %bitcast.99), calls=%async_computation | async-start | bytes 16777216 | tf_op jit(solution)/shard_map/all_to_all | solution.py:19
  217.6 187.3 %all-to-all-start.1 = ((bf16[16,16,32,512]{3,2,1,0:T(8,128)(2,1)}), bf16[16,16,32,512]{3,2,1,0:T(8,128)(2,1)}, u32[]{:S(2)}, u32[]{:S(2)}) async-start(bf16[16,16,32,512]{3,2,1,0:T(8,128)(2,1)} %bitcast.98), calls=%async_computation.1 | async-start | bytes 16777216 | tf_op jit(solution)/shard_map/all_to_all | solution.py:19
  404.9 187.1 %all-to-all-start.2 = ((bf16[16,16,32,512]{3,2,1,0:T(8,128)(2,1)}), bf16[16,16,32,512]{3,2,1,0:T(8,128)(2,1)}, u32[]{:S(2)}, u32[]{:S(2)}) async-start(bf16[16,16,32,512]{3,2,1,0:T(8,128)(2,1)} %bitcast.97), calls=%async_computation.2 | async-start | bytes 16777216 | tf_op jit(solution)/shard_map/all_to_all | solution.py:34
  410.0 385.7 %reduce-scatter.7.cloned.1.call-start = ((), (), s32[]{:S(2)}) async-start(), calls=%async_computation.8 | async-start | bytes 6291456
  490.6 310.2 %reduce-scatter.5.cloned.1.call-start = ((), (), s32[]{:S(2)}) async-start(), calls=%async_computation.7 | async-start | bytes 12582912 | tf_op jit(solution)/shard_map/reduce_scatter | solution.py:109
  592.0 97.7 %all-to-all-start.3 = ((bf16[16,8,32,512]{3,1,2,0:T(8,128)(2,1)}), bf16[16,8,32,512]{3,1,2,0:T(8,128)(2,1)}, u32[]{:S(2)}, u32[]{:S(2)}) async-start(bf16[16,8,32,512]{3,1,2,0:T(8,128)(2,1)} %copy.85), calls=%async_computation.3 | async-start | bytes 8388608 | tf_op jit(solution)/shard_map/all_to_all | solution.py:34
  689.7 97.4 %all-to-all-start.4 = ((bf16[16,8,32,512]{3,1,2,0:T(8,128)(2,1)}), bf16[16,8,32,512]{3,1,2,0:T(8,128)(2,1)}, u32[]{:S(2)}, u32[]{:S(2)}) async-start(bf16[16,8,32,512]{3,1,2,0:T(8,128)(2,1)} %copy.86), calls=%async_computation.4 | async-start | bytes 8388608 | tf_op jit(solution)/shard_map/all_to_all | solution.py:34
  695.1 9.7 %copy-start = (f32[16,512,512]{2,1,0:T(8,128)S(1)}, f32[16,512,512]{2,1,0:T(8,128)}, u32[]{:S(2)}) copy-start(f32[16,512,512]{2,1,0:T(8,128)} %fusion.77) | copy-start | bytes 50331652
  704.8 7.2 copy-start.1
  718.5 90.4 %collective-permute-start = (bf16[8,512,256]{2,1,0:T(8,128)(2,1)}, bf16[8,512,256]{2,1,0:T(8,128)(2,1)}, u32[]{:S(2)}, u32[]{:S(2)}) collective-permute-start(bf16[8,512,256]{2,1,0:T(8,128)(2,1)} %multiply_convert_fusion.3), channel_id=1, source_target_pairs={{0,16},{16,0},{1,17},{17,1},{2,18},{18,2},{3,19},{19,3},{4,20},{20... | collective-permute-start | bytes 6291464 | tf_op jit(solution)/shard_map/ppermute | solution.py:154
  794.1 48.3 %collective-permute-start.1 = (bf16[8,512,256]{2,1,0:T(8,128)(2,1)}, bf16[8,512,256]{2,1,0:T(8,128)(2,1)}, u32[]{:S(2)}, u32[]{:S(2)}) collective-permute-start(bf16[8,512,256]{2,1,0:T(8,128)(2,1)} %multiply_convert_fusion.2), channel_id=1, source_target_pairs={{0,16},{16,0},{1,17},{17,1},{2,18},{18,2},{3,19},{19,3},{4,20},{20... | collective-permute-start | bytes 6291464 | tf_op jit(solution)/shard_map/ppermute | solution.py:154
Sparse Core Ops, SparseCore 0:
  490.8 55.2 reduce-scatter.6
  548.4 99.2 reduce-scatter.4
